TPU v7x, 256 devices: a whole 4x4x8 slice. The times are simulated.
256 devices in a mesh: tm: 64 (over z, y, core), ingest: 4 (over x).
Axes of the slice: x: 4, y: 4, z: 8, core: 2. Of those that a mesh axis runs over, the one named last changes fastest.
Arguments:
- trans: float32 [512, 384, 384], P('tm')
- gain: float32 [512, 384, 192], P('tm', None, 'ingest'), may hold values from -0.0048828125 to 0.0048828125
- prior_mean: float32 [384], replicated, may hold values from -8 to 8
- obs_basis: bfloat16 [131072, 192], P(('tm', 'ingest')), may hold values from -6 to 6
- obs_value: float32 [131072], P(('tm', 'ingest')), may hold values from -6 to 6
- measurement_within_tile: int32 [131072], P(('tm', 'ingest')), may hold values from 0 to 7
- observed_row_count: int32 [256, 64], P(('tm', 'ingest')), may hold values from 1 to 8, as said below
Outputs:
- filtered: float32 [512, 384], P('tm')
Inputs may be any that keep to these rules, and one draw needn't show every extreme that they name: `observed_row_count`: rows of a group at positions from its count on are not live; every device's row of counts has one group of 8 live rows.
All inputs are finite; a program needn't handle non-finite values.
Results may differ from a plain program's by a relative error of at most 0.0023.
Values may be sent and summed in bfloat16 or wider, within the bound.
No kernel may reach another device: no remote copies, remote signals or barrier semaphores. Data moves between devices by JAX's collectives and lax.ppermute only.
A program may use at most 128 MiB of HBM per device.

v0:
```python
import jax
import jax.numpy as jnp
from jax import lax
from jax.sharding import PartitionSpec as P


def passed_along(block, axis, distance):
    devices = range(lax.axis_size(axis))
    route = [(i - distance, i) for i in devices if i - distance in devices]
    return lax.ppermute(block, axis, route)


def on_device(
    trans, gain, prior_mean, obs_basis, obs_value, measurement_within_tile, observed_row_count
):
    exact = lax.Precision.HIGHEST
    tm_count = lax.axis_size("tm")
    in_count = lax.axis_size("ingest")
    steps_here = trans.shape[0]
    state_width = trans.shape[1]
    col_width = state_width // in_count
    basis_count = obs_basis.shape[1]
    piece_width = basis_count // in_count
    group_rows = obs_basis.shape[0] // tm_count
    weighted = (obs_basis * obs_value[:, None]).astype(jnp.bfloat16)
    sent_rows = weighted.reshape(tm_count, group_rows, in_count, piece_width)
    slot_ids = measurement_within_tile.reshape(tm_count, group_rows)
    is_valid = lax.broadcasted_iota(
        jnp.int32, (tm_count, group_rows), 1
    ) < observed_row_count.reshape(tm_count, 1)
    marked = jnp.where(is_valid, slot_ids, -1)
    step_ids = lax.broadcasted_iota(jnp.int32, (1, 1, steps_here), 2)
    got_rows, got_marks = (
        lax.all_to_all(sent_rows, "tm", split_axis=0, concat_axis=0, tiled=True),
        lax.all_to_all(marked, "tm", split_axis=0, concat_axis=0, tiled=True),
    )
    onehot = (got_marks[:, :, None] == step_ids).astype(jnp.bfloat16)
    term_sums = jnp.einsum("kcl,kcjs->ljs", onehot, got_rows, preferred_element_type=jnp.float32)
    drive_sums = lax.psum_scatter(term_sums, "ingest", scatter_dimension=1, tiled=True)[:, 0]
    partial_force = jnp.einsum("lsq,lq->ls", gain, drive_sums, precision=exact)
    forcing = lax.psum(partial_force, "ingest")
    column_index = lax.axis_index("ingest")
    eye_block = lax.dynamic_slice_in_dim(
        jnp.eye(state_width, dtype=jnp.float32), column_index * col_width, col_width, 1
    )

    def advance(carried, inputs):
        columns, offset = carried
        step_map, step_force = inputs
        columns = jnp.dot(step_map, columns, precision=exact)
        offset = jnp.dot(step_map, offset, precision=exact) + step_force
        return ((columns, offset), (columns, offset))

    initial_pair = (eye_block, jnp.zeros((state_width,), jnp.float32))
    _, (prefix_cols, offsets) = lax.scan(advance, initial_pair, (trans, forcing))
    summary = lax.all_gather(prefix_cols[-1], "ingest", axis=1, tiled=True)
    ending = offsets[-1]
    is_first = lax.axis_index("tm") == 0

    def relay_turn(_, incoming):
        outgoing = jnp.dot(summary, incoming, precision=exact) + ending
        arrived_rows = passed_along(outgoing, "tm", 1)
        return jnp.where(is_first, prior_mean, arrived_rows)

    initial = jnp.where(is_first, prior_mean, jnp.zeros_like(prior_mean))
    entering = lax.fori_loop(0, tm_count - 1, relay_turn, initial)
    own_part = lax.dynamic_slice_in_dim(entering, column_index * col_width, col_width, 0)
    partial_means = jnp.einsum("lsq,q->ls", prefix_cols, own_part, precision=exact)
    filtered = lax.psum(partial_means, "ingest") + offsets
    return filtered


def solution(mesh):
    return jax.shard_map(
        on_device,
        mesh=mesh,
        in_specs=(
            P("tm", None, None),
            P("tm", None, "ingest"),
            P(),
            P(("tm", "ingest"), None),
            P(("tm", "ingest")),
            P(("tm", "ingest")),
            P(("tm", "ingest"), None),
        ),
        out_specs=P("tm", None),
        check_vma=False,
    )
```

profile of v0, /device:TPU:128, one launch (start us, length us, event | category | flops | bytes accessed | tf_op | source)
XLA Modules:
  0.0 688.7 jit_solution(15369590563298886019)
XLA Ops:
  2.2 10.5 %all-to-all-start = ((s32[64,1,8]{2,1,0:T(1,128)}), s32[64,1,8]{2,1,0:T(1,128)S(1)}, u32[]{:S(2)}, u32[]{:S(2)}) async-start(s32[64,1,8]{2,1,0:T(1,128)} %bitcast.1), calls=%async_computation | async-start | bytes 65536 | tf_op jit(solution)/shard_map/all_to_all | solution.py:35
  17.5 9.4 %all-to-all-start.1 = ((bf16[64,2,768]{2,1,0:T(2,128)(2,1)}), bf16[64,2,768]{2,1,0:T(2,128)(2,1)S(1)}, u32[]{:S(2)}, u32[]{:S(2)}) async-start(bf16[64,2,768]{2,1,0:T(2,128)(2,1)} %reshape.76), calls=%async_computation.1 | async-start | bytes 393216 | tf_op jit(solution)/shard_map/all_to_all | solution.py:34
  27.7 7.1 %all-to-all-done.1 = bf16[64,2,768]{2,1,0:T(2,128)(2,1)S(1)} async-done(((bf16[64,2,768]{2,1,0:T(2,128)(2,1)}), bf16[64,2,768]{2,1,0:T(2,128)(2,1)S(1)}, u32[]{:S(2)}, u32[]{:S(2)}) %all-to-all-start.1) | async-done | bytes 196640 | tf_op jit(solution)/shard_map/all_to_all | solution.py:34
  35.6 16.9 %all-reduce = f32[8,4,48]{2,0,1:T(8,128)S(1)} all-reduce(f32[8,4,48]{2,0,1:T(8,128)S(1)} %convolution_bitcast_fusion), channel_id=3, replica_groups=mesh['tm'=64,'ingest'=4] {'ingest'}, use_global_device_ids=true, to_apply=%region_0.1.clone | all-reduce | flops 1536 | bytes 12288
  53.5 14.3 %psum.14 = f32[8,384]{1,0:T(8,128)S(1)} all-reduce(f32[8,384]{1,0:T(8,128)S(1)} %bitcast.62), channel_id=1, replica_groups=mesh['tm'=64,'ingest'=4] {'ingest'}, use_global_device_ids=true, to_apply=%region_1.2 | all-reduce | flops 3072 | bytes 24576 | tf_op jit(solution)/shard_map/psum | solution.py:41
  67.8 29.6 %while.28 = (s32[]{:T(128)}, f32[384,96]{0,1:T(8,128)S(1)}, f32[384]{0:T(512)S(1)}, f32[8,384,96]{1,2,0:T(8,128)S(1)}, f32[8,384]{1,0:T(8,128)S(1)}, /*index=5*/...) while((s32[]{:T(128)}, f32[384,96]{0,1:T(8,128)S(1)}, f32[384]{0:T(512)S(1)}, ...), condition=%wide.region_3.4_spmd.clone, body=%wide.region_2.3_spmd.clone.sunk | while | flops 171639552 | bytes 1941615 | solution.py:55
  97.4 12.9 %all-gather = f32[1,384,384]{1,2,0:T(8,128)S(1)} all-gather(f32[1,384,96]{1,2,0:T(8,128)S(1)} %slice.6), channel_id=2, replica_groups=mesh['tm'=64,'ingest'=4] {'ingest'}, dimensions={2}, use_global_device_ids=true | all-gather | bytes 737280 | tf_op jit(solution)/shard_map/all_gather | solution.py:56
  110.6 561.5 %while.27 = (s32[]{:T(128)}, f32[384]{0:T(512)S(1)}, pred[]{:T(512)}, f32[384,384]{1,0:T(8,128)S(1)}, f32[384]{0:T(512)S(1)}, /*index=5*/f32[384]{0:T(512)S(1)}, s32[]{:T(128)}) while((s32[]{:T(128)}, f32[384]{0:T(512)S(1)}, pred[]{:T(512)}, f32[384,384]{1,0:T(8,128)S(1)}, f32[384]{0:T(512)S(1)}, /*index=5*/f32[384]{0:T(512)S(1)}, ...), condition=%wide.region_5.6_spmd, body=%wide.region_4.5_spmd.sunk | while | flops 1770242 | bytes 611446 | solution.py:66
  122.1 6.3 collective-permute-done
  148.8 6.3 collective-permute-done
  157.7 6.3 collective-permute-done
  184.5 6.3 collective-permute-done
  193.4 6.3 collective-permute-done
  220.1 6.3 collective-permute-done
  229.0 6.3 collective-permute-done
  255.8 6.3 collective-permute-done
  264.7 6.3 collective-permute-done
  291.4 6.3 collective-permute-done
  318.2 6.3 collective-permute-done
  327.1 6.3 collective-permute-done
  353.8 6.3 collective-permute-done
  362.7 6.3 collective-permute-done
  389.5 6.3 collective-permute-done
  398.4 6.3 collective-permute-done
  425.1 6.3 collective-permute-done
  434.0 6.3 collective-permute-done
  460.8 6.3 collective-permute-done
  487.5 6.3 collective-permute-done
  496.4 6.3 collective-permute-done
  523.1 6.3 collective-permute-done
  532.1 6.3 collective-permute-done
  672.8 15.3 %psum.15 = f32[8,384]{1,0:T(8,128)S(1)} all-reduce(f32[8,384]{1,0:T(8,128)S(1)} %bitcast.63), channel_id=1, replica_groups=mesh['tm'=64,'ingest'=4] {'ingest'}, use_global_device_ids=true, to_apply=%region_6.7 | all-reduce | flops 3072 | bytes 24576 | tf_op jit(solution)/shard_map/psum | solution.py:69
  (459 shorter events, 455.4 us)
Async XLA Ops:
  2.2 15.3 %all-to-all-start = ((s32[64,1,8]{2,1,0:T(1,128)}), s32[64,1,8]{2,1,0:T(1,128)S(1)}, u32[]{:S(2)}, u32[]{:S(2)}) async-start(s32[64,1,8]{2,1,0:T(1,128)} %bitcast.1), calls=%async_computation | async-start | bytes 65536 | tf_op jit(solution)/shard_map/all_to_all | solution.py:35
  17.5 17.3 %all-to-all-start.1 = ((bf16[64,2,768]{2,1,0:T(2,128)(2,1)}), bf16[64,2,768]{2,1,0:T(2,128)(2,1)S(1)}, u32[]{:S(2)}, u32[]{:S(2)}) async-start(bf16[64,2,768]{2,1,0:T(2,128)(2,1)} %reshape.76), calls=%async_computation.1 | async-start | bytes 393216 | tf_op jit(solution)/shard_map/all_to_all | solution.py:34
  120.2 8.2 %collective-permute-start = (f32[384]{0:T(512)S(1)}, f32[384]{0:T(512)S(1)}, u32[]{:S(2)}, u32[]{:S(2)}) collective-permute-start(f32[384]{0:T(512)S(1)} %add.44), channel_id=1, source_target_pairs={{0,4},{4,8},{8,12},{12,16},{16,20},{20,24},{24,28},{28,32},{32,36}... | collective-permute-start | bytes 4616 | tf_op jit(solution)/shard_map/while/body/eval_jaxpr/ppermute | solution.py:10
  129.1 8.2 %collective-permute-start = (f32[384]{0:T(512)S(1)}, f32[384]{0:T(512)S(1)}, u32[]{:S(2)}, u32[]{:S(2)}) collective-permute-start(f32[384]{0:T(512)S(1)} %add.44), channel_id=1, source_target_pairs={{0,4},{4,8},{8,12},{12,16},{16,20},{20,24},{24,28},{28,32},{32,36}... | collective-permute-start | bytes 4616 | tf_op jit(solution)/shard_map/while/body/eval_jaxpr/ppermute | solution.py:10
  146.9 8.2 %collective-permute-start = (f32[384]{0:T(512)S(1)}, f32[384]{0:T(512)S(1)}, u32[]{:S(2)}, u32[]{:S(2)}) collective-permute-start(f32[384]{0:T(512)S(1)} %add.44), channel_id=1, source_target_pairs={{0,4},{4,8},{8,12},{12,16},{16,20},{20,24},{24,28},{28,32},{32,36}... | collective-permute-start | bytes 4616 | tf_op jit(solution)/shard_map/while/body/eval_jaxpr/ppermute | solution.py:10
  155.8 8.2 %collective-permute-start = (f32[384]{0:T(512)S(1)}, f32[384]{0:T(512)S(1)}, u32[]{:S(2)}, u32[]{:S(2)}) collective-permute-start(f32[384]{0:T(512)S(1)} %add.44), channel_id=1, source_target_pairs={{0,4},{4,8},{8,12},{12,16},{16,20},{20,24},{24,28},{28,32},{32,36}... | collective-permute-start | bytes 4616 | tf_op jit(solution)/shard_map/while/body/eval_jaxpr/ppermute | solution.py:10
  182.6 8.2 %collective-permute-start = (f32[384]{0:T(512)S(1)}, f32[384]{0:T(512)S(1)}, u32[]{:S(2)}, u32[]{:S(2)}) collective-permute-start(f32[384]{0:T(512)S(1)} %add.44), channel_id=1, source_target_pairs={{0,4},{4,8},{8,12},{12,16},{16,20},{20,24},{24,28},{28,32},{32,36}... | collective-permute-start | bytes 4616 | tf_op jit(solution)/shard_map/while/body/eval_jaxpr/ppermute | solution.py:10
  191.5 8.2 %collective-permute-start = (f32[384]{0:T(512)S(1)}, f32[384]{0:T(512)S(1)}, u32[]{:S(2)}, u32[]{:S(2)}) collective-permute-start(f32[384]{0:T(512)S(1)} %add.44), channel_id=1, source_target_pairs={{0,4},{4,8},{8,12},{12,16},{16,20},{20,24},{24,28},{28,32},{32,36}... | collective-permute-start | bytes 4616 | tf_op jit(solution)/shard_map/while/body/eval_jaxpr/ppermute | solution.py:10
  218.2 8.2 %collective-permute-start = (f32[384]{0:T(512)S(1)}, f32[384]{0:T(512)S(1)}, u32[]{:S(2)}, u32[]{:S(2)}) collective-permute-start(f32[384]{0:T(512)S(1)} %add.44), channel_id=1, source_target_pairs={{0,4},{4,8},{8,12},{12,16},{16,20},{20,24},{24,28},{28,32},{32,36}... | collective-permute-start | bytes 4616 | tf_op jit(solution)/shard_map/while/body/eval_jaxpr/ppermute | solution.py:10
  227.1 8.2 %collective-permute-start = (f32[384]{0:T(512)S(1)}, f32[384]{0:T(512)S(1)}, u32[]{:S(2)}, u32[]{:S(2)}) collective-permute-start(f32[384]{0:T(512)S(1)} %add.44), channel_id=1, source_target_pairs={{0,4},{4,8},{8,12},{12,16},{16,20},{20,24},{24,28},{28,32},{32,36}... | collective-permute-start | bytes 4616 | tf_op jit(solution)/shard_map/while/body/eval_jaxpr/ppermute | solution.py:10
  253.8 8.2 %collective-permute-start = (f32[384]{0:T(512)S(1)}, f32[384]{0:T(512)S(1)}, u32[]{:S(2)}, u32[]{:S(2)}) collective-permute-start(f32[384]{0:T(512)S(1)} %add.44), channel_id=1, source_target_pairs={{0,4},{4,8},{8,12},{12,16},{16,20},{20,24},{24,28},{28,32},{32,36}... | collective-permute-start | bytes 4616 | tf_op jit(solution)/shard_map/while/body/eval_jaxpr/ppermute | solution.py:10
  262.8 8.2 %collective-permute-start = (f32[384]{0:T(512)S(1)}, f32[384]{0:T(512)S(1)}, u32[]{:S(2)}, u32[]{:S(2)}) collective-permute-start(f32[384]{0:T(512)S(1)} %add.44), channel_id=1, source_target_pairs={{0,4},{4,8},{8,12},{12,16},{16,20},{20,24},{24,28},{28,32},{32,36}... | collective-permute-start | bytes 4616 | tf_op jit(solution)/shard_map/while/body/eval_jaxpr/ppermute | solution.py:10
  289.5 8.2 %collective-permute-start = (f32[384]{0:T(512)S(1)}, f32[384]{0:T(512)S(1)}, u32[]{:S(2)}, u32[]{:S(2)}) collective-permute-start(f32[384]{0:T(512)S(1)} %add.44), channel_id=1, source_target_pairs={{0,4},{4,8},{8,12},{12,16},{16,20},{20,24},{24,28},{28,32},{32,36}... | collective-permute-start | bytes 4616 | tf_op jit(solution)/shard_map/while/body/eval_jaxpr/ppermute | solution.py:10
  298.4 8.2 %collective-permute-start = (f32[384]{0:T(512)S(1)}, f32[384]{0:T(512)S(1)}, u32[]{:S(2)}, u32[]{:S(2)}) collective-permute-start(f32[384]{0:T(512)S(1)} %add.44), channel_id=1, source_target_pairs={{0,4},{4,8},{8,12},{12,16},{16,20},{20,24},{24,28},{28,32},{32,36}... | collective-permute-start | bytes 4616 | tf_op jit(solution)/shard_map/while/body/eval_jaxpr/ppermute | solution.py:10
  316.2 8.2 %collective-permute-start = (f32[384]{0:T(512)S(1)}, f32[384]{0:T(512)S(1)}, u32[]{:S(2)}, u32[]{:S(2)}) collective-permute-start(f32[384]{0:T(512)S(1)} %add.44), channel_id=1, source_target_pairs={{0,4},{4,8},{8,12},{12,16},{16,20},{20,24},{24,28},{28,32},{32,36}... | collective-permute-start | bytes 4616 | tf_op jit(solution)/shard_map/while/body/eval_jaxpr/ppermute | solution.py:10
  325.1 8.2 %collective-permute-start = (f32[384]{0:T(512)S(1)}, f32[384]{0:T(512)S(1)}, u32[]{:S(2)}, u32[]{:S(2)}) collective-permute-start(f32[384]{0:T(512)S(1)} %add.44), channel_id=1, source_target_pairs={{0,4},{4,8},{8,12},{12,16},{16,20},{20,24},{24,28},{28,32},{32,36}... | collective-permute-start | bytes 4616 | tf_op jit(solution)/shard_map/while/body/eval_jaxpr/ppermute | solution.py:10
  351.9 8.2 %collective-permute-start = (f32[384]{0:T(512)S(1)}, f32[384]{0:T(512)S(1)}, u32[]{:S(2)}, u32[]{:S(2)}) collective-permute-start(f32[384]{0:T(512)S(1)} %add.44), channel_id=1, source_target_pairs={{0,4},{4,8},{8,12},{12,16},{16,20},{20,24},{24,28},{28,32},{32,36}... | collective-permute-start | bytes 4616 | tf_op jit(solution)/shard_map/while/body/eval_jaxpr/ppermute | solution.py:10
  360.8 8.2 %collective-permute-start = (f32[384]{0:T(512)S(1)}, f32[384]{0:T(512)S(1)}, u32[]{:S(2)}, u32[]{:S(2)}) collective-permute-start(f32[384]{0:T(512)S(1)} %add.44), channel_id=1, source_target_pairs={{0,4},{4,8},{8,12},{12,16},{16,20},{20,24},{24,28},{28,32},{32,36}... | collective-permute-start | bytes 4616 | tf_op jit(solution)/shard_map/while/body/eval_jaxpr/ppermute | solution.py:10
  387.5 8.2 %collective-permute-start = (f32[384]{0:T(512)S(1)}, f32[384]{0:T(512)S(1)}, u32[]{:S(2)}, u32[]{:S(2)}) collective-permute-start(f32[384]{0:T(512)S(1)} %add.44), channel_id=1, source_target_pairs={{0,4},{4,8},{8,12},{12,16},{16,20},{20,24},{24,28},{28,32},{32,36}... | collective-permute-start | bytes 4616 | tf_op jit(solution)/shard_map/while/body/eval_jaxpr/ppermute | solution.py:10
  396.4 8.2 %collective-permute-start = (f32[384]{0:T(512)S(1)}, f32[384]{0:T(512)S(1)}, u32[]{:S(2)}, u32[]{:S(2)}) collective-permute-start(f32[384]{0:T(512)S(1)} %add.44), channel_id=1, source_target_pairs={{0,4},{4,8},{8,12},{12,16},{16,20},{20,24},{24,28},{28,32},{32,36}... | collective-permute-start | bytes 4616 | tf_op jit(solution)/shard_map/while/body/eval_jaxpr/ppermute | solution.py:10
  423.2 8.2 %collective-permute-start = (f32[384]{0:T(512)S(1)}, f32[384]{0:T(512)S(1)}, u32[]{:S(2)}, u32[]{:S(2)}) collective-permute-start(f32[384]{0:T(512)S(1)} %add.44), channel_id=1, source_target_pairs={{0,4},{4,8},{8,12},{12,16},{16,20},{20,24},{24,28},{28,32},{32,36}... | collective-permute-start | bytes 4616 | tf_op jit(solution)/shard_map/while/body/eval_jaxpr/ppermute | solution.py:10
  432.1 8.2 %collective-permute-start = (f32[384]{0:T(512)S(1)}, f32[384]{0:T(512)S(1)}, u32[]{:S(2)}, u32[]{:S(2)}) collective-permute-start(f32[384]{0:T(512)S(1)} %add.44), channel_id=1, source_target_pairs={{0,4},{4,8},{8,12},{12,16},{16,20},{20,24},{24,28},{28,32},{32,36}... | collective-permute-start | bytes 4616 | tf_op jit(solution)/shard_map/while/body/eval_jaxpr/ppermute | solution.py:10
  458.8 8.2 %collective-permute-start = (f32[384]{0:T(512)S(1)}, f32[384]{0:T(512)S(1)}, u32[]{:S(2)}, u32[]{:S(2)}) collective-permute-start(f32[384]{0:T(512)S(1)} %add.44), channel_id=1, source_target_pairs={{0,4},{4,8},{8,12},{12,16},{16,20},{20,24},{24,28},{28,32},{32,36}... | collective-permute-start | bytes 4616 | tf_op jit(solution)/shard_map/while/body/eval_jaxpr/ppermute | solution.py:10
  467.7 8.2 %collective-permute-start = (f32[384]{0:T(512)S(1)}, f32[384]{0:T(512)S(1)}, u32[]{:S(2)}, u32[]{:S(2)}) collective-permute-start(f32[384]{0:T(512)S(1)} %add.44), channel_id=1, source_target_pairs={{0,4},{4,8},{8,12},{12,16},{16,20},{20,24},{24,28},{28,32},{32,36}... | collective-permute-start | bytes 4616 | tf_op jit(solution)/shard_map/while/body/eval_jaxpr/ppermute | solution.py:10
  485.6 8.2 %collective-permute-start = (f32[384]{0:T(512)S(1)}, f32[384]{0:T(512)S(1)}, u32[]{:S(2)}, u32[]{:S(2)}) collective-permute-start(f32[384]{0:T(512)S(1)} %add.44), channel_id=1, source_target_pairs={{0,4},{4,8},{8,12},{12,16},{16,20},{20,24},{24,28},{28,32},{32,36}... | collective-permute-start | bytes 4616 | tf_op jit(solution)/shard_map/while/body/eval_jaxpr/ppermute | solution.py:10
  494.5 8.2 %collective-permute-start = (f32[384]{0:T(512)S(1)}, f32[384]{0:T(512)S(1)}, u32[]{:S(2)}, u32[]{:S(2)}) collective-permute-start(f32[384]{0:T(512)S(1)} %add.44), channel_id=1, source_target_pairs={{0,4},{4,8},{8,12},{12,16},{16,20},{20,24},{24,28},{28,32},{32,36}... | collective-permute-start | bytes 4616 | tf_op jit(solution)/shard_map/while/body/eval_jaxpr/ppermute | solution.py:10
  521.2 8.2 %collective-permute-start = (f32[384]{0:T(512)S(1)}, f32[384]{0:T(512)S(1)}, u32[]{:S(2)}, u32[]{:S(2)}) collective-permute-start(f32[384]{0:T(512)S(1)} %add.44), channel_id=1, source_target_pairs={{0,4},{4,8},{8,12},{12,16},{16,20},{20,24},{24,28},{28,32},{32,36}... | collective-permute-start | bytes 4616 | tf_op jit(solution)/shard_map/while/body/eval_jaxpr/ppermute | solution.py:10
  530.1 8.2 %collective-permute-start = (f32[384]{0:T(512)S(1)}, f32[384]{0:T(512)S(1)}, u32[]{:S(2)}, u32[]{:S(2)}) collective-permute-start(f32[384]{0:T(512)S(1)} %add.44), channel_id=1, source_target_pairs={{0,4},{4,8},{8,12},{12,16},{16,20},{20,24},{24,28},{28,32},{32,36}... | collective-permute-start | bytes 4616 | tf_op jit(solution)/shard_map/while/body/eval_jaxpr/ppermute | solution.py:10
  556.9 8.2 %collective-permute-start = (f32[384]{0:T(512)S(1)}, f32[384]{0:T(512)S(1)}, u32[]{:S(2)}, u32[]{:S(2)}) collective-permute-start(f32[384]{0:T(512)S(1)} %add.44), channel_id=1, source_target_pairs={{0,4},{4,8},{8,12},{12,16},{16,20},{20,24},{24,28},{28,32},{32,36}... | collective-permute-start | bytes 4616 | tf_op jit(solution)/shard_map/while/body/eval_jaxpr/ppermute | solution.py:10
  565.8 8.2 %collective-permute-start = (f32[384]{0:T(512)S(1)}, f32[384]{0:T(512)S(1)}, u32[]{:S(2)}, u32[]{:S(2)}) collective-permute-start(f32[384]{0:T(512)S(1)} %add.44), channel_id=1, source_target_pairs={{0,4},{4,8},{8,12},{12,16},{16,20},{20,24},{24,28},{28,32},{32,36}... | collective-permute-start | bytes 4616 | tf_op jit(solution)/shard_map/while/body/eval_jaxpr/ppermute | solution.py:10
  592.5 8.2 %collective-permute-start = (f32[384]{0:T(512)S(1)}, f32[384]{0:T(512)S(1)}, u32[]{:S(2)}, u32[]{:S(2)}) collective-permute-start(f32[384]{0:T(512)S(1)} %add.44), channel_id=1, source_target_pairs={{0,4},{4,8},{8,12},{12,16},{16,20},{20,24},{24,28},{28,32},{32,36}... | collective-permute-start | bytes 4616 | tf_op jit(solution)/shard_map/while/body/eval_jaxpr/ppermute | solution.py:10
  601.4 8.2 %collective-permute-start = (f32[384]{0:T(512)S(1)}, f32[384]{0:T(512)S(1)}, u32[]{:S(2)}, u32[]{:S(2)}) collective-permute-start(f32[384]{0:T(512)S(1)} %add.44), channel_id=1, source_target_pairs={{0,4},{4,8},{8,12},{12,16},{16,20},{20,24},{24,28},{28,32},{32,36}... | collective-permute-start | bytes 4616 | tf_op jit(solution)/shard_map/while/body/eval_jaxpr/ppermute | solution.py:10
  (36 other events, 350.8 us)
where the time goes:
time: 694 us; the launch traced here: 689 us
  waiting for transfers between devices  406 us (59%)
  starting transfers between devices  141 us (20%)
  matrix products  71.3 us (10%)
  blocking collectives  59.4 us (9%)
    ppermute x63, waiting for transfers between devices, passed_along(): return lax.ppermute(block, axis, route)  397 us
    ppermute x63, starting transfers between devices, passed_along(): return lax.ppermute(block, axis, route)  121 us
    dot_general x63, matrix products, relay_turn(): outgoing = jnp.dot(summary, incoming, precision=exact) + ending  41.6 us
    unnamed x1, blocking collectives  16.9 us
    psum x1, blocking collectives, on_device(): filtered = lax.psum(partial_means, 'ingest') + offsets  15.3 us
    dot_general x8, matrix products, advance(): columns = jnp.dot(step_map, columns, precision=exact)  14.4 us
    psum x1, blocking collectives, on_device(): forcing = lax.psum(partial_force, 'ingest')  14.3 us
  transfers between devices with their start and end apart: 65, of which 65 were waited for; matrix products, arithmetic and copies ran while one was open for 1% of the time, Pallas kernels for 0%

commit v1 on v0

v1 whole, which is shorter than its diff:
```python
import jax
import jax.numpy as jnp
from jax import lax
from jax.sharding import PartitionSpec as P


def passed_along(block, axis, distance):
    devices = range(lax.axis_size(axis))
    route = [(i - distance, i) for i in devices if i - distance in devices]
    return lax.ppermute(block, axis, route)


def on_device(
    trans, gain, prior_mean, obs_basis, obs_value, measurement_within_tile, observed_row_count
):
    exact = lax.Precision.HIGHEST
    tm_count = lax.axis_size("tm")
    in_count = lax.axis_size("ingest")
    steps_here = trans.shape[0]
    state_width = trans.shape[1]
    basis_count = obs_basis.shape[1]
    piece_width = basis_count // in_count
    group_rows = obs_basis.shape[0] // tm_count

    weighted = (obs_basis.astype(jnp.float32) * obs_value[:, None]).astype(jnp.bfloat16)
    pieces = weighted.reshape(tm_count, group_rows, in_count, piece_width)
    pieces = pieces.transpose(0, 2, 1, 3).reshape(tm_count * in_count, group_rows * piece_width)
    is_valid = lax.broadcasted_iota(
        jnp.int32, (tm_count, group_rows), 1
    ) < observed_row_count.reshape(tm_count, 1)
    marked = jnp.where(is_valid, measurement_within_tile.reshape(tm_count, group_rows), -1)
    marks = jnp.broadcast_to(
        marked.astype(jnp.bfloat16)[:, None, :], (tm_count, in_count, group_rows)
    ).reshape(tm_count * in_count, group_rows)
    sent = jnp.concatenate([pieces, marks], axis=1)
    got = lax.all_to_all(sent, ("tm", "ingest"), split_axis=0, concat_axis=0, tiled=True)
    got_rows = got[:, : group_rows * piece_width].reshape(-1, piece_width)
    got_marks = got[:, group_rows * piece_width :].reshape(-1).astype(jnp.int32)
    step_ids = lax.broadcasted_iota(jnp.int32, (1, steps_here), 1)
    onehot = (got_marks[:, None] == step_ids).astype(jnp.bfloat16)
    drive_piece = jnp.einsum("rl,rq->lq", onehot, got_rows, preferred_element_type=jnp.float32)
    partial_force = jnp.einsum("lsq,lq->ls", gain, drive_piece, precision=exact)
    forcing = lax.psum(partial_force, "ingest")

    def compose(prefix, step_map):
        prefix = jnp.dot(step_map, prefix, precision=exact)
        return prefix, prefix

    _, prefix_maps = lax.scan(compose, jnp.eye(state_width, dtype=jnp.float32), trans)

    def advance(offset, inputs):
        step_map, step_force = inputs
        offset = jnp.dot(step_map, offset, precision=exact) + step_force
        return offset, offset

    _, offsets = lax.scan(advance, jnp.zeros((state_width,), jnp.float32), (trans, forcing))

    tm_index = lax.axis_index("tm")
    is_first = tm_index == 0
    slab_map = prefix_maps[-1]
    acc_vec = jnp.where(
        is_first, jnp.dot(slab_map, prior_mean, precision=exact) + offsets[-1], offsets[-1]
    )
    acc_map = jnp.where(is_first, jnp.zeros_like(slab_map), slab_map)
    distance = 1
    while distance < tm_count:
        got_vec = passed_along(acc_vec, "tm", distance)
        last = distance * 2 >= tm_count
        if not last:
            got_map = passed_along(acc_map, "tm", distance)
        acc_vec = jnp.dot(acc_map, got_vec, precision=exact) + acc_vec
        if not last:
            acc_map = jnp.dot(acc_map, got_map, precision=exact)
        distance *= 2
    entering = jnp.where(is_first, prior_mean, passed_along(acc_vec, "tm", 1))
    filtered = jnp.einsum("lsq,q->ls", prefix_maps, entering, precision=exact) + offsets
    return filtered


def solution(mesh):
    return jax.shard_map(
        on_device,
        mesh=mesh,
        in_specs=(
            P("tm", None, None),
            P("tm", None, "ingest"),
            P(),
            P(("tm", "ingest"), None),
            P(("tm", "ingest")),
            P(("tm", "ingest")),
            P(("tm", "ingest"), None),
        ),
        out_specs=P("tm", None),
        check_vma=False,
    )
```

time: 694 us -> 226 us (0.33)
  waiting for transfers between devices: 406 us -> 83.5 us
  starting transfers between devices: 141 us -> 39.5 us
  blocking collectives: 59.4 us -> 15.5 us
  local copies, waits for them, and re-layouts: 5.82 us -> 22.4 us
  matrix products: 71.3 us -> 59.6 us
    ppermute x63 -> x12, waiting for transfers between devices: 397 us -> 74.9 us  [passed_along(): return lax.ppermute(block, axis, route)]
    ppermute x63 -> x12, starting transfers between devices: 121 us -> 25.6 us  [passed_along(): return lax.ppermute(block, axis, route)]
    unnamed x1 -> x0, blocking collectives: 16.9 us -> none
    psum x1 -> x0, blocking collectives: 15.3 us -> none  [on_device(): filtered = lax.psum(partial_means, 'ingest') + offsets]
    all_gather x1 -> x0, blocking collectives: 12.9 us -> none  [on_device(): summary = lax.all_gather(prefix_cols[-1], 'ingest', axis=1, tiled=True)]
    dot_general x74 -> x23, matrix products: 57.5 us -> 45.9 us  [the longest x8 25.3 us: compose(): prefix = jnp.dot(step_map, prefix, precision=exact)]
    dynamic_update_slice x8, local copies, waits for them, and re-layouts: 0.41 us -> 10.6 us  [on_device(): lax.scan(advance, jnp.zeros((state_width,), jnp.float32), (trans, forcing))]
    all_to_all x2 -> x1, starting transfers between devices: 19.9 us -> 13.9 us  [on_device(): lax.all_to_all(sent, ('tm', 'ingest'), split_axis=0, concat_axis=0, tiled...]
  transfers between devices with their start and end apart: 65 -> 13, of which waited for: 65 -> 9; matrix products, arithmetic and copies ran while one was open for 1% -> 20% of each run, Pallas kernels for 0% -> 0%
where the time goes in v1:
time: 226 us; the launch traced here: 224 us
  waiting for transfers between devices  83.5 us (37%)
  matrix products  59.6 us (26%)
  starting transfers between devices  39.5 us (17%)
  local copies, waits for them, and re-layouts  22.4 us (10%)
  blocking collectives  15.5 us (7%)
  other arithmetic  2.82 us (1%)
    ppermute x12, waiting for transfers between devices, passed_along(): return lax.ppermute(block, axis, route)  74.9 us
    ppermute x12, starting transfers between devices, passed_along(): return lax.ppermute(block, axis, route)  25.6 us
    dot_general x8, matrix products, compose(): prefix = jnp.dot(step_map, prefix, precision=exact)  25.3 us
    psum x1, blocking collectives, on_device(): forcing = lax.psum(partial_force, 'ingest')  15.5 us
    all_to_all x1, starting transfers between devices, on_device(): lax.all_to_all(sent, ('tm', 'ingest'), split_axis=0, concat_axis=0, tiled...  13.9 us
    dot_general x8, matrix products, advance(): offset = jnp.dot(step_map, offset, precision=exact) + step_force  13.8 us
    dynamic_update_slice x8, local copies, waits for them, and re-layouts, on_device(): lax.scan(advance, jnp.zeros((state_width,), jnp.float32), (trans, forcing))  10.6 us
    all_to_all x1, waiting for transfers between devices, on_device(): lax.all_to_all(sent, ('tm', 'ingest'), split_axis=0, concat_axis=0, tiled...  8.65 us
  transfers between devices with their start and end apart: 13, of which 9 were waited for; matrix products, arithmetic and copies ran while one was open for 20% of the time, Pallas kernels for 0%

profile of v1, /device:TPU:128, one launch (start us, length us, event | category | flops | bytes accessed | tf_op | source)
XLA Modules:
  0.0 224.0 jit_solution(79529686420630875)
XLA Ops:
  0.1 25.7 %while.25 = (s32[]{:T(128)}, f32[384,384]{1,0:T(8,128)S(1)}, f32[8,384,384]{2,1,0:T(8,128)}, f32[8,384,384]{2,1,0:T(8,128)}, s32[]{:T(128)}) while((s32[]{:T(128)}, f32[384,384]{1,0:T(8,128)S(1)}, f32[8,384,384]{2,1,0:T(8,128)}, f32[8,384,384]{2,1,0:T(8,128)}, s32[]{:T(128)}) %tuple.41), condition=%wide.region_1.2_spmd, body=%wide.region_0.1_spmd.sunk | while | flops 679477248 | bytes 3540037 | solution.py:49
  0.2 3.2 %bitcast_dynamic-update-slice_fusion.2 = (f32[8,384,384]{2,1,0:T(8,128)}, f32[384,384]{1,0:T(8,128)S(1)}) fusion(f32[8,384,384]{2,1,0:T(8,128)} %get-tuple-element.182, s32[]{:T(128)S(6)} %copy.40, f32[384,384]{1,0:T(8,128)S(1)} %copy.47, f32[8,384,384]{2,1,0:T(8,128)} %get-tuple-element.188), kind=kOutput, calls=%fused_computation.clone.1 | convolution fusion | flops 679477248 | bytes 2360320 | tf_op jit(solution)/shard_map/while/body/eval_jaxpr/dot_general | solution.py:46
  3.4 3.1 %bitcast_dynamic-update-slice_fusion.2 = (f32[8,384,384]{2,1,0:T(8,128)}, f32[384,384]{1,0:T(8,128)S(1)}) fusion(f32[8,384,384]{2,1,0:T(8,128)} %get-tuple-element.182, s32[]{:T(128)S(6)} %copy.40, f32[384,384]{1,0:T(8,128)S(1)} %copy.47, f32[8,384,384]{2,1,0:T(8,128)} %get-tuple-element.188), kind=kOutput, calls=%fused_computation.clone.1 | convolution fusion | flops 679477248 | bytes 2360320 | tf_op jit(solution)/shard_map/while/body/eval_jaxpr/dot_general | solution.py:46
  6.6 3.2 %bitcast_dynamic-update-slice_fusion.2 = (f32[8,384,384]{2,1,0:T(8,128)}, f32[384,384]{1,0:T(8,128)S(1)}) fusion(f32[8,384,384]{2,1,0:T(8,128)} %get-tuple-element.182, s32[]{:T(128)S(6)} %copy.40, f32[384,384]{1,0:T(8,128)S(1)} %copy.47, f32[8,384,384]{2,1,0:T(8,128)} %get-tuple-element.188), kind=kOutput, calls=%fused_computation.clone.1 | convolution fusion | flops 679477248 | bytes 2360320 | tf_op jit(solution)/shard_map/while/body/eval_jaxpr/dot_general | solution.py:46
  9.8 3.2 %bitcast_dynamic-update-slice_fusion.2 = (f32[8,384,384]{2,1,0:T(8,128)}, f32[384,384]{1,0:T(8,128)S(1)}) fusion(f32[8,384,384]{2,1,0:T(8,128)} %get-tuple-element.182, s32[]{:T(128)S(6)} %copy.40, f32[384,384]{1,0:T(8,128)S(1)} %copy.47, f32[8,384,384]{2,1,0:T(8,128)} %get-tuple-element.188), kind=kOutput, calls=%fused_computation.clone.1 | convolution fusion | flops 679477248 | bytes 2360320 | tf_op jit(solution)/shard_map/while/body/eval_jaxpr/dot_general | solution.py:46
  13.0 3.2 %bitcast_dynamic-update-slice_fusion.2 = (f32[8,384,384]{2,1,0:T(8,128)}, f32[384,384]{1,0:T(8,128)S(1)}) fusion(f32[8,384,384]{2,1,0:T(8,128)} %get-tuple-element.182, s32[]{:T(128)S(6)} %copy.40, f32[384,384]{1,0:T(8,128)S(1)} %copy.47, f32[8,384,384]{2,1,0:T(8,128)} %get-tuple-element.188), kind=kOutput, calls=%fused_computation.clone.1 | convolution fusion | flops 679477248 | bytes 2360320 | tf_op jit(solution)/shard_map/while/body/eval_jaxpr/dot_general | solution.py:46
  16.2 3.1 %bitcast_dynamic-update-slice_fusion.2 = (f32[8,384,384]{2,1,0:T(8,128)}, f32[384,384]{1,0:T(8,128)S(1)}) fusion(f32[8,384,384]{2,1,0:T(8,128)} %get-tuple-element.182, s32[]{:T(128)S(6)} %copy.40, f32[384,384]{1,0:T(8,128)S(1)} %copy.47, f32[8,384,384]{2,1,0:T(8,128)} %get-tuple-element.188), kind=kOutput, calls=%fused_computation.clone.1 | convolution fusion | flops 679477248 | bytes 2360320 | tf_op jit(solution)/shard_map/while/body/eval_jaxpr/dot_general | solution.py:46
  19.4 3.1 %bitcast_dynamic-update-slice_fusion.2 = (f32[8,384,384]{2,1,0:T(8,128)}, f32[384,384]{1,0:T(8,128)S(1)}) fusion(f32[8,384,384]{2,1,0:T(8,128)} %get-tuple-element.182, s32[]{:T(128)S(6)} %copy.40, f32[384,384]{1,0:T(8,128)S(1)} %copy.47, f32[8,384,384]{2,1,0:T(8,128)} %get-tuple-element.188), kind=kOutput, calls=%fused_computation.clone.1 | convolution fusion | flops 679477248 | bytes 2360320 | tf_op jit(solution)/shard_map/while/body/eval_jaxpr/dot_general | solution.py:46
  22.6 3.1 %bitcast_dynamic-update-slice_fusion.2 = (f32[8,384,384]{2,1,0:T(8,128)}, f32[384,384]{1,0:T(8,128)S(1)}) fusion(f32[8,384,384]{2,1,0:T(8,128)} %get-tuple-element.182, s32[]{:T(128)S(6)} %copy.40, f32[384,384]{1,0:T(8,128)S(1)} %copy.47, f32[8,384,384]{2,1,0:T(8,128)} %get-tuple-element.188), kind=kOutput, calls=%fused_computation.clone.1 | convolution fusion | flops 679477248 | bytes 2360320 | tf_op jit(solution)/shard_map/while/body/eval_jaxpr/dot_general | solution.py:46
  26.9 1.9 collective-permute-start
  29.0 12.4 %collective-permute-done = f32[384,384]{1,0:T(8,128)S(1)} collective-permute-done((f32[384,384]{1,0:T(8,128)S(1)}, f32[384,384]{1,0:T(8,128)S(1)}, u32[]{:S(2)}, u32[]{:S(2)}) %collective-permute-start) | collective-permute-done | bytes 589856 | tf_op jit(solution)/shard_map/ppermute | solution.py:10
  42.7 1.9 collective-permute-start.1
  47.8 13.9 %all-to-all-start = ((bf16[256,2,196]{2,1,0:T(2,128)(2,1)}), bf16[256,2,196]{2,1,0:T(2,128)(2,1)S(1)}, u32[]{:S(2)}, u32[]{:S(2)}) async-start(bf16[256,2,196]{2,1,0:T(2,128)(2,1)} %reshape.87), calls=%async_computation | async-start | bytes 524288 | tf_op jit(solution)/shard_map/all_to_all | solution.py:36
  63.5 8.7 %all-to-all-done = bf16[256,2,196]{2,1,0:T(2,128)(2,1)S(1)} async-done(((bf16[256,2,196]{2,1,0:T(2,128)(2,1)}), bf16[256,2,196]{2,1,0:T(2,128)(2,1)S(1)}, u32[]{:S(2)}, u32[]{:S(2)}) %all-to-all-start) | async-done | bytes 200736 | tf_op jit(solution)/shard_map/all_to_all | solution.py:36
  74.2 3.3 %collective-permute-start.2 = (f32[384,384]{1,0:T(8,128)S(1)}, f32[384,384]{1,0:T(8,128)S(1)}, u32[]{:S(2)}, u32[]{:S(2)}) collective-permute-start(f32[384,384]{1,0:T(8,128)S(1)} %fusion.13), channel_id=1, source_target_pairs={{0,16},{4,20},{8,24},{12,28},{16,32},{20,36},{24,40},{28,44},{32,4... | collective-permute-start | bytes 1769480 | tf_op jit(solution)/shard_map/ppermute | solution.py:10
  81.4 15.5 %psum.7 = f32[8,384]{1,0:T(8,128)} all-reduce(f32[8,384]{1,0:T(8,128)S(1)} %bitcast.74), channel_id=1, replica_groups=mesh['tm'=64,'ingest'=4] {'ingest'}, use_global_device_ids=true, to_apply=%region_2.3 | all-reduce | flops 3072 | bytes 24576 | tf_op jit(solution)/shard_map/psum | solution.py:43
  98.2 2.6 %collective-permute-start.3 = (f32[384,384]{1,0:T(8,128)S(1)}, f32[384,384]{1,0:T(8,128)S(1)}, u32[]{:S(2)}, u32[]{:S(2)}) collective-permute-start(f32[384,384]{1,0:T(8,128)S(1)} %fusion.14), channel_id=1, source_target_pairs={{0,32},{4,36},{8,40},{12,44},{16,48},{20,52},{24,56},{28,60},{32,6... | collective-permute-start | bytes 1769480 | tf_op jit(solution)/shard_map/ppermute | solution.py:10
  100.7 30.5 %while.26 = (s32[]{:T(128)}, f32[384]{0:T(512)S(1)}, f32[8,384]{1,0:T(8,128)}, f32[8,384,384]{2,1,0:T(8,128)}, f32[8,384]{1,0:T(8,128)}, /*index=5*/s32[]{:T(128)}, s32[]{:T(128)}) while((s32[]{:T(128)}, f32[384]{0:T(512)S(1)}, f32[8,384]{1,0:T(8,128)}, f32[8,384,384]{2,1,0:T(8,128)}, f32[8,384]{1,0:T(8,128)}, ...), condition=%wide.region_4.5_spmd.clone, body=%wide.region_3.4_spmd.clone.sunk | while | flops 1770243 | bytes 612971 | solution.py:56
  132.0 2.1 collective-permute-start.5
  134.1 6.1 %collective-permute-done.5 = f32[384]{0:T(512)S(1)} collective-permute-done((f32[384]{0:T(512)S(1)}, f32[384]{0:T(512)S(1)}, u32[]{:S(2)}, u32[]{:S(2)}) %collective-permute-start.5) | collective-permute-done | bytes 1568 | tf_op jit(solution)/shard_map/ppermute | solution.py:10
  141.5 2.9 %collective-permute-start.4 = (f32[384,384]{1,0:T(8,128)S(1)}, f32[384,384]{1,0:T(8,128)S(1)}, u32[]{:S(2)}, u32[]{:S(2)}) collective-permute-start(f32[384,384]{1,0:T(8,128)S(1)} %fusion.15), channel_id=1, source_target_pairs={{0,64},{4,68},{8,72},{12,76},{16,80},{20,84},{24,88},{28,92},{32,9... | collective-permute-start | bytes 1769480 | tf_op jit(solution)/shard_map/ppermute | solution.py:10
  145.1 1.9 collective-permute-start.6
  147.0 24.4 %collective-permute-done.6 = f32[384]{0:T(512)S(1)} collective-permute-done((f32[384]{0:T(512)S(1)}, f32[384]{0:T(512)S(1)}, u32[]{:S(2)}, u32[]{:S(2)}) %collective-permute-start.6) | collective-permute-done | bytes 1568 | tf_op jit(solution)/shard_map/ppermute | solution.py:10
  172.1 1.9 collective-permute-start.7
  174.0 7.2 %collective-permute-done.7 = f32[384]{0:T(512)S(1)} collective-permute-done((f32[384]{0:T(512)S(1)}, f32[384]{0:T(512)S(1)}, u32[]{:S(2)}, u32[]{:S(2)}) %collective-permute-start.7) | collective-permute-done | bytes 1568 | tf_op jit(solution)/shard_map/ppermute | solution.py:10
  181.8 1.9 collective-permute-start.8
  183.8 4.8 %collective-permute-done.8 = f32[384]{0:T(512)S(1)} collective-permute-done((f32[384]{0:T(512)S(1)}, f32[384]{0:T(512)S(1)}, u32[]{:S(2)}, u32[]{:S(2)}) %collective-permute-start.8) | collective-permute-done | bytes 1568 | tf_op jit(solution)/shard_map/ppermute | solution.py:10
  189.2 1.9 collective-permute-start.9
  191.1 5.7 %collective-permute-done.9 = f32[384]{0:T(512)S(1)} collective-permute-done((f32[384]{0:T(512)S(1)}, f32[384]{0:T(512)S(1)}, u32[]{:S(2)}, u32[]{:S(2)}) %collective-permute-start.9) | collective-permute-done | bytes 1568 | tf_op jit(solution)/shard_map/ppermute | solution.py:10
  198.8 8.1 %collective-permute-done.10 = f32[384]{0:T(512)S(1)} collective-permute-done((f32[384]{0:T(512)S(1)}, f32[384]{0:T(512)S(1)}, u32[]{:S(2)}, u32[]{:S(2)}) %collective-permute-start.10) | collective-permute-done | bytes 1568 | tf_op jit(solution)/shard_map/ppermute | solution.py:10
  210.8 6.3 %collective-permute-done.11 = f32[384]{0:T(512)S(1)} collective-permute-done((f32[384]{0:T(512)S(1)}, f32[384]{0:T(512)S(1)}, u32[]{:S(2)}, u32[]{:S(2)}) %collective-permute-start.11) | collective-permute-done | bytes 1568 | tf_op jit(solution)/shard_map/ppermute | solution.py:10
  217.1 6.4 %fusion.18 = f32[1,8,384]{2,0,1:T(1,128)S(1)} fusion(f32[8,384,384]{2,1,0:T(8,128)} %get-tuple-element.54, f32[384,1,1]{0,1,2:T(1,128)S(1)} %reshape.75), kind=kOutput, calls=%fused_computation.42 | convolution fusion | flops 14155776 | bytes 4732416 | tf_op jit(solution)/shard_map/lsq,q->ls/dot_general | solution.py:76
  (142 shorter events, 56.5 us)
Async XLA Ops:
  0.0 80.9 %copy-start = (f32[8,384,48]{1,2,0:T(8,128)S(1)}, f32[8,384,48]{1,2,0:T(8,128)}, u32[]{:S(2)}) copy-start(f32[8,384,48]{1,2,0:T(8,128)} %param.12) | copy-start | bytes 1769476
  0.1 28.8 %copy-start.5 = (s32[512]{0:T(512)S(1)}, s32[512]{0:T(512)}, u32[]{:S(2)}) copy-start(s32[512]{0:T(512)} %param.16) | copy-start | bytes 6148
  0.1 28.9 %copy-start.1 = (bf16[512,192]{0,1:T(8,128)(2,1)S(1)}, bf16[512,192]{0,1:T(8,128)(2,1)}, u32[]{:S(2)}) copy-start(bf16[512,192]{0,1:T(8,128)(2,1)} %param.14) | copy-start | bytes 589828
  0.1 28.8 %copy-start.4 = (f32[512]{0:T(512)S(1)}, f32[512]{0:T(512)}, u32[]{:S(2)}) copy-start(f32[512]{0:T(512)} %param.15) | copy-start | bytes 6148
  0.1 44.5 %copy-start.6 = (s32[1,64]{1,0:T(1,128)S(1)}, s32[1,64]{1,0:T(1,128)}, u32[]{:S(2)}) copy-start(s32[1,64]{1,0:T(1,128)} %param.17) | copy-start | bytes 772
  25.8 36.0 %copy-start.3 = (f32[384]{0:T(512)S(1)}, f32[384]{0:T(512)}, u32[]{:S(2)}) copy-start(f32[384]{0:T(512)} %param.13) | copy-start | bytes 4612
  26.9 14.5 %collective-permute-start = (f32[384,384]{1,0:T(8,128)S(1)}, f32[384,384]{1,0:T(8,128)S(1)}, u32[]{:S(2)}, u32[]{:S(2)}) collective-permute-start(f32[384,384]{1,0:T(8,128)S(1)} %bitcast_select_fusion), channel_id=1, source_target_pairs={{0,4},{4,8},{8,12},{12,16},{16,20},{20,24},{24,28},{28,32},{32,36}... | collective-permute-start | bytes 1769480 | tf_op jit(solution)/shard_map/ppermute | solution.py:10
  42.7 30.2 %collective-permute-start.1 = (f32[384,384]{1,0:T(8,128)S(1)}, f32[384,384]{1,0:T(8,128)S(1)}, u32[]{:S(2)}, u32[]{:S(2)}) collective-permute-start(f32[384,384]{1,0:T(8,128)S(1)} %fusion.12), channel_id=1, source_target_pairs={{0,8},{4,12},{8,16},{12,20},{16,24},{20,28},{24,32},{28,36},{32,40... | collective-permute-start | bytes 1769480 | tf_op jit(solution)/shard_map/ppermute | solution.py:10
  47.8 24.3 %all-to-all-start = ((bf16[256,2,196]{2,1,0:T(2,128)(2,1)}), bf16[256,2,196]{2,1,0:T(2,128)(2,1)S(1)}, u32[]{:S(2)}, u32[]{:S(2)}) async-start(bf16[256,2,196]{2,1,0:T(2,128)(2,1)} %reshape.87), calls=%async_computation | async-start | bytes 524288 | tf_op jit(solution)/shard_map/all_to_all | solution.py:36
  74.2 22.8 %collective-permute-start.2 = (f32[384,384]{1,0:T(8,128)S(1)}, f32[384,384]{1,0:T(8,128)S(1)}, u32[]{:S(2)}, u32[]{:S(2)}) collective-permute-start(f32[384,384]{1,0:T(8,128)S(1)} %fusion.13), channel_id=1, source_target_pairs={{0,16},{4,20},{8,24},{12,28},{16,32},{20,36},{24,40},{28,44},{32,4... | collective-permute-start | bytes 1769480 | tf_op jit(solution)/shard_map/ppermute | solution.py:10
  98.2 42.0 %collective-permute-start.3 = (f32[384,384]{1,0:T(8,128)S(1)}, f32[384,384]{1,0:T(8,128)S(1)}, u32[]{:S(2)}, u32[]{:S(2)}) collective-permute-start(f32[384,384]{1,0:T(8,128)S(1)} %fusion.14), channel_id=1, source_target_pairs={{0,32},{4,36},{8,40},{12,44},{16,48},{20,52},{24,56},{28,60},{32,6... | collective-permute-start | bytes 1769480 | tf_op jit(solution)/shard_map/ppermute | solution.py:10
  132.0 8.2 %collective-permute-start.5 = (f32[384]{0:T(512)S(1)}, f32[384]{0:T(512)S(1)}, u32[]{:S(2)}, u32[]{:S(2)}) collective-permute-start(f32[384]{0:T(512)S(1)} %add_select_fusion), channel_id=1, source_target_pairs={{0,4},{4,8},{8,12},{12,16},{16,20},{20,24},{24,28},{28,32},{32,36}... | collective-permute-start | bytes 4616 | tf_op jit(solution)/shard_map/ppermute | solution.py:10
  141.5 65.4 %collective-permute-start.4 = (f32[384,384]{1,0:T(8,128)S(1)}, f32[384,384]{1,0:T(8,128)S(1)}, u32[]{:S(2)}, u32[]{:S(2)}) collective-permute-start(f32[384,384]{1,0:T(8,128)S(1)} %fusion.15), channel_id=1, source_target_pairs={{0,64},{4,68},{8,72},{12,76},{16,80},{20,84},{24,88},{28,92},{32,9... | collective-permute-start | bytes 1769480 | tf_op jit(solution)/shard_map/ppermute | solution.py:10
  145.1 26.3 %collective-permute-start.6 = (f32[384]{0:T(512)S(1)}, f32[384]{0:T(512)S(1)}, u32[]{:S(2)}, u32[]{:S(2)}) collective-permute-start(f32[384]{0:T(512)S(1)} %add.36), channel_id=1, source_target_pairs={{0,8},{4,12},{8,16},{12,20},{16,24},{20,28},{24,32},{28,36},{32,40... | collective-permute-start | bytes 4616 | tf_op jit(solution)/shard_map/ppermute | solution.py:10
  171.4 52.0 %copy-start.2 = (f32[8,384]{1,0:T(8,128)S(1)}, f32[8,384]{1,0:T(8,128)}, u32[]{:S(2)}) copy-start(f32[8,384]{1,0:T(8,128)} %get-tuple-element.55) | copy-start | bytes 36868
  172.1 9.1 %collective-permute-start.7 = (f32[384]{0:T(512)S(1)}, f32[384]{0:T(512)S(1)}, u32[]{:S(2)}, u32[]{:S(2)}) collective-permute-start(f32[384]{0:T(512)S(1)} %add.37), channel_id=1, source_target_pairs={{0,16},{4,20},{8,24},{12,28},{16,32},{20,36},{24,40},{28,44},{32,4... | collective-permute-start | bytes 4616 | tf_op jit(solution)/shard_map/ppermute | solution.py:10
  181.8 6.7 %collective-permute-start.8 = (f32[384]{0:T(512)S(1)}, f32[384]{0:T(512)S(1)}, u32[]{:S(2)}, u32[]{:S(2)}) collective-permute-start(f32[384]{0:T(512)S(1)} %add.38), channel_id=1, source_target_pairs={{0,32},{4,36},{8,40},{12,44},{16,48},{20,52},{24,56},{28,60},{32,6... | collective-permute-start | bytes 4616 | tf_op jit(solution)/shard_map/ppermute | solution.py:10
  189.2 7.6 %collective-permute-start.9 = (f32[384]{0:T(512)S(1)}, f32[384]{0:T(512)S(1)}, u32[]{:S(2)}, u32[]{:S(2)}) collective-permute-start(f32[384]{0:T(512)S(1)} %add.39), channel_id=1, source_target_pairs={{0,64},{4,68},{8,72},{12,76},{16,80},{20,84},{24,88},{28,92},{32,9... | collective-permute-start | bytes 4616 | tf_op jit(solution)/shard_map/ppermute | solution.py:10
  197.5 9.4 %collective-permute-start.10 = (f32[384]{0:T(512)S(1)}, f32[384]{0:T(512)S(1)}, u32[]{:S(2)}, u32[]{:S(2)}) collective-permute-start(f32[384]{0:T(512)S(1)} %add.40), channel_id=1, source_target_pairs={{0,128},{4,132},{8,136},{12,140},{16,144},{20,148},{24,152},{28,15... | collective-permute-start | bytes 4616 | tf_op jit(solution)/shard_map/ppermute | solution.py:10
  208.8 8.2 %collective-permute-start.11 = (f32[384]{0:T(512)S(1)}, f32[384]{0:T(512)S(1)}, u32[]{:S(2)}, u32[]{:S(2)}) collective-permute-start(f32[384]{0:T(512)S(1)} %add.41), channel_id=1, source_target_pairs={{0,4},{4,8},{8,12},{12,16},{16,20},{20,24},{24,28},{28,32},{32,36}... | collective-permute-start | bytes 4616 | tf_op jit(solution)/shard_map/ppermute | solution.py:10

commit v2 on v1

--- a/solution.py
+++ b/solution.py
@@ -8,6 +8,15 @@
     devices = range(lax.axis_size(axis))
     route = [(i - distance, i) for i in devices if i - distance in devices]
     return lax.ppermute(block, axis, route)
+
+
+def summed_over(block, axis):
+    distance = 1
+    while distance < lax.axis_size(axis):
+        route = [(i, i ^ distance) for i in range(lax.axis_size(axis))]
+        block = block + lax.ppermute(block, axis, route)
+        distance *= 2
+    return block
 
 
 def on_device(
@@ -40,27 +49,20 @@
     onehot = (got_marks[:, None] == step_ids).astype(jnp.bfloat16)
     drive_piece = jnp.einsum("rl,rq->lq", onehot, got_rows, preferred_element_type=jnp.float32)
     partial_force = jnp.einsum("lsq,lq->ls", gain, drive_piece, precision=exact)
-    forcing = lax.psum(partial_force, "ingest")
+    forcing = summed_over(partial_force, "ingest")
 
-    def compose(prefix, step_map):
-        prefix = jnp.dot(step_map, prefix, precision=exact)
-        return prefix, prefix
-
-    _, prefix_maps = lax.scan(compose, jnp.eye(state_width, dtype=jnp.float32), trans)
-
-    def advance(offset, inputs):
-        step_map, step_force = inputs
-        offset = jnp.dot(step_map, offset, precision=exact) + step_force
-        return offset, offset
-
-    _, offsets = lax.scan(advance, jnp.zeros((state_width,), jnp.float32), (trans, forcing))
+    level = trans
+    while level.shape[0] > 1:
+        pairs = level.reshape(level.shape[0] // 2, 2, state_width, state_width)
+        level = jnp.einsum("jab,jbc->jac", pairs[:, 1], pairs[:, 0], precision=exact)
+    slab_map = level[0]
+    offset = forcing[0]
+    for step in range(1, steps_here):
+        offset = jnp.dot(trans[step], offset, precision=exact) + forcing[step]
 
     tm_index = lax.axis_index("tm")
     is_first = tm_index == 0
-    slab_map = prefix_maps[-1]
-    acc_vec = jnp.where(
-        is_first, jnp.dot(slab_map, prior_mean, precision=exact) + offsets[-1], offsets[-1]
-    )
+    acc_vec = jnp.where(is_first, jnp.dot(slab_map, prior_mean, precision=exact) + offset, offset)
     acc_map = jnp.where(is_first, jnp.zeros_like(slab_map), slab_map)
     distance = 1
     while distance < tm_count:
@@ -72,9 +74,12 @@
         if not last:
             acc_map = jnp.dot(acc_map, got_map, precision=exact)
         distance *= 2
-    entering = jnp.where(is_first, prior_mean, passed_along(acc_vec, "tm", 1))
-    filtered = jnp.einsum("lsq,q->ls", prefix_maps, entering, precision=exact) + offsets
-    return filtered
+    state = jnp.where(is_first, prior_mean, passed_along(acc_vec, "tm", 1))
+    means = []
+    for step in range(steps_here):
+        state = jnp.dot(trans[step], state, precision=exact) + forcing[step]
+        means.append(state)
+    return jnp.stack(means)
 
 
 def solution(mesh):

time: 226 us -> 179 us (0.79)
  matrix products: 59.6 us -> 37.3 us
  blocking collectives: 15.5 us -> 0 us
  local copies, waits for them, and re-layouts: 22.4 us -> 7.51 us
  starting transfers between devices: 39.5 us -> 43.7 us
  waiting for transfers between devices: 83.5 us -> 85.9 us
    dot_general x18 -> x19, matrix products: 47.1 us -> 24.8 us  [the longest x3 10.2 us: on_device(): jnp.einsum('jab,jbc->jac', pairs[:, 1], pairs[:, 0], precision=exact)]
    psum x1 -> x0, blocking collectives: 15.5 us -> none  [on_device(): forcing = lax.psum(partial_force, 'ingest')]
    dynamic_update_slice x8 -> x0, local copies, waits for them, and re-layouts: 10.6 us -> none  [on_device(): lax.scan(advance, jnp.zeros((state_width,), jnp.float32), (trans, forcing))]
    all_to_all x1, waiting for transfers between devices: 8.65 us -> 0.01 us  [on_device(): lax.all_to_all(sent, ('tm', 'ingest'), split_axis=0, concat_axis=0, tiled...]
    ppermute x12, waiting for transfers between devices: 74.9 us -> 82.2 us  [passed_along(): return lax.ppermute(block, axis, route)]
    dynamic_slice x8 -> x0, local copies, waits for them, and re-layouts: 5.86 us -> none  [on_device(): lax.scan(advance, jnp.zeros((state_width,), jnp.float32), (trans, forcing))]
    ppermute x0 -> x2, starting transfers between devices: none -> 4.55 us  [summed_over(): block = block + lax.ppermute(block, axis, route)]
    ppermute x0 -> x2, waiting for transfers between devices: none -> 3.79 us  [summed_over(): block = block + lax.ppermute(block, axis, route)]
  transfers between devices with their start and end apart: 13 -> 15, of which waited for: 9 -> 12; matrix products, arithmetic and copies ran while one was open for 20% -> 16% of each run, Pallas kernels for 0% -> 0%
where the time goes in v2:
time: 179 us; the launch traced here: 178 us
  waiting for transfers between devices  85.9 us (48%)
  starting transfers between devices  43.7 us (24%)
  matrix products  37.3 us (21%)
  local copies, waits for them, and re-layouts  7.51 us (4%)
  other arithmetic  2.68 us (1%)
    ppermute x12, waiting for transfers between devices, passed_along(): return lax.ppermute(block, axis, route)  82.2 us
    ppermute x12, starting transfers between devices, passed_along(): return lax.ppermute(block, axis, route)  24.3 us
    all_to_all x1, starting transfers between devices, on_device(): lax.all_to_all(sent, ('tm', 'ingest'), split_axis=0, concat_axis=0, tiled...  14.8 us
    dot_general x3, matrix products, on_device(): jnp.einsum('jab,jbc->jac', pairs[:, 1], pairs[:, 0], precision=exact)  10.2 us
    dot_general x7, matrix products, on_device(): offset = jnp.dot(trans[step], offset, precision=exact) + forcing[step]  8.79 us
    dot_general x5, matrix products, on_device(): acc_map = jnp.dot(acc_map, got_map, precision=exact)  7.42 us
    dot_general x8, matrix products, on_device(): state = jnp.dot(trans[step], state, precision=exact) + forcing[step]  5.19 us
    ppermute x2, starting transfers between devices, summed_over(): block = block + lax.ppermute(block, axis, route)  4.55 us
  transfers between devices with their start and end apart: 15, of which 12 were waited for; matrix products, arithmetic and copies ran while one was open for 16% of the time, Pallas kernels for 0%

profile of v2, /device:TPU:128, one launch (start us, length us, event | category | flops | bytes accessed | tf_op | source)
XLA Modules:
  0.0 177.9 jit_solution(4817728378229583894)
XLA Ops:
  5.7 14.8 %all-to-all-start = ((bf16[256,2,196]{2,1,0:T(2,128)(2,1)}), bf16[256,2,196]{2,1,0:T(2,128)(2,1)}, u32[]{:S(2)}, u32[]{:S(2)}) async-start(bf16[256,2,196]{2,1,0:T(2,128)(2,1)} %reshape.158), calls=%async_computation | async-start | bytes 524288 | tf_op jit(solution)/shard_map/all_to_all | solution.py:45
  20.5 6.5 %fusion = f32[4,384,384]{2,1,0:T(8,128)S(1)} fusion(f32[4,2,384,384]{3,2,1,0:T(8,128)} %bitcast.132), kind=kOutput, calls=%fused_computation.1 | convolution fusion | flops 2717908992 | bytes 7077888 | tf_op jit(solution)/shard_map/jab,jbc->jac/dot_general | solution.py:57
  27.1 2.4 %convolution_bitcast_fusion = f32[1,2,384,384]{3,2,1,0:T(8,128)S(1)} fusion(f32[2,2,384,384]{3,2,1,0:T(8,128)S(1)} %bitcast.135), kind=kOutput, calls=%fused_computation.3 | convolution fusion | flops 1358954496 | bytes 3538944 | tf_op jit(solution)/shard_map/jab,jbc->jac/dot_general | solution.py:57
  30.7 2.0 %collective-permute-start = (f32[384,384]{1,0:T(8,128)S(1)}, f32[384,384]{1,0:T(8,128)}, u32[]{:S(2)}, u32[]{:S(2)}) collective-permute-start(f32[384,384]{1,0:T(8,128)S(1)} %get-tuple-element.13), channel_id=1, source_target_pairs={{0,4},{4,8},{8,12},{12,16},{16,20},{20,24},{24,28},{28,32},{32,36}... | collective-permute-start | bytes 1769480 | tf_op jit(solution)/shard_map/ppermute | solution.py:10
  32.8 2.5 %reshape.159 = bf16[256,1,392]{2,1,0:T(2,128)(2,1)S(1)} reshape(bf16[256,2,196]{2,1,0:T(2,128)(2,1)} %all-to-all-done) | data formatting | bytes 401408
  37.2 8.1 %collective-permute-done = f32[384,384]{1,0:T(8,128)} collective-permute-done((f32[384,384]{1,0:T(8,128)S(1)}, f32[384,384]{1,0:T(8,128)}, u32[]{:S(2)}, u32[]{:S(2)}) %collective-permute-start) | collective-permute-done | bytes 589856 | tf_op jit(solution)/shard_map/ppermute | solution.py:10
  45.4 2.3 %fusion.37 = f32[384,384]{1,0:T(8,128)S(1)} fusion(f32[384,384]{1,0:T(8,128)S(1)} %get-tuple-element.13, f32[384,384]{1,0:T(8,128)} %collective-permute-done), kind=kOutput, calls=%fused_computation.84 | convolution fusion | flops 679477248 | bytes 1769472 | tf_op jit(solution)/shard_map/dot_general | solution.py:75
  47.7 2.1 %collective-permute-start.1 = (f32[384,384]{1,0:T(8,128)S(1)}, f32[384,384]{1,0:T(8,128)S(1)}, u32[]{:S(2)}, u32[]{:S(2)}) collective-permute-start(f32[384,384]{1,0:T(8,128)S(1)} %fusion.37), channel_id=1, source_target_pairs={{0,8},{4,12},{8,16},{12,20},{16,24},{20,28},{24,32},{28,36},{32,40... | collective-permute-start | bytes 1769480 | tf_op jit(solution)/shard_map/ppermute | solution.py:10
  51.9 2.2 %collective-permute-done.5 = f32[8,384]{1,0:T(8,128)S(1)} collective-permute-done((f32[8,384]{1,0:T(8,128)S(1)}, f32[8,384]{1,0:T(8,128)S(1)}, u32[]{:S(2)}, u32[]{:S(2)}) %collective-permute-start.5) | collective-permute-done | bytes 12320 | tf_op jit(solution)/shard_map/ppermute | solution.py:17
  54.1 3.0 %collective-permute-start.6 = (f32[8,384]{1,0:T(8,128)S(1)}, f32[8,384]{1,0:T(8,128)S(1)}, u32[]{:S(2)}, u32[]{:S(2)}) collective-permute-start(f32[8,384]{1,0:T(8,128)S(1)} %fusion.36), channel_id=1, source_target_pairs={{0,2},{1,3},{2,0},{3,1},{4,6},{5,7},{6,4},{7,5},{8,10},{9,11},{10,... | collective-permute-start | bytes 36872 | tf_op jit(solution)/shard_map/ppermute | solution.py:17
  59.3 4.6 %collective-permute-done.1 = f32[384,384]{1,0:T(8,128)S(1)} collective-permute-done((f32[384,384]{1,0:T(8,128)S(1)}, f32[384,384]{1,0:T(8,128)S(1)}, u32[]{:S(2)}, u32[]{:S(2)}) %collective-permute-start.1) | collective-permute-done | bytes 589856 | tf_op jit(solution)/shard_map/ppermute | solution.py:10
  65.2 1.9 %collective-permute-start.2 = (f32[384,384]{1,0:T(8,128)S(1)}, f32[384,384]{1,0:T(8,128)S(1)}, u32[]{:S(2)}, u32[]{:S(2)}) collective-permute-start(f32[384,384]{1,0:T(8,128)S(1)} %fusion.38), channel_id=1, source_target_pairs={{0,16},{4,20},{8,24},{12,28},{16,32},{20,36},{24,40},{28,44},{32,4... | collective-permute-start | bytes 1769480 | tf_op jit(solution)/shard_map/ppermute | solution.py:10
  67.1 1.7 convolution_reduce_fusion.20
  68.9 1.7 convolution_reduce_fusion.19
  70.6 1.7 convolution_reduce_fusion.18
  72.4 1.7 convolution_reduce_fusion.17
  74.1 6.7 %collective-permute-done.2 = f32[384,384]{1,0:T(8,128)S(1)} collective-permute-done((f32[384,384]{1,0:T(8,128)S(1)}, f32[384,384]{1,0:T(8,128)S(1)}, u32[]{:S(2)}, u32[]{:S(2)}) %collective-permute-start.2) | collective-permute-done | bytes 589856 | tf_op jit(solution)/shard_map/ppermute | solution.py:10
  82.1 1.9 %collective-permute-start.3 = (f32[384,384]{1,0:T(8,128)S(1)}, f32[384,384]{1,0:T(8,128)S(1)}, u32[]{:S(2)}, u32[]{:S(2)}) collective-permute-start(f32[384,384]{1,0:T(8,128)S(1)} %fusion.39), channel_id=1, source_target_pairs={{0,32},{4,36},{8,40},{12,44},{16,48},{20,52},{24,56},{28,60},{32,6... | collective-permute-start | bytes 1769480 | tf_op jit(solution)/shard_map/ppermute | solution.py:10
  86.0 1.9 %collective-permute-start.7 = (f32[384]{0:T(512)S(1)}, f32[384]{0:T(512)S(1)}, u32[]{:S(2)}, u32[]{:S(2)}) collective-permute-start(f32[384]{0:T(512)S(1)} %add_select_fusion), channel_id=1, source_target_pairs={{0,4},{4,8},{8,12},{12,16},{16,20},{20,24},{24,28},{28,32},{32,36}... | collective-permute-start | bytes 4616 | tf_op jit(solution)/shard_map/ppermute | solution.py:10
  88.0 8.4 %collective-permute-done.7 = f32[384]{0:T(512)S(1)} collective-permute-done((f32[384]{0:T(512)S(1)}, f32[384]{0:T(512)S(1)}, u32[]{:S(2)}, u32[]{:S(2)}) %collective-permute-start.7) | collective-permute-done | bytes 1568 | tf_op jit(solution)/shard_map/ppermute | solution.py:10
  97.7 1.9 %collective-permute-start.4 = (f32[384,384]{1,0:T(8,128)S(1)}, f32[384,384]{1,0:T(8,128)S(1)}, u32[]{:S(2)}, u32[]{:S(2)}) collective-permute-start(f32[384,384]{1,0:T(8,128)S(1)} %fusion.40), channel_id=1, source_target_pairs={{0,64},{4,68},{8,72},{12,76},{16,80},{20,84},{24,88},{28,92},{32,9... | collective-permute-start | bytes 1769480 | tf_op jit(solution)/shard_map/ppermute | solution.py:10
  100.3 2.8 %collective-permute-start.8 = (f32[384]{0:T(512)S(1)}, f32[384]{0:T(512)S(1)}, u32[]{:S(2)}, u32[]{:S(2)}) collective-permute-start(f32[384]{0:T(512)S(1)} %add.82), channel_id=1, source_target_pairs={{0,8},{4,12},{8,16},{12,20},{16,24},{20,28},{24,32},{28,36},{32,40... | collective-permute-start | bytes 4616 | tf_op jit(solution)/shard_map/ppermute | solution.py:10
  103.1 23.1 %collective-permute-done.8 = f32[384]{0:T(512)S(1)} collective-permute-done((f32[384]{0:T(512)S(1)}, f32[384]{0:T(512)S(1)}, u32[]{:S(2)}, u32[]{:S(2)}) %collective-permute-start.8) | collective-permute-done | bytes 1568 | tf_op jit(solution)/shard_map/ppermute | solution.py:10
  126.9 1.9 %collective-permute-start.9 = (f32[384]{0:T(512)S(1)}, f32[384]{0:T(512)S(1)}, u32[]{:S(2)}, u32[]{:S(2)}) collective-permute-start(f32[384]{0:T(512)S(1)} %add.83), channel_id=1, source_target_pairs={{0,16},{4,20},{8,24},{12,28},{16,32},{20,36},{24,40},{28,44},{32,4... | collective-permute-start | bytes 4616 | tf_op jit(solution)/shard_map/ppermute | solution.py:10
  128.8 7.2 %collective-permute-done.9 = f32[384]{0:T(512)S(1)} collective-permute-done((f32[384]{0:T(512)S(1)}, f32[384]{0:T(512)S(1)}, u32[]{:S(2)}, u32[]{:S(2)}) %collective-permute-start.9) | collective-permute-done | bytes 1568 | tf_op jit(solution)/shard_map/ppermute | solution.py:10
  136.6 2.4 %collective-permute-start.10 = (f32[384]{0:T(512)S(1)}, f32[384]{0:T(512)S(1)}, u32[]{:S(2)}, u32[]{:S(2)}) collective-permute-start(f32[384]{0:T(512)S(1)} %add.84), channel_id=1, source_target_pairs={{0,32},{4,36},{8,40},{12,44},{16,48},{20,52},{24,56},{28,60},{32,6... | collective-permute-start | bytes 4616 | tf_op jit(solution)/shard_map/ppermute | solution.py:10
  139.1 4.2 %collective-permute-done.10 = f32[384]{0:T(512)S(1)} collective-permute-done((f32[384]{0:T(512)S(1)}, f32[384]{0:T(512)S(1)}, u32[]{:S(2)}, u32[]{:S(2)}) %collective-permute-start.10) | collective-permute-done | bytes 1568 | tf_op jit(solution)/shard_map/ppermute | solution.py:10
  144.0 1.9 %collective-permute-start.11 = (f32[384]{0:T(512)S(1)}, f32[384]{0:T(512)S(1)}, u32[]{:S(2)}, u32[]{:S(2)}) collective-permute-start(f32[384]{0:T(512)S(1)} %add.85), channel_id=1, source_target_pairs={{0,64},{4,68},{8,72},{12,76},{16,80},{20,84},{24,88},{28,92},{32,9... | collective-permute-start | bytes 4616 | tf_op jit(solution)/shard_map/ppermute | solution.py:10
  145.9 5.7 %collective-permute-done.11 = f32[384]{0:T(512)S(1)} collective-permute-done((f32[384]{0:T(512)S(1)}, f32[384]{0:T(512)S(1)}, u32[]{:S(2)}, u32[]{:S(2)}) %collective-permute-start.11) | collective-permute-done | bytes 1568 | tf_op jit(solution)/shard_map/ppermute | solution.py:10
  153.8 7.9 %collective-permute-done.12 = f32[384]{0:T(512)S(1)} collective-permute-done((f32[384]{0:T(512)S(1)}, f32[384]{0:T(512)S(1)}, u32[]{:S(2)}, u32[]{:S(2)}) %collective-permute-start.12) | collective-permute-done | bytes 1568 | tf_op jit(solution)/shard_map/ppermute | solution.py:10
  163.6 1.9 %collective-permute-start.13 = (f32[384]{0:T(512)S(1)}, f32[384]{0:T(512)S(1)}, u32[]{:S(2)}, u32[]{:S(2)}) collective-permute-start(f32[384]{0:T(512)S(1)} %add.87), channel_id=1, source_target_pairs={{0,4},{4,8},{8,12},{12,16},{16,20},{20,24},{24,28},{28,32},{32,36}... | collective-permute-start | bytes 4616 | tf_op jit(solution)/shard_map/ppermute | solution.py:10
  165.5 6.3 %collective-permute-done.13 = f32[384]{0:T(512)S(1)} collective-permute-done((f32[384]{0:T(512)S(1)}, f32[384]{0:T(512)S(1)}, u32[]{:S(2)}, u32[]{:S(2)}) %collective-permute-start.13) | collective-permute-done | bytes 1568 | tf_op jit(solution)/shard_map/ppermute | solution.py:10
  (115 shorter events, 31.6 us)
Async XLA Ops:
  0.0 49.8 %copy-start = (f32[8,384,48]{1,2,0:T(8,128)S(1)}, f32[8,384,48]{1,2,0:T(8,128)}, u32[]{:S(2)}) copy-start(f32[8,384,48]{1,2,0:T(8,128)} %param.8) | copy-start | bytes 1769476
  5.7 27.1 %all-to-all-start = ((bf16[256,2,196]{2,1,0:T(2,128)(2,1)}), bf16[256,2,196]{2,1,0:T(2,128)(2,1)}, u32[]{:S(2)}, u32[]{:S(2)}) async-start(bf16[256,2,196]{2,1,0:T(2,128)(2,1)} %reshape.158), calls=%async_computation | async-start | bytes 524288 | tf_op jit(solution)/shard_map/all_to_all | solution.py:45
  29.4 22.4 %copy-start.1 = (f32[384]{0:T(512)S(1)}, f32[384]{0:T(512)}, u32[]{:S(2)}) copy-start(f32[384]{0:T(512)} %param.9) | copy-start | bytes 4612
  29.5 54.5 %slice-start = ((s8[4718592]{0:T(1024)(128)(4,1)}), s8[524288]{0:T(1024)(128)(4,1)S(1)}, s32[]{:S(2)}) async-start(s8[4718592]{0:T(1024)(128)(4,1)} %bitcast.133), calls=%async_computation.1 | async-start | bytes 1048576
  30.7 14.6 %collective-permute-start = (f32[384,384]{1,0:T(8,128)S(1)}, f32[384,384]{1,0:T(8,128)}, u32[]{:S(2)}, u32[]{:S(2)}) collective-permute-start(f32[384,384]{1,0:T(8,128)S(1)} %get-tuple-element.13), channel_id=1, source_target_pairs={{0,4},{4,8},{8,12},{12,16},{16,20},{20,24},{24,28},{28,32},{32,36}... | collective-permute-start | bytes 1769480 | tf_op jit(solution)/shard_map/ppermute | solution.py:10
  37.2 46.8 %slice-start.1 = ((s8[4718592]{0:T(1024)(128)(4,1)}), s8[4194304]{0:T(1024)(128)(4,1)S(1)}, s32[]{:S(2)}) async-start(s8[4718592]{0:T(1024)(128)(4,1)} %bitcast.133), calls=%async_computation.2 | async-start | bytes 8388608
  47.7 16.2 %collective-permute-start.1 = (f32[384,384]{1,0:T(8,128)S(1)}, f32[384,384]{1,0:T(8,128)S(1)}, u32[]{:S(2)}, u32[]{:S(2)}) collective-permute-start(f32[384,384]{1,0:T(8,128)S(1)} %fusion.37), channel_id=1, source_target_pairs={{0,8},{4,12},{8,16},{12,20},{16,24},{20,28},{24,32},{28,36},{32,40... | collective-permute-start | bytes 1769480 | tf_op jit(solution)/shard_map/ppermute | solution.py:10
  50.3 3.8 %collective-permute-start.5 = (f32[8,384]{1,0:T(8,128)S(1)}, f32[8,384]{1,0:T(8,128)S(1)}, u32[]{:S(2)}, u32[]{:S(2)}) collective-permute-start(f32[8,384]{1,0:T(8,128)S(1)} %bitcast.140), channel_id=1, source_target_pairs={{0,1},{1,0},{2,3},{3,2},{4,5},{5,4},{6,7},{7,6},{8,9},{9,8},{10,11... | collective-permute-start | bytes 36872 | tf_op jit(solution)/shard_map/ppermute | solution.py:17
  54.1 5.2 %collective-permute-start.6 = (f32[8,384]{1,0:T(8,128)S(1)}, f32[8,384]{1,0:T(8,128)S(1)}, u32[]{:S(2)}, u32[]{:S(2)}) collective-permute-start(f32[8,384]{1,0:T(8,128)S(1)} %fusion.36), channel_id=1, source_target_pairs={{0,2},{1,3},{2,0},{3,1},{4,6},{5,7},{6,4},{7,5},{8,10},{9,11},{10,... | collective-permute-start | bytes 36872 | tf_op jit(solution)/shard_map/ppermute | solution.py:17
  65.2 15.6 %collective-permute-start.2 = (f32[384,384]{1,0:T(8,128)S(1)}, f32[384,384]{1,0:T(8,128)S(1)}, u32[]{:S(2)}, u32[]{:S(2)}) collective-permute-start(f32[384,384]{1,0:T(8,128)S(1)} %fusion.38), channel_id=1, source_target_pairs={{0,16},{4,20},{8,24},{12,28},{16,32},{20,36},{24,40},{28,44},{32,4... | collective-permute-start | bytes 1769480 | tf_op jit(solution)/shard_map/ppermute | solution.py:10
  82.1 14.3 %collective-permute-start.3 = (f32[384,384]{1,0:T(8,128)S(1)}, f32[384,384]{1,0:T(8,128)S(1)}, u32[]{:S(2)}, u32[]{:S(2)}) collective-permute-start(f32[384,384]{1,0:T(8,128)S(1)} %fusion.39), channel_id=1, source_target_pairs={{0,32},{4,36},{8,40},{12,44},{16,48},{20,52},{24,56},{28,60},{32,6... | collective-permute-start | bytes 1769480 | tf_op jit(solution)/shard_map/ppermute | solution.py:10
  86.0 10.4 %collective-permute-start.7 = (f32[384]{0:T(512)S(1)}, f32[384]{0:T(512)S(1)}, u32[]{:S(2)}, u32[]{:S(2)}) collective-permute-start(f32[384]{0:T(512)S(1)} %add_select_fusion), channel_id=1, source_target_pairs={{0,4},{4,8},{8,12},{12,16},{16,20},{20,24},{24,28},{28,32},{32,36}... | collective-permute-start | bytes 4616 | tf_op jit(solution)/shard_map/ppermute | solution.py:10
  97.7 64.0 %collective-permute-start.4 = (f32[384,384]{1,0:T(8,128)S(1)}, f32[384,384]{1,0:T(8,128)S(1)}, u32[]{:S(2)}, u32[]{:S(2)}) collective-permute-start(f32[384,384]{1,0:T(8,128)S(1)} %fusion.40), channel_id=1, source_target_pairs={{0,64},{4,68},{8,72},{12,76},{16,80},{20,84},{24,88},{28,92},{32,9... | collective-permute-start | bytes 1769480 | tf_op jit(solution)/shard_map/ppermute | solution.py:10
  100.3 25.9 %collective-permute-start.8 = (f32[384]{0:T(512)S(1)}, f32[384]{0:T(512)S(1)}, u32[]{:S(2)}, u32[]{:S(2)}) collective-permute-start(f32[384]{0:T(512)S(1)} %add.82), channel_id=1, source_target_pairs={{0,8},{4,12},{8,16},{12,20},{16,24},{20,28},{24,32},{28,36},{32,40... | collective-permute-start | bytes 4616 | tf_op jit(solution)/shard_map/ppermute | solution.py:10
  126.9 9.1 %collective-permute-start.9 = (f32[384]{0:T(512)S(1)}, f32[384]{0:T(512)S(1)}, u32[]{:S(2)}, u32[]{:S(2)}) collective-permute-start(f32[384]{0:T(512)S(1)} %add.83), channel_id=1, source_target_pairs={{0,16},{4,20},{8,24},{12,28},{16,32},{20,36},{24,40},{28,44},{32,4... | collective-permute-start | bytes 4616 | tf_op jit(solution)/shard_map/ppermute | solution.py:10
  136.6 6.7 %collective-permute-start.10 = (f32[384]{0:T(512)S(1)}, f32[384]{0:T(512)S(1)}, u32[]{:S(2)}, u32[]{:S(2)}) collective-permute-start(f32[384]{0:T(512)S(1)} %add.84), channel_id=1, source_target_pairs={{0,32},{4,36},{8,40},{12,44},{16,48},{20,52},{24,56},{28,60},{32,6... | collective-permute-start | bytes 4616 | tf_op jit(solution)/shard_map/ppermute | solution.py:10
  144.0 7.6 %collective-permute-start.11 = (f32[384]{0:T(512)S(1)}, f32[384]{0:T(512)S(1)}, u32[]{:S(2)}, u32[]{:S(2)}) collective-permute-start(f32[384]{0:T(512)S(1)} %add.85), channel_id=1, source_target_pairs={{0,64},{4,68},{8,72},{12,76},{16,80},{20,84},{24,88},{28,92},{32,9... | collective-permute-start | bytes 4616 | tf_op jit(solution)/shard_map/ppermute | solution.py:10
  152.3 9.4 %collective-permute-start.12 = (f32[384]{0:T(512)S(1)}, f32[384]{0:T(512)S(1)}, u32[]{:S(2)}, u32[]{:S(2)}) collective-permute-start(f32[384]{0:T(512)S(1)} %add.86), channel_id=1, source_target_pairs={{0,128},{4,132},{8,136},{12,140},{16,144},{20,148},{24,152},{28,15... | collective-permute-start | bytes 4616 | tf_op jit(solution)/shard_map/ppermute | solution.py:10
  163.6 8.2 %collective-permute-start.13 = (f32[384]{0:T(512)S(1)}, f32[384]{0:T(512)S(1)}, u32[]{:S(2)}, u32[]{:S(2)}) collective-permute-start(f32[384]{0:T(512)S(1)} %add.87), channel_id=1, source_target_pairs={{0,4},{4,8},{8,12},{12,16},{16,20},{20,24},{24,28},{28,32},{32,36}... | collective-permute-start | bytes 4616 | tf_op jit(solution)/shard_map/ppermute | solution.py:10

commit v3 on v2

--- a/solution.py
+++ b/solution.py
@@ -11,12 +11,16 @@
 
 
 def summed_over(block, axis):
-    distance = 1
-    while distance < lax.axis_size(axis):
-        route = [(i, i ^ distance) for i in range(lax.axis_size(axis))]
-        block = block + lax.ppermute(block, axis, route)
-        distance *= 2
-    return block
+    count = lax.axis_size(axis)
+    shares = [block] + [
+        lax.ppermute(block, axis, [(i, (i + shift) % count) for i in range(count)])
+        for shift in range(1, count)
+    ]
+    by_source = jnp.stack(shares)[(lax.axis_index(axis) - jnp.arange(count)) % count]
+    total = by_source[0]
+    for source in range(1, count):
+        total = total + by_source[source]
+    return total
 
 
 def on_device(
@@ -65,14 +69,18 @@
     acc_vec = jnp.where(is_first, jnp.dot(slab_map, prior_mean, precision=exact) + offset, offset)
     acc_map = jnp.where(is_first, jnp.zeros_like(slab_map), slab_map)
     distance = 1
+    history = [acc_vec]
     while distance < tm_count:
+        last = distance * 2 >= tm_count
+        if len(history) >= 3 and not last:
+            acc_map, _ = lax.optimization_barrier((acc_map, history[-3]))
         got_vec = passed_along(acc_vec, "tm", distance)
-        last = distance * 2 >= tm_count
         if not last:
             got_map = passed_along(acc_map, "tm", distance)
         acc_vec = jnp.dot(acc_map, got_vec, precision=exact) + acc_vec
         if not last:
             acc_map = jnp.dot(acc_map, got_map, precision=exact)
+        history.append(acc_vec)
         distance *= 2
     state = jnp.where(is_first, prior_mean, passed_along(acc_vec, "tm", 1))
     means = []

time: 179 us -> 192 us (1.073)
  matrix products: 37.3 us -> 49 us
    dot_general x8, matrix products: 5.19 us -> 13.7 us  [on_device(): state = jnp.dot(trans[step], state, precision=exact) + forcing[step]]
    dot_general x7, matrix products: 8.79 us -> 12 us  [on_device(): offset = jnp.dot(trans[step], offset, precision=exact) + forcing[step]]
    ppermute x12, starting transfers between devices: 24.3 us -> 27.1 us  [passed_along(): return lax.ppermute(block, axis, route)]
    unnamed x11 -> x7, local copies, waits for them, and re-layouts: 3.36 us -> 1.26 us
    ppermute x2 -> x3, waiting for transfers between devices: 3.79 us -> 4.15 us  [summed_over(): lax.ppermute(block, axis, [(i, (i + shift) % count) for i in range(count)])]
    ppermute x2 -> x3, starting transfers between devices: 4.55 us -> 4.5 us  [summed_over(): lax.ppermute(block, axis, [(i, (i + shift) % count) for i in range(count)])]
  transfers between devices with their start and end apart: 15 -> 16, of which waited for: 12 -> 12; matrix products, arithmetic and copies ran while one was open for 16% -> 15% of each run, Pallas kernels for 0% -> 0%
where the time goes in v3:
time: 192 us; the launch traced here: 191 us
  waiting for transfers between devices  87 us (45%)
  matrix products  49 us (26%)
  starting transfers between devices  45.4 us (24%)
  local copies, waits for them, and re-layouts  6.02 us (3%)
  other arithmetic  2.65 us (1%)
    ppermute x12, waiting for transfers between devices, passed_along(): return lax.ppermute(block, axis, route)  82.9 us
    ppermute x12, starting transfers between devices, passed_along(): return lax.ppermute(block, axis, route)  27.1 us
    all_to_all x1, starting transfers between devices, on_device(): lax.all_to_all(sent, ('tm', 'ingest'), split_axis=0, concat_axis=0, tiled...  13.8 us
    dot_general x8, matrix products, on_device(): state = jnp.dot(trans[step], state, precision=exact) + forcing[step]  13.7 us
    dot_general x7, matrix products, on_device(): offset = jnp.dot(trans[step], offset, precision=exact) + forcing[step]  12 us
    dot_general x3, matrix products, on_device(): jnp.einsum('jab,jbc->jac', pairs[:, 1], pairs[:, 0], precision=exact)  10.2 us
    dot_general x5, matrix products, on_device(): acc_map = jnp.dot(acc_map, got_map, precision=exact)  7.42 us
    ppermute x3, starting transfers between devices, summed_over(): lax.ppermute(block, axis, [(i, (i + shift) % count) for i in range(count)])  4.5 us
  transfers between devices with their start and end apart: 16, of which 12 were waited for; matrix products, arithmetic and copies ran while one was open for 15% of the time, Pallas kernels for 0%

profile of v3, /device:TPU:128, one launch (start us, length us, event | category | flops | bytes accessed | tf_op | source)
XLA Modules:
  0.0 190.9 jit_solution(8641495654557322927)
XLA Ops:
  5.7 13.8 %all-to-all-start = ((bf16[256,2,196]{2,1,0:T(2,128)(2,1)}), bf16[256,2,196]{2,1,0:T(2,128)(2,1)S(1)}, u32[]{:S(2)}, u32[]{:S(2)}) async-start(bf16[256,2,196]{2,1,0:T(2,128)(2,1)} %reshape.234), calls=%async_computation | async-start | bytes 524288 | tf_op jit(solution)/shard_map/all_to_all | solution.py:49
  19.5 6.5 %fusion = f32[4,384,384]{2,1,0:T(8,128)S(1)} fusion(f32[4,2,384,384]{3,2,1,0:T(8,128)} %bitcast.137), kind=kOutput, calls=%fused_computation.2 | convolution fusion | flops 2717908992 | bytes 7077888 | tf_op jit(solution)/shard_map/jab,jbc->jac/dot_general | solution.py:61
  26.1 2.4 %convolution_bitcast_fusion = f32[1,2,384,384]{3,2,1,0:T(8,128)S(1)} fusion(f32[2,2,384,384]{3,2,1,0:T(8,128)S(1)} %bitcast.138), kind=kOutput, calls=%fused_computation.4 | convolution fusion | flops 1358954496 | bytes 3538944 | tf_op jit(solution)/shard_map/jab,jbc->jac/dot_general | solution.py:61
  29.7 2.0 %collective-permute-start = (f32[384,384]{1,0:T(8,128)S(1)}, f32[384,384]{1,0:T(8,128)}, u32[]{:S(2)}, u32[]{:S(2)}) collective-permute-start(f32[384,384]{1,0:T(8,128)S(1)} %get-tuple-element.21), channel_id=1, source_target_pairs={{0,4},{4,8},{8,12},{12,16},{16,20},{20,24},{24,28},{28,32},{32,36}... | collective-permute-start | bytes 1769480 | tf_op jit(solution)/shard_map/ppermute | solution.py:10
  35.3 2.8 %collective-permute-start.4 = (f32[8,384]{1,0:T(8,128)S(1)}, f32[8,384]{1,0:T(8,128)S(1)}, u32[]{:S(2)}, u32[]{:S(2)}) collective-permute-start(f32[8,384]{1,0:T(8,128)S(1)} %bitcast.143), channel_id=1, source_target_pairs={{0,3},{1,0},{2,1},{3,2},{4,7},{5,4},{6,5},{7,6},{8,11},{9,8},{10,9... | collective-permute-start | bytes 36872 | tf_op jit(solution)/shard_map/ppermute | solution.py:16
  39.8 3.5 %collective-permute-done.3 = f32[8,384]{1,0:T(8,128)S(1)} collective-permute-done((f32[8,384]{1,0:T(8,128)S(1)}, f32[8,384]{1,0:T(8,128)S(1)}, u32[]{:S(2)}, u32[]{:S(2)}) %collective-permute-start.3) | collective-permute-done | bytes 12320 | tf_op jit(solution)/shard_map/ppermute | solution.py:16
  44.6 1.7 convolution_reduce_fusion.20
  46.3 1.7 convolution_reduce_fusion.19
  48.1 1.7 convolution_reduce_fusion.18
  49.8 1.7 convolution_reduce_fusion.17
  51.6 2.3 %fusion.38 = f32[384,384]{1,0:T(8,128)S(1)} fusion(f32[384,384]{1,0:T(8,128)S(1)} %get-tuple-element.21, f32[384,384]{1,0:T(8,128)} %collective-permute-done), kind=kOutput, calls=%fused_computation.96 | convolution fusion | flops 679477248 | bytes 1769472 | tf_op jit(solution)/shard_map/dot_general | solution.py:82
  53.9 3.4 %collective-permute-start.1 = (f32[384,384]{1,0:T(8,128)S(1)}, f32[384,384]{1,0:T(8,128)S(1)}, u32[]{:S(2)}, u32[]{:S(2)}) collective-permute-start(f32[384,384]{1,0:T(8,128)S(1)} %fusion.38), channel_id=1, source_target_pairs={{0,8},{4,12},{8,16},{12,20},{16,24},{20,28},{24,32},{28,36},{32,40... | collective-permute-start | bytes 1769480 | tf_op jit(solution)/shard_map/ppermute | solution.py:10
  57.4 1.7 convolution_reduce_fusion.16
  62.6 12.0 %collective-permute-done.1 = f32[384,384]{1,0:T(8,128)S(1)} collective-permute-done((f32[384,384]{1,0:T(8,128)S(1)}, f32[384,384]{1,0:T(8,128)S(1)}, u32[]{:S(2)}, u32[]{:S(2)}) %collective-permute-start.1) | collective-permute-done | bytes 589856 | tf_op jit(solution)/shard_map/ppermute | solution.py:10
  75.9 1.9 %collective-permute-start.5 = (f32[384,384]{1,0:T(8,128)S(1)}, f32[384,384]{1,0:T(8,128)S(1)}, u32[]{:S(2)}, u32[]{:S(2)}) collective-permute-start(f32[384,384]{1,0:T(8,128)S(1)} %fusion.39), channel_id=1, source_target_pairs={{0,16},{4,20},{8,24},{12,28},{16,32},{20,36},{24,40},{28,44},{32,4... | collective-permute-start | bytes 1769480 | tf_op jit(solution)/shard_map/ppermute | solution.py:10
  77.8 1.9 %collective-permute-start.6 = (f32[384]{0:T(512)S(1)}, f32[384]{0:T(512)S(1)}, u32[]{:S(2)}, u32[]{:S(2)}) collective-permute-start(f32[384]{0:T(512)S(1)} %add_select_fusion), channel_id=1, source_target_pairs={{0,4},{4,8},{8,12},{12,16},{16,20},{20,24},{24,28},{28,32},{32,36}... | collective-permute-start | bytes 4616 | tf_op jit(solution)/shard_map/ppermute | solution.py:10
  79.7 11.7 %collective-permute-done.6 = f32[384]{0:T(512)S(1)} collective-permute-done((f32[384]{0:T(512)S(1)}, f32[384]{0:T(512)S(1)}, u32[]{:S(2)}, u32[]{:S(2)}) %collective-permute-start.6) | collective-permute-done | bytes 1568 | tf_op jit(solution)/shard_map/ppermute | solution.py:10
  92.1 3.9 %collective-permute-done.5 = f32[384,384]{1,0:T(8,128)S(1)} collective-permute-done((f32[384,384]{1,0:T(8,128)S(1)}, f32[384,384]{1,0:T(8,128)S(1)}, u32[]{:S(2)}, u32[]{:S(2)}) %collective-permute-start.5) | collective-permute-done | bytes 589856 | tf_op jit(solution)/shard_map/ppermute | solution.py:10
  97.3 1.9 %collective-permute-start.7 = (f32[384,384]{1,0:T(8,128)S(1)}, f32[384,384]{1,0:T(8,128)S(1)}, u32[]{:S(2)}, u32[]{:S(2)}) collective-permute-start(f32[384,384]{1,0:T(8,128)S(1)} %fusion.41), channel_id=1, source_target_pairs={{0,32},{4,36},{8,40},{12,44},{16,48},{20,52},{24,56},{28,60},{32,6... | collective-permute-start | bytes 1769480 | tf_op jit(solution)/shard_map/ppermute | solution.py:10
  99.2 1.9 %collective-permute-start.8 = (f32[384]{0:T(512)S(1)}, f32[384]{0:T(512)S(1)}, u32[]{:S(2)}, u32[]{:S(2)}) collective-permute-start(f32[384]{0:T(512)S(1)} %add.114), channel_id=1, source_target_pairs={{0,8},{4,12},{8,16},{12,20},{16,24},{20,28},{24,32},{28,36},{32,40... | collective-permute-start | bytes 4616 | tf_op jit(solution)/shard_map/ppermute | solution.py:10
  101.1 9.3 %collective-permute-done.8 = f32[384]{0:T(512)S(1)} collective-permute-done((f32[384]{0:T(512)S(1)}, f32[384]{0:T(512)S(1)}, u32[]{:S(2)}, u32[]{:S(2)}) %collective-permute-start.8) | collective-permute-done | bytes 1568 | tf_op jit(solution)/shard_map/ppermute | solution.py:10
  111.1 3.0 %collective-permute-done.7 = f32[384,384]{1,0:T(8,128)S(1)} collective-permute-done((f32[384,384]{1,0:T(8,128)S(1)}, f32[384,384]{1,0:T(8,128)S(1)}, u32[]{:S(2)}, u32[]{:S(2)}) %collective-permute-start.7) | collective-permute-done | bytes 589856 | tf_op jit(solution)/shard_map/ppermute | solution.py:10
  115.4 1.9 %collective-permute-start.9 = (f32[384,384]{1,0:T(8,128)S(1)}, f32[384,384]{1,0:T(8,128)S(1)}, u32[]{:S(2)}, u32[]{:S(2)}) collective-permute-start(f32[384,384]{1,0:T(8,128)S(1)} %fusion.42), channel_id=1, source_target_pairs={{0,64},{4,68},{8,72},{12,76},{16,80},{20,84},{24,88},{28,92},{32,9... | collective-permute-start | bytes 1769480 | tf_op jit(solution)/shard_map/ppermute | solution.py:10
  117.3 1.9 %collective-permute-start.10 = (f32[384]{0:T(512)S(1)}, f32[384]{0:T(512)S(1)}, u32[]{:S(2)}, u32[]{:S(2)}) collective-permute-start(f32[384]{0:T(512)S(1)} %add.115), channel_id=1, source_target_pairs={{0,16},{4,20},{8,24},{12,28},{16,32},{20,36},{24,40},{28,44},{32,4... | collective-permute-start | bytes 4616 | tf_op jit(solution)/shard_map/ppermute | solution.py:10
  119.2 19.3 %collective-permute-done.10 = f32[384]{0:T(512)S(1)} collective-permute-done((f32[384]{0:T(512)S(1)}, f32[384]{0:T(512)S(1)}, u32[]{:S(2)}, u32[]{:S(2)}) %collective-permute-start.10) | collective-permute-done | bytes 1568 | tf_op jit(solution)/shard_map/ppermute | solution.py:10
  139.2 4.7 %collective-permute-start.11 = (f32[384]{0:T(512)S(1)}, f32[384]{0:T(512)S(1)}, u32[]{:S(2)}, u32[]{:S(2)}) collective-permute-start(f32[384]{0:T(512)S(1)} %add.116), channel_id=1, source_target_pairs={{0,32},{4,36},{8,40},{12,44},{16,48},{20,52},{24,56},{28,60},{32,6... | collective-permute-start | bytes 4616 | tf_op jit(solution)/shard_map/ppermute | solution.py:10
  144.0 3.8 %collective-permute-done.11 = f32[384]{0:T(512)S(1)} collective-permute-done((f32[384]{0:T(512)S(1)}, f32[384]{0:T(512)S(1)}, u32[]{:S(2)}, u32[]{:S(2)}) %collective-permute-start.11) | collective-permute-done | bytes 1568 | tf_op jit(solution)/shard_map/ppermute | solution.py:10
  148.5 1.9 %collective-permute-start.12 = (f32[384]{0:T(512)S(1)}, f32[384]{0:T(512)S(1)}, u32[]{:S(2)}, u32[]{:S(2)}) collective-permute-start(f32[384]{0:T(512)S(1)} %add.117), channel_id=1, source_target_pairs={{0,64},{4,68},{8,72},{12,76},{16,80},{20,84},{24,88},{28,92},{32,9... | collective-permute-start | bytes 4616 | tf_op jit(solution)/shard_map/ppermute | solution.py:10
  150.4 5.7 %collective-permute-done.12 = f32[384]{0:T(512)S(1)} collective-permute-done((f32[384]{0:T(512)S(1)}, f32[384]{0:T(512)S(1)}, u32[]{:S(2)}, u32[]{:S(2)}) %collective-permute-start.12) | collective-permute-done | bytes 1568 | tf_op jit(solution)/shard_map/ppermute | solution.py:10
  158.2 7.9 %collective-permute-done.13 = f32[384]{0:T(512)S(1)} collective-permute-done((f32[384]{0:T(512)S(1)}, f32[384]{0:T(512)S(1)}, u32[]{:S(2)}, u32[]{:S(2)}) %collective-permute-start.13) | collective-permute-done | bytes 1568 | tf_op jit(solution)/shard_map/ppermute | solution.py:10
  168.1 1.9 %collective-permute-start.14 = (f32[384]{0:T(512)S(1)}, f32[384]{0:T(512)S(1)}, u32[]{:S(2)}, u32[]{:S(2)}) collective-permute-start(f32[384]{0:T(512)S(1)} %add.119), channel_id=1, source_target_pairs={{0,4},{4,8},{8,12},{12,16},{16,20},{20,24},{24,28},{28,32},{32,36}... | collective-permute-start | bytes 4616 | tf_op jit(solution)/shard_map/ppermute | solution.py:10
  170.0 6.3 %collective-permute-done.14 = f32[384]{0:T(512)S(1)} collective-permute-done((f32[384]{0:T(512)S(1)}, f32[384]{0:T(512)S(1)}, u32[]{:S(2)}, u32[]{:S(2)}) %collective-permute-start.14) | collective-permute-done | bytes 1568 | tf_op jit(solution)/shard_map/ppermute | solution.py:10
  (115 shorter events, 41.8 us)
Async XLA Ops:
  0.0 34.8 %copy-start = (f32[8,384,48]{1,2,0:T(8,128)S(1)}, f32[8,384,48]{1,2,0:T(8,128)}, u32[]{:S(2)}) copy-start(f32[8,384,48]{1,2,0:T(8,128)} %param.8) | copy-start | bytes 1769476
  5.7 26.8 %all-to-all-start = ((bf16[256,2,196]{2,1,0:T(2,128)(2,1)}), bf16[256,2,196]{2,1,0:T(2,128)(2,1)S(1)}, u32[]{:S(2)}, u32[]{:S(2)}) async-start(bf16[256,2,196]{2,1,0:T(2,128)(2,1)} %reshape.234), calls=%async_computation | async-start | bytes 524288 | tf_op jit(solution)/shard_map/all_to_all | solution.py:49
  26.1 5.7 %copy-start.1 = (f32[384]{0:T(512)S(1)}, f32[384]{0:T(512)}, u32[]{:S(2)}) copy-start(f32[384]{0:T(512)} %param.9) | copy-start | bytes 4612
  29.7 21.8 %collective-permute-start = (f32[384,384]{1,0:T(8,128)S(1)}, f32[384,384]{1,0:T(8,128)}, u32[]{:S(2)}, u32[]{:S(2)}) collective-permute-start(f32[384,384]{1,0:T(8,128)S(1)} %get-tuple-element.21), channel_id=1, source_target_pairs={{0,4},{4,8},{8,12},{12,16},{16,20},{20,24},{24,28},{28,32},{32,36}... | collective-permute-start | bytes 1769480 | tf_op jit(solution)/shard_map/ppermute | solution.py:10
  35.3 4.5 %collective-permute-start.4 = (f32[8,384]{1,0:T(8,128)S(1)}, f32[8,384]{1,0:T(8,128)S(1)}, u32[]{:S(2)}, u32[]{:S(2)}) collective-permute-start(f32[8,384]{1,0:T(8,128)S(1)} %bitcast.143), channel_id=1, source_target_pairs={{0,3},{1,0},{2,1},{3,2},{4,7},{5,4},{6,5},{7,6},{8,11},{9,8},{10,9... | collective-permute-start | bytes 36872 | tf_op jit(solution)/shard_map/ppermute | solution.py:16
  38.1 5.2 %collective-permute-start.3 = (f32[8,384]{1,0:T(8,128)S(1)}, f32[8,384]{1,0:T(8,128)S(1)}, u32[]{:S(2)}, u32[]{:S(2)}) collective-permute-start(f32[8,384]{1,0:T(8,128)S(1)} %bitcast.144), channel_id=1, source_target_pairs={{0,2},{1,3},{2,0},{3,1},{4,6},{5,7},{6,4},{7,5},{8,10},{9,11},{10,... | collective-permute-start | bytes 36872 | tf_op jit(solution)/shard_map/ppermute | solution.py:16
  38.9 5.0 %collective-permute-start.2 = (f32[8,384]{1,0:T(8,128)S(1)}, f32[8,384]{1,0:T(8,128)S(1)}, u32[]{:S(2)}, u32[]{:S(2)}) collective-permute-start(f32[8,384]{1,0:T(8,128)S(1)} %bitcast.145), channel_id=1, source_target_pairs={{0,1},{1,2},{2,3},{3,0},{4,5},{5,6},{6,7},{7,4},{8,9},{9,10},{10,1... | collective-permute-start | bytes 36872 | tf_op jit(solution)/shard_map/ppermute | solution.py:16
  53.9 20.7 %collective-permute-start.1 = (f32[384,384]{1,0:T(8,128)S(1)}, f32[384,384]{1,0:T(8,128)S(1)}, u32[]{:S(2)}, u32[]{:S(2)}) collective-permute-start(f32[384,384]{1,0:T(8,128)S(1)} %fusion.38), channel_id=1, source_target_pairs={{0,8},{4,12},{8,16},{12,20},{16,24},{20,28},{24,32},{28,36},{32,40... | collective-permute-start | bytes 1769480 | tf_op jit(solution)/shard_map/ppermute | solution.py:10
  75.9 20.1 %collective-permute-start.5 = (f32[384,384]{1,0:T(8,128)S(1)}, f32[384,384]{1,0:T(8,128)S(1)}, u32[]{:S(2)}, u32[]{:S(2)}) collective-permute-start(f32[384,384]{1,0:T(8,128)S(1)} %fusion.39), channel_id=1, source_target_pairs={{0,16},{4,20},{8,24},{12,28},{16,32},{20,36},{24,40},{28,44},{32,4... | collective-permute-start | bytes 1769480 | tf_op jit(solution)/shard_map/ppermute | solution.py:10
  77.8 13.7 %collective-permute-start.6 = (f32[384]{0:T(512)S(1)}, f32[384]{0:T(512)S(1)}, u32[]{:S(2)}, u32[]{:S(2)}) collective-permute-start(f32[384]{0:T(512)S(1)} %add_select_fusion), channel_id=1, source_target_pairs={{0,4},{4,8},{8,12},{12,16},{16,20},{20,24},{24,28},{28,32},{32,36}... | collective-permute-start | bytes 4616 | tf_op jit(solution)/shard_map/ppermute | solution.py:10
  97.3 16.8 %collective-permute-start.7 = (f32[384,384]{1,0:T(8,128)S(1)}, f32[384,384]{1,0:T(8,128)S(1)}, u32[]{:S(2)}, u32[]{:S(2)}) collective-permute-start(f32[384,384]{1,0:T(8,128)S(1)} %fusion.41), channel_id=1, source_target_pairs={{0,32},{4,36},{8,40},{12,44},{16,48},{20,52},{24,56},{28,60},{32,6... | collective-permute-start | bytes 1769480 | tf_op jit(solution)/shard_map/ppermute | solution.py:10
  99.2 11.2 %collective-permute-start.8 = (f32[384]{0:T(512)S(1)}, f32[384]{0:T(512)S(1)}, u32[]{:S(2)}, u32[]{:S(2)}) collective-permute-start(f32[384]{0:T(512)S(1)} %add.114), channel_id=1, source_target_pairs={{0,8},{4,12},{8,16},{12,20},{16,24},{20,28},{24,32},{28,36},{32,40... | collective-permute-start | bytes 4616 | tf_op jit(solution)/shard_map/ppermute | solution.py:10
  115.4 50.7 %collective-permute-start.9 = (f32[384,384]{1,0:T(8,128)S(1)}, f32[384,384]{1,0:T(8,128)S(1)}, u32[]{:S(2)}, u32[]{:S(2)}) collective-permute-start(f32[384,384]{1,0:T(8,128)S(1)} %fusion.42), channel_id=1, source_target_pairs={{0,64},{4,68},{8,72},{12,76},{16,80},{20,84},{24,88},{28,92},{32,9... | collective-permute-start | bytes 1769480 | tf_op jit(solution)/shard_map/ppermute | solution.py:10
  117.3 21.3 %collective-permute-start.10 = (f32[384]{0:T(512)S(1)}, f32[384]{0:T(512)S(1)}, u32[]{:S(2)}, u32[]{:S(2)}) collective-permute-start(f32[384]{0:T(512)S(1)} %add.115), channel_id=1, source_target_pairs={{0,16},{4,20},{8,24},{12,28},{16,32},{20,36},{24,40},{28,44},{32,4... | collective-permute-start | bytes 4616 | tf_op jit(solution)/shard_map/ppermute | solution.py:10
  139.2 8.5 %collective-permute-start.11 = (f32[384]{0:T(512)S(1)}, f32[384]{0:T(512)S(1)}, u32[]{:S(2)}, u32[]{:S(2)}) collective-permute-start(f32[384]{0:T(512)S(1)} %add.116), channel_id=1, source_target_pairs={{0,32},{4,36},{8,40},{12,44},{16,48},{20,52},{24,56},{28,60},{32,6... | collective-permute-start | bytes 4616 | tf_op jit(solution)/shard_map/ppermute | solution.py:10
  148.5 7.6 %collective-permute-start.12 = (f32[384]{0:T(512)S(1)}, f32[384]{0:T(512)S(1)}, u32[]{:S(2)}, u32[]{:S(2)}) collective-permute-start(f32[384]{0:T(512)S(1)} %add.117), channel_id=1, source_target_pairs={{0,64},{4,68},{8,72},{12,76},{16,80},{20,84},{24,88},{28,92},{32,9... | collective-permute-start | bytes 4616 | tf_op jit(solution)/shard_map/ppermute | solution.py:10
  156.7 9.4 %collective-permute-start.13 = (f32[384]{0:T(512)S(1)}, f32[384]{0:T(512)S(1)}, u32[]{:S(2)}, u32[]{:S(2)}) collective-permute-start(f32[384]{0:T(512)S(1)} %add.118), channel_id=1, source_target_pairs={{0,128},{4,132},{8,136},{12,140},{16,144},{20,148},{24,152},{28,15... | collective-permute-start | bytes 4616 | tf_op jit(solution)/shard_map/ppermute | solution.py:10
  168.1 8.2 %collective-permute-start.14 = (f32[384]{0:T(512)S(1)}, f32[384]{0:T(512)S(1)}, u32[]{:S(2)}, u32[]{:S(2)}) collective-permute-start(f32[384]{0:T(512)S(1)} %add.119), channel_id=1, source_target_pairs={{0,4},{4,8},{8,12},{12,16},{16,20},{20,24},{24,28},{28,32},{32,36}... | collective-permute-start | bytes 4616 | tf_op jit(solution)/shard_map/ppermute | solution.py:10

commit v4 on v3

--- a/solution.py
+++ b/solution.py
@@ -55,32 +55,43 @@
     partial_force = jnp.einsum("lsq,lq->ls", gain, drive_piece, precision=exact)
     forcing = summed_over(partial_force, "ingest")
 
-    level = trans
-    while level.shape[0] > 1:
-        pairs = level.reshape(level.shape[0] // 2, 2, state_width, state_width)
-        level = jnp.einsum("jab,jbc->jac", pairs[:, 1], pairs[:, 0], precision=exact)
-    slab_map = level[0]
-    offset = forcing[0]
-    for step in range(1, steps_here):
-        offset = jnp.dot(trans[step], offset, precision=exact) + forcing[step]
+    pairs = trans.reshape(steps_here // 2, 2, state_width, state_width)
+    force_pairs = forcing.reshape(steps_here // 2, 2, state_width)
+    level_t = jnp.einsum("jba,jcb->jac", pairs[:, 0], pairs[:, 1], precision=exact)
+    level_off = (
+        jnp.einsum("jab,jb->ja", pairs[:, 1], force_pairs[:, 0], precision=exact)
+        + force_pairs[:, 1]
+    )
+    while level_t.shape[0] > 1:
+        map_pairs = level_t.reshape(-1, 2, state_width, state_width)
+        off_pairs = level_off.reshape(-1, 2, state_width)
+        level_off = (
+            jnp.einsum("ja,jab->jb", off_pairs[:, 0], map_pairs[:, 1], precision=exact)
+            + off_pairs[:, 1]
+        )
+        level_t = jnp.einsum("jab,jbc->jac", map_pairs[:, 0], map_pairs[:, 1], precision=exact)
+    slab_t = level_t[0]
+    offset = level_off[0]
 
     tm_index = lax.axis_index("tm")
     is_first = tm_index == 0
-    acc_vec = jnp.where(is_first, jnp.dot(slab_map, prior_mean, precision=exact) + offset, offset)
-    acc_map = jnp.where(is_first, jnp.zeros_like(slab_map), slab_map)
+    acc_vec = jnp.where(is_first, jnp.dot(prior_mean, slab_t, precision=exact) + offset, offset)
+    acc_t = jnp.where(is_first, jnp.zeros_like(slab_t), slab_t)
     distance = 1
-    history = [acc_vec]
     while distance < tm_count:
-        last = distance * 2 >= tm_count
-        if len(history) >= 3 and not last:
-            acc_map, _ = lax.optimization_barrier((acc_map, history[-3]))
-        got_vec = passed_along(acc_vec, "tm", distance)
-        if not last:
-            got_map = passed_along(acc_map, "tm", distance)
-        acc_vec = jnp.dot(acc_map, got_vec, precision=exact) + acc_vec
-        if not last:
-            acc_map = jnp.dot(acc_map, got_map, precision=exact)
-        history.append(acc_vec)
+        if distance * 2 >= tm_count:
+            got_vec = passed_along(acc_vec, "tm", distance)
+            acc_vec = jnp.dot(got_vec, acc_t, precision=exact) + acc_vec
+        elif distance < 4:
+            got_vec = passed_along(acc_vec, "tm", distance)
+            got_t = passed_along(acc_t, "tm", distance)
+            acc_vec = jnp.dot(got_vec, acc_t, precision=exact) + acc_vec
+            acc_t = jnp.dot(got_t, acc_t, precision=exact)
+        else:
+            carried = jnp.concatenate([acc_t, acc_vec[None]], axis=0)
+            got = jnp.dot(passed_along(carried, "tm", distance), acc_t, precision=exact)
+            acc_t = got[:state_width]
+            acc_vec = got[state_width] + acc_vec
         distance *= 2
     state = jnp.where(is_first, prior_mean, passed_along(acc_vec, "tm", 1))
     means = []

time: 192 us -> 205 us (1.068)
  local copies, waits for them, and re-layouts: 6.02 us -> 20.1 us
  starting transfers between devices: 45.4 us -> 39.2 us
  other arithmetic: 2.65 us -> 5.98 us
    ppermute x12 -> x9, starting transfers between devices: 27.1 us -> 18.7 us  [passed_along(): return lax.ppermute(block, axis, route)]
    ppermute x12 -> x9, waiting for transfers between devices: 82.9 us -> 86.6 us  [passed_along(): return lax.ppermute(block, axis, route)]
    slice x2, local copies, waits for them, and re-layouts: 0.18 us -> 3.34 us  [on_device(): got_rows = got[:, :group_rows * piece_width].reshape(-1, piece_width)]
    unnamed x7 -> x15, local copies, waits for them, and re-layouts: 1.26 us -> 4.01 us
    ppermute x3, waiting for transfers between devices: 4.15 us -> 1.72 us  [summed_over(): lax.ppermute(block, axis, [(i, (i + shift) % count) for i in range(count)])]
    dot_general x22 -> x15, matrix products: 34.2 us -> 33.5 us  [the longest x1 9.48 us: on_device(): jnp.einsum('jba,jcb->jac', pairs[:, 0], pairs[:, 1], precision=exact)]
  transfers between devices with their start and end apart: 16 -> 13, of which waited for: 12 -> 9; matrix products, arithmetic and copies ran while one was open for 15% -> 24% of each run, Pallas kernels for 0% -> 0%
where the time goes in v4:
time: 205 us; the launch traced here: 204 us
  waiting for transfers between devices  88.3 us (43%)
  matrix products  49.4 us (24%)
  starting transfers between devices  39.2 us (19%)
  local copies, waits for them, and re-layouts  20.1 us (10%)
  other arithmetic  5.98 us (3%)
    ppermute x9, waiting for transfers between devices, passed_along(): return lax.ppermute(block, axis, route)  86.6 us
    ppermute x9, starting transfers between devices, passed_along(): return lax.ppermute(block, axis, route)  18.7 us
    all_to_all x1, starting transfers between devices, on_device(): lax.all_to_all(sent, ('tm', 'ingest'), split_axis=0, concat_axis=0, tiled...  14.8 us
    dot_general x8, matrix products, on_device(): state = jnp.dot(trans[step], state, precision=exact) + forcing[step]  13.7 us
    dot_general x1, matrix products, on_device(): jnp.einsum('jba,jcb->jac', pairs[:, 0], pairs[:, 1], precision=exact)  9.48 us
    dot_general x2, matrix products, on_device(): jnp.einsum('jab,jbc->jac', map_pairs[:, 0], map_pairs[:, 1], precision=ex...  6.72 us
    ppermute x3, starting transfers between devices, summed_over(): lax.ppermute(block, axis, [(i, (i + shift) % count) for i in range(count)])  5.71 us
    dot_general x3, matrix products, on_device(): got = jnp.dot(passed_along(carried, 'tm', distance), acc_t, precision=exact)  4.26 us
  transfers between devices with their start and end apart: 13, of which 9 were waited for; matrix products, arithmetic and copies ran while one was open for 24% of the time, Pallas kernels for 0%

profile of v4, /device:TPU:128, one launch (start us, length us, event | category | flops | bytes accessed | tf_op | source)
XLA Modules:
  0.0 203.7 jit_solution(11671190524789015110)
XLA Ops:
  4.4 14.8 %all-to-all-start = ((bf16[256,2,196]{2,1,0:T(2,128)(2,1)}), bf16[256,2,196]{2,1,0:T(2,128)(2,1)}, u32[]{:S(2)}, u32[]{:S(2)}) async-start(bf16[256,2,196]{2,1,0:T(2,128)(2,1)} %reshape.244), calls=%async_computation | async-start | bytes 524288 | tf_op jit(solution)/shard_map/all_to_all | solution.py:49
  19.2 9.5 %fusion = f32[4,384,384]{2,1,0:T(8,128)S(1)} fusion(f32[4,2,384,384]{3,2,1,0:T(8,128)} %bitcast.128), kind=kOutput, calls=%fused_computation.3 | convolution fusion | flops 2717908992 | bytes 7077888 | tf_op jit(solution)/shard_map/jba,jcb->jac/dot_general | solution.py:60
  28.7 3.4 %convolution_bitcast_fusion = f32[1,2,384,384]{3,2,1,0:T(8,128)} fusion(f32[2,2,384,384]{3,2,1,0:T(8,128)S(1)} %bitcast.130), kind=kOutput, calls=%fused_computation.5 | convolution fusion | flops 1358954496 | bytes 3538944 | tf_op jit(solution)/shard_map/jab,jbc->jac/dot_general | solution.py:72
  32.1 3.3 %broadcast_select_fusion = (f32[384,384]{1,0:T(8,128)S(1)}, f32[384,384]{1,0:T(8,128)}) fusion(pred[]{:T(512)S(6)} %eq.18, f32[1,2,384,384]{3,2,1,0:T(8,128)} %convolution_bitcast_fusion), kind=kOutput, calls=%fused_computation.49 | convolution fusion | flops 679624704 | bytes 2359297 | tf_op jit(solution)/shard_map/jab,jbc->jac/dot_general | solution.py:72
  35.4 2.2 %collective-permute-start = (f32[384,384]{1,0:T(8,128)S(1)}, f32[384,384]{1,0:T(8,128)}, u32[]{:S(2)}, u32[]{:S(2)}) collective-permute-start(f32[384,384]{1,0:T(8,128)S(1)} %get-tuple-element.15), channel_id=1, source_target_pairs={{0,4},{4,8},{8,12},{12,16},{16,20},{20,24},{24,28},{28,32},{32,36}... | collective-permute-start | bytes 1769480 | tf_op jit(solution)/shard_map/ppermute | solution.py:10
  39.7 3.1 %reshape.245 = bf16[256,1,392]{2,1,0:T(2,128)(2,1)} reshape(bf16[256,2,196]{2,1,0:T(2,128)(2,1)} %all-to-all-done) | data formatting | bytes 401408
  42.8 1.9 copy.31
  47.0 1.7 copy.33
  48.7 2.2 %reshape.171 = bf16[2048,48]{1,0:T(8,128)(2,1)} reshape(bf16[256,384]{1,0:T(8,128)(2,1)} %copy.33) | data formatting | bytes 393216 | tf_op jit(solution)/shard_map/reshape | solution.py:50
  52.7 1.7 fusion.3
  56.4 2.7 %collective-permute-start.3 = (f32[8,384]{1,0:T(8,128)S(1)}, f32[8,384]{1,0:T(8,128)S(1)}, u32[]{:S(2)}, u32[]{:S(2)}) collective-permute-start(f32[8,384]{1,0:T(8,128)S(1)} %bitcast.137), channel_id=1, source_target_pairs={{0,2},{1,3},{2,0},{3,1},{4,6},{5,7},{6,4},{7,5},{8,10},{9,11},{10,... | collective-permute-start | bytes 36872 | tf_op jit(solution)/shard_map/ppermute | solution.py:16
  63.6 2.0 gather_fusion
  66.9 3.9 %fusion.1 = f32[4,1,384]{2,1,0:T(1,128)S(1)} fusion(f32[4,2,384,384]{3,2,1,0:T(8,128)} %bitcast.129, f32[4,2,384]{2,1,0:T(2,128)} %add.103), kind=kOutput, calls=%fused_computation.4 | convolution fusion | flops 7077888 | bytes 2371584 | tf_op jit(solution)/shard_map/jab,jb->ja/dot_general | solution.py:62
  76.3 2.3 %fusion.30 = f32[384,384]{1,0:T(8,128)S(1)} fusion(f32[384,384]{1,0:T(8,128)} %collective-permute-done, f32[384,384]{1,0:T(8,128)S(1)} %get-tuple-element.15), kind=kOutput, calls=%fused_computation.91 | convolution fusion | flops 679477248 | bytes 1769472 | tf_op jit(solution)/shard_map/dot_general | solution.py:89
  78.7 3.4 %collective-permute-start.1 = (f32[384,384]{1,0:T(8,128)S(1)}, f32[384,384]{1,0:T(8,128)S(1)}, u32[]{:S(2)}, u32[]{:S(2)}) collective-permute-start(f32[384,384]{1,0:T(8,128)S(1)} %fusion.30), channel_id=1, source_target_pairs={{0,8},{4,12},{8,16},{12,20},{16,24},{20,28},{24,32},{28,36},{32,40... | collective-permute-start | bytes 1769480 | tf_op jit(solution)/shard_map/ppermute | solution.py:10
  82.1 1.9 collective-permute-start.5
  84.1 14.3 %collective-permute-done.5 = f32[384]{0:T(512)S(1)} collective-permute-done((f32[384]{0:T(512)S(1)}, f32[384]{0:T(512)S(1)}, u32[]{:S(2)}, u32[]{:S(2)}) %collective-permute-start.5) | collective-permute-done | bytes 1568 | tf_op jit(solution)/shard_map/ppermute | solution.py:10
  98.8 1.9 collective-permute-start.6
  100.8 6.9 %collective-permute-done.6 = f32[384]{0:T(512)S(1)} collective-permute-done((f32[384]{0:T(512)S(1)}, f32[384]{0:T(512)S(1)}, u32[]{:S(2)}, u32[]{:S(2)}) %collective-permute-start.6) | collective-permute-done | bytes 1568 | tf_op jit(solution)/shard_map/ppermute | solution.py:10
  109.4 2.1 %collective-permute-start.7 = (f32[385,384]{1,0:T(8,128)S(1)}, f32[385,384]{1,0:T(8,128)S(1)}, u32[]{:S(2)}, u32[]{:S(2)}) collective-permute-start(f32[385,384]{1,0:T(8,128)S(1)} %pad_maximum_fusion), channel_id=1, source_target_pairs={{0,16},{4,20},{8,24},{12,28},{16,32},{20,36},{24,40},{28,44},{32,4... | collective-permute-start | bytes 1774088 | tf_op jit(solution)/shard_map/ppermute | solution.py:10
  111.5 13.5 %collective-permute-done.7 = f32[385,384]{1,0:T(8,128)S(1)} collective-permute-done((f32[385,384]{1,0:T(8,128)S(1)}, f32[385,384]{1,0:T(8,128)S(1)}, u32[]{:S(2)}, u32[]{:S(2)}) %collective-permute-start.7) | collective-permute-done | bytes 591392 | tf_op jit(solution)/shard_map/ppermute | solution.py:10
  126.6 1.9 collective-permute-start.8
  128.6 19.2 %collective-permute-done.8 = f32[385,384]{1,0:T(8,128)S(1)} collective-permute-done((f32[385,384]{1,0:T(8,128)S(1)}, f32[385,384]{1,0:T(8,128)S(1)}, u32[]{:S(2)}, u32[]{:S(2)}) %collective-permute-start.8) | collective-permute-done | bytes 591392 | tf_op jit(solution)/shard_map/ppermute | solution.py:10
  149.3 1.9 collective-permute-start.9
  151.3 18.3 %collective-permute-done.9 = f32[385,384]{1,0:T(8,128)S(1)} collective-permute-done((f32[385,384]{1,0:T(8,128)S(1)}, f32[385,384]{1,0:T(8,128)S(1)}, u32[]{:S(2)}, u32[]{:S(2)}) %collective-permute-start.9) | collective-permute-done | bytes 591392 | tf_op jit(solution)/shard_map/ppermute | solution.py:10
  172.3 8.1 %collective-permute-done.10 = f32[384]{0:T(512)S(1)} collective-permute-done((f32[384]{0:T(512)S(1)}, f32[384]{0:T(512)S(1)}, u32[]{:S(2)}, u32[]{:S(2)}) %collective-permute-start.10) | collective-permute-done | bytes 1568 | tf_op jit(solution)/shard_map/ppermute | solution.py:10
  180.9 1.9 collective-permute-start.11
  182.8 6.2 %collective-permute-done.11 = f32[384]{0:T(512)S(1)} collective-permute-done((f32[384]{0:T(512)S(1)}, f32[384]{0:T(512)S(1)}, u32[]{:S(2)}, u32[]{:S(2)}) %collective-permute-start.11) | collective-permute-done | bytes 1568 | tf_op jit(solution)/shard_map/ppermute | solution.py:10
  190.8 1.7 convolution_reduce_fusion.6
  192.6 1.7 convolution_reduce_fusion.5
  194.3 1.7 convolution_reduce_fusion.4
  196.0 1.7 convolution_reduce_fusion.3
  (113 shorter events, 39.8 us)
Async XLA Ops:
  0.0 54.4 %copy-start = (f32[8,384,48]{1,2,0:T(8,128)S(1)}, f32[8,384,48]{1,2,0:T(8,128)}, u32[]{:S(2)}) copy-start(f32[8,384,48]{1,2,0:T(8,128)} %param.8) | copy-start | bytes 1769476
  0.0 1.9 copy-start.4
  0.0 2.0 %copy-start.5 = (s32[1,64]{1,0:T(1,128)S(1)}, s32[1,64]{1,0:T(1,128)}, u32[]{:S(2)}) copy-start(s32[1,64]{1,0:T(1,128)} %param.13) | copy-start | bytes 772
  4.4 35.3 %all-to-all-start = ((bf16[256,2,196]{2,1,0:T(2,128)(2,1)}), bf16[256,2,196]{2,1,0:T(2,128)(2,1)}, u32[]{:S(2)}, u32[]{:S(2)}) async-start(bf16[256,2,196]{2,1,0:T(2,128)(2,1)} %reshape.244), calls=%async_computation | async-start | bytes 524288 | tf_op jit(solution)/shard_map/all_to_all | solution.py:49
  28.7 8.9 %copy-start.2 = (f32[384]{0:T(512)S(1)}, f32[384]{0:T(512)}, u32[]{:S(2)}) copy-start(f32[384]{0:T(512)} %param.9) | copy-start | bytes 4612
  35.4 40.9 %collective-permute-start = (f32[384,384]{1,0:T(8,128)S(1)}, f32[384,384]{1,0:T(8,128)}, u32[]{:S(2)}, u32[]{:S(2)}) collective-permute-start(f32[384,384]{1,0:T(8,128)S(1)} %get-tuple-element.15), channel_id=1, source_target_pairs={{0,4},{4,8},{8,12},{12,16},{16,20},{20,24},{24,28},{28,32},{32,36}... | collective-permute-start | bytes 1769480 | tf_op jit(solution)/shard_map/ppermute | solution.py:10
  54.9 6.4 %collective-permute-start.2 = (f32[8,384]{1,0:T(8,128)S(1)}, f32[8,384]{1,0:T(8,128)S(1)}, u32[]{:S(2)}, u32[]{:S(2)}) collective-permute-start(f32[8,384]{1,0:T(8,128)S(1)} %bitcast.136), channel_id=1, source_target_pairs={{0,1},{1,2},{2,3},{3,0},{4,5},{5,6},{6,7},{7,4},{8,9},{9,10},{10,1... | collective-permute-start | bytes 36872 | tf_op jit(solution)/shard_map/ppermute | solution.py:16
  56.4 5.2 %collective-permute-start.3 = (f32[8,384]{1,0:T(8,128)S(1)}, f32[8,384]{1,0:T(8,128)S(1)}, u32[]{:S(2)}, u32[]{:S(2)}) collective-permute-start(f32[8,384]{1,0:T(8,128)S(1)} %bitcast.137), channel_id=1, source_target_pairs={{0,2},{1,3},{2,0},{3,1},{4,6},{5,7},{6,4},{7,5},{8,10},{9,11},{10,... | collective-permute-start | bytes 36872 | tf_op jit(solution)/shard_map/ppermute | solution.py:16
  59.1 3.8 %collective-permute-start.4 = (f32[8,384]{1,0:T(8,128)S(1)}, f32[8,384]{1,0:T(8,128)S(1)}, u32[]{:S(2)}, u32[]{:S(2)}) collective-permute-start(f32[8,384]{1,0:T(8,128)S(1)} %bitcast.138), channel_id=1, source_target_pairs={{0,3},{1,0},{2,1},{3,2},{4,7},{5,4},{6,5},{7,6},{8,11},{9,8},{10,9... | collective-permute-start | bytes 36872 | tf_op jit(solution)/shard_map/ppermute | solution.py:16
  66.9 3.9 %copy-start.1 = (f32[4,2,384]{2,1,0:T(2,128)S(1)}, f32[4,2,384]{2,1,0:T(2,128)}, u32[]{:S(2)}) copy-start(f32[4,2,384]{2,1,0:T(2,128)} %add.103) | copy-start | bytes 36868
  78.7 29.4 %collective-permute-start.1 = (f32[384,384]{1,0:T(8,128)S(1)}, f32[384,384]{1,0:T(8,128)S(1)}, u32[]{:S(2)}, u32[]{:S(2)}) collective-permute-start(f32[384,384]{1,0:T(8,128)S(1)} %fusion.30), channel_id=1, source_target_pairs={{0,8},{4,12},{8,16},{12,20},{16,24},{20,28},{24,32},{28,36},{32,40... | collective-permute-start | bytes 1769480 | tf_op jit(solution)/shard_map/ppermute | solution.py:10
  82.1 16.3 %collective-permute-start.5 = (f32[384]{0:T(512)S(1)}, f32[384]{0:T(512)S(1)}, u32[]{:S(2)}, u32[]{:S(2)}) collective-permute-start(f32[384]{0:T(512)S(1)} %add_select_fusion), channel_id=1, source_target_pairs={{0,4},{4,8},{8,12},{12,16},{16,20},{20,24},{24,28},{28,32},{32,36}... | collective-permute-start | bytes 4616 | tf_op jit(solution)/shard_map/ppermute | solution.py:10
  98.8 8.8 %collective-permute-start.6 = (f32[384]{0:T(512)S(1)}, f32[384]{0:T(512)S(1)}, u32[]{:S(2)}, u32[]{:S(2)}) collective-permute-start(f32[384]{0:T(512)S(1)} %add.108), channel_id=1, source_target_pairs={{0,8},{4,12},{8,16},{12,20},{16,24},{20,28},{24,32},{28,36},{32,40... | collective-permute-start | bytes 4616 | tf_op jit(solution)/shard_map/ppermute | solution.py:10
  109.4 15.7 %collective-permute-start.7 = (f32[385,384]{1,0:T(8,128)S(1)}, f32[385,384]{1,0:T(8,128)S(1)}, u32[]{:S(2)}, u32[]{:S(2)}) collective-permute-start(f32[385,384]{1,0:T(8,128)S(1)} %pad_maximum_fusion), channel_id=1, source_target_pairs={{0,16},{4,20},{8,24},{12,28},{16,32},{20,36},{24,40},{28,44},{32,4... | collective-permute-start | bytes 1774088 | tf_op jit(solution)/shard_map/ppermute | solution.py:10
  126.6 21.1 %collective-permute-start.8 = (f32[385,384]{1,0:T(8,128)S(1)}, f32[385,384]{1,0:T(8,128)S(1)}, u32[]{:S(2)}, u32[]{:S(2)}) collective-permute-start(f32[385,384]{1,0:T(8,128)S(1)} %pad_maximum_fusion.1), channel_id=1, source_target_pairs={{0,32},{4,36},{8,40},{12,44},{16,48},{20,52},{24,56},{28,60},{32,6... | collective-permute-start | bytes 1774088 | tf_op jit(solution)/shard_map/ppermute | solution.py:10
  149.2 39.9 %copy-start.3 = (f32[384]{0:T(512)S(1)}, f32[384]{0:T(512)}, u32[]{:S(2)}) copy-start(f32[384]{0:T(512)} %param.9) | copy-start | bytes 4612
  149.3 20.3 %collective-permute-start.9 = (f32[385,384]{1,0:T(8,128)S(1)}, f32[385,384]{1,0:T(8,128)S(1)}, u32[]{:S(2)}, u32[]{:S(2)}) collective-permute-start(f32[385,384]{1,0:T(8,128)S(1)} %pad_maximum_fusion.2), channel_id=1, source_target_pairs={{0,64},{4,68},{8,72},{12,76},{16,80},{20,84},{24,88},{28,92},{32,9... | collective-permute-start | bytes 1774088 | tf_op jit(solution)/shard_map/ppermute | solution.py:10
  171.0 9.4 %collective-permute-start.10 = (f32[384]{0:T(512)S(1)}, f32[384]{0:T(512)S(1)}, u32[]{:S(2)}, u32[]{:S(2)}) collective-permute-start(f32[384]{0:T(512)S(1)} %add.112), channel_id=1, source_target_pairs={{0,128},{4,132},{8,136},{12,140},{16,144},{20,148},{24,152},{28,15... | collective-permute-start | bytes 4616 | tf_op jit(solution)/shard_map/ppermute | solution.py:10
  180.9 8.2 %collective-permute-start.11 = (f32[384]{0:T(512)S(1)}, f32[384]{0:T(512)S(1)}, u32[]{:S(2)}, u32[]{:S(2)}) collective-permute-start(f32[384]{0:T(512)S(1)} %add.113), channel_id=1, source_target_pairs={{0,4},{4,8},{8,12},{12,16},{16,20},{20,24},{24,28},{28,32},{32,36}... | collective-permute-start | bytes 4616 | tf_op jit(solution)/shard_map/ppermute | solution.py:10

commit v5 on v3

--- a/solution.py
+++ b/solution.py
@@ -46,6 +46,12 @@
         marked.astype(jnp.bfloat16)[:, None, :], (tm_count, in_count, group_rows)
     ).reshape(tm_count * in_count, group_rows)
     sent = jnp.concatenate([pieces, marks], axis=1)
+    level = trans
+    while level.shape[0] > 1:
+        pairs = level.reshape(level.shape[0] // 2, 2, state_width, state_width)
+        level = jnp.einsum("jab,jbc->jac", pairs[:, 1], pairs[:, 0], precision=exact)
+    slab_map = level[0]
+    sent, slab_map = lax.optimization_barrier((sent, slab_map))
     got = lax.all_to_all(sent, ("tm", "ingest"), split_axis=0, concat_axis=0, tiled=True)
     got_rows = got[:, : group_rows * piece_width].reshape(-1, piece_width)
     got_marks = got[:, group_rows * piece_width :].reshape(-1).astype(jnp.int32)
@@ -55,11 +61,6 @@
     partial_force = jnp.einsum("lsq,lq->ls", gain, drive_piece, precision=exact)
     forcing = summed_over(partial_force, "ingest")
 
-    level = trans
-    while level.shape[0] > 1:
-        pairs = level.reshape(level.shape[0] // 2, 2, state_width, state_width)
-        level = jnp.einsum("jab,jbc->jac", pairs[:, 1], pairs[:, 0], precision=exact)
-    slab_map = level[0]
     offset = forcing[0]
     for step in range(1, steps_here):
         offset = jnp.dot(trans[step], offset, precision=exact) + forcing[step]
@@ -69,18 +70,14 @@
     acc_vec = jnp.where(is_first, jnp.dot(slab_map, prior_mean, precision=exact) + offset, offset)
     acc_map = jnp.where(is_first, jnp.zeros_like(slab_map), slab_map)
     distance = 1
-    history = [acc_vec]
     while distance < tm_count:
+        got_vec = passed_along(acc_vec, "tm", distance)
         last = distance * 2 >= tm_count
-        if len(history) >= 3 and not last:
-            acc_map, _ = lax.optimization_barrier((acc_map, history[-3]))
-        got_vec = passed_along(acc_vec, "tm", distance)
         if not last:
             got_map = passed_along(acc_map, "tm", distance)
         acc_vec = jnp.dot(acc_map, got_vec, precision=exact) + acc_vec
         if not last:
             acc_map = jnp.dot(acc_map, got_map, precision=exact)
-        history.append(acc_vec)
         distance *= 2
     state = jnp.where(is_first, prior_mean, passed_along(acc_vec, "tm", 1))
     means = []

time: 192 us -> 179 us (0.932)
  matrix products: 49 us -> 39.6 us
    dot_general x8, matrix products: 13.7 us -> 5.19 us  [on_device(): state = jnp.dot(trans[step], state, precision=exact) + forcing[step]]
    all_to_all x1, waiting for transfers between devices: 0.01 us -> 7.97 us  [on_device(): lax.all_to_all(sent, ('tm', 'ingest'), split_axis=0, concat_axis=0, tiled...]
    ppermute x12, waiting for transfers between devices: 82.9 us -> 76.7 us  [passed_along(): return lax.ppermute(block, axis, route)]
    ppermute x12, starting transfers between devices: 27.1 us -> 24.3 us  [passed_along(): return lax.ppermute(block, axis, route)]
  transfers between devices with their start and end apart: 16 -> 16, of which waited for: 12 -> 13; matrix products, arithmetic and copies ran while one was open for 15% -> 11% of each run, Pallas kernels for 0% -> 0%
where the time goes in v5:
time: 179 us; the launch traced here: 177 us
  waiting for transfers between devices  87 us (49%)
  starting transfers between devices  43.5 us (24%)
  matrix products  39.6 us (22%)
  local copies, waits for them, and re-layouts  5.3 us (3%)
    ppermute x12, waiting for transfers between devices, passed_along(): return lax.ppermute(block, axis, route)  76.7 us
    ppermute x12, starting transfers between devices, passed_along(): return lax.ppermute(block, axis, route)  24.3 us
    all_to_all x1, starting transfers between devices, on_device(): lax.all_to_all(sent, ('tm', 'ingest'), split_axis=0, concat_axis=0, tiled...  13.8 us
    dot_general x7, matrix products, on_device(): offset = jnp.dot(trans[step], offset, precision=exact) + forcing[step]  12 us
    dot_general x3, matrix products, on_device(): jnp.einsum('jab,jbc->jac', pairs[:, 1], pairs[:, 0], precision=exact)  10.3 us
    all_to_all x1, waiting for transfers between devices, on_device(): lax.all_to_all(sent, ('tm', 'ingest'), split_axis=0, concat_axis=0, tiled...  7.97 us
    dot_general x5, matrix products, on_device(): acc_map = jnp.dot(acc_map, got_map, precision=exact)  6.34 us
    ppermute x3, starting transfers between devices, summed_over(): lax.ppermute(block, axis, [(i, (i + shift) % count) for i in range(count)])  5.36 us
  transfers between devices with their start and end apart: 16, of which 13 were waited for; matrix products, arithmetic and copies ran while one was open for 11% of the time, Pallas kernels for 0%

profile of v5, /device:TPU:128, one launch (start us, length us, event | category | flops | bytes accessed | tf_op | source)
XLA Modules:
  0.0 177.4 jit_solution(17650825074758682989)
XLA Ops:
  0.0 6.6 %fusion = f32[4,384,384]{2,1,0:T(8,128)S(1)} fusion(f32[4,2,384,384]{3,2,1,0:T(8,128)} %bitcast.132), kind=kOutput, calls=%fused_computation.2 | convolution fusion | flops 2717908992 | bytes 7077888 | tf_op jit(solution)/shard_map/jab,jbc->jac/dot_general | solution.py:52
  6.6 2.4 %convolution_bitcast_fusion = f32[1,2,384,384]{3,2,1,0:T(8,128)S(1)} fusion(f32[2,2,384,384]{3,2,1,0:T(8,128)S(1)} %bitcast.135), kind=kOutput, calls=%fused_computation.4 | convolution fusion | flops 1358954496 | bytes 3538944 | tf_op jit(solution)/shard_map/jab,jbc->jac/dot_general | solution.py:52
  13.8 13.8 %all-to-all-start = ((bf16[256,2,196]{2,1,0:T(2,128)(2,1)}), bf16[256,2,196]{2,1,0:T(2,128)(2,1)S(1)}, u32[]{:S(2)}, u32[]{:S(2)}) async-start(bf16[256,2,196]{2,1,0:T(2,128)(2,1)} %reshape.234), calls=%async_computation | async-start | bytes 524288 | tf_op jit(solution)/shard_map/all_to_all | solution.py:55
  27.7 2.0 %collective-permute-start = (f32[384,384]{1,0:T(8,128)S(1)}, f32[384,384]{1,0:T(8,128)S(1)}, u32[]{:S(2)}, u32[]{:S(2)}) collective-permute-start(f32[384,384]{1,0:T(8,128)S(1)} %broadcast_select_fusion), channel_id=1, source_target_pairs={{0,4},{4,8},{8,12},{12,16},{16,20},{20,24},{24,28},{28,32},{32,36}... | collective-permute-start | bytes 1769480 | tf_op jit(solution)/shard_map/ppermute | solution.py:10
  30.4 8.0 %all-to-all-done = bf16[256,2,196]{2,1,0:T(2,128)(2,1)S(1)} async-done(((bf16[256,2,196]{2,1,0:T(2,128)(2,1)}), bf16[256,2,196]{2,1,0:T(2,128)(2,1)S(1)}, u32[]{:S(2)}, u32[]{:S(2)}) %all-to-all-start) | async-done | bytes 200736 | tf_op jit(solution)/shard_map/all_to_all | solution.py:55
  40.7 1.8 %collective-permute-done = f32[384,384]{1,0:T(8,128)S(1)} collective-permute-done((f32[384,384]{1,0:T(8,128)S(1)}, f32[384,384]{1,0:T(8,128)S(1)}, u32[]{:S(2)}, u32[]{:S(2)}) %collective-permute-start) | collective-permute-done | bytes 589856 | tf_op jit(solution)/shard_map/ppermute | solution.py:10
  43.8 2.1 %collective-permute-start.1 = (f32[384,384]{1,0:T(8,128)S(1)}, f32[384,384]{1,0:T(8,128)S(1)}, u32[]{:S(2)}, u32[]{:S(2)}) collective-permute-start(f32[384,384]{1,0:T(8,128)S(1)} %fusion.38), channel_id=1, source_target_pairs={{0,8},{4,12},{8,16},{12,20},{16,24},{20,28},{24,32},{28,36},{32,40... | collective-permute-start | bytes 1769480 | tf_op jit(solution)/shard_map/ppermute | solution.py:10
  47.7 2.6 %collective-permute-start.6 = (f32[8,384]{1,0:T(8,128)S(1)}, f32[8,384]{1,0:T(8,128)S(1)}, u32[]{:S(2)}, u32[]{:S(2)}) collective-permute-start(f32[8,384]{1,0:T(8,128)S(1)} %bitcast.142), channel_id=1, source_target_pairs={{0,2},{1,3},{2,0},{3,1},{4,6},{5,7},{6,4},{7,5},{8,10},{9,11},{10,... | collective-permute-start | bytes 36872 | tf_op jit(solution)/shard_map/ppermute | solution.py:16
  54.6 7.7 %collective-permute-done.1 = f32[384,384]{1,0:T(8,128)S(1)} collective-permute-done((f32[384,384]{1,0:T(8,128)S(1)}, f32[384,384]{1,0:T(8,128)S(1)}, u32[]{:S(2)}, u32[]{:S(2)}) %collective-permute-start.1) | collective-permute-done | bytes 589856 | tf_op jit(solution)/shard_map/ppermute | solution.py:10
  63.6 1.9 %collective-permute-start.2 = (f32[384,384]{1,0:T(8,128)S(1)}, f32[384,384]{1,0:T(8,128)S(1)}, u32[]{:S(2)}, u32[]{:S(2)}) collective-permute-start(f32[384,384]{1,0:T(8,128)S(1)} %fusion.39), channel_id=1, source_target_pairs={{0,16},{4,20},{8,24},{12,28},{16,32},{20,36},{24,40},{28,44},{32,4... | collective-permute-start | bytes 1769480 | tf_op jit(solution)/shard_map/ppermute | solution.py:10
  65.6 1.7 convolution_reduce_fusion.20
  67.3 1.7 convolution_reduce_fusion.19
  69.1 1.7 convolution_reduce_fusion.18
  70.8 1.7 convolution_reduce_fusion.17
  72.5 9.0 %collective-permute-done.2 = f32[384,384]{1,0:T(8,128)S(1)} collective-permute-done((f32[384,384]{1,0:T(8,128)S(1)}, f32[384,384]{1,0:T(8,128)S(1)}, u32[]{:S(2)}, u32[]{:S(2)}) %collective-permute-start.2) | collective-permute-done | bytes 589856 | tf_op jit(solution)/shard_map/ppermute | solution.py:10
  82.8 1.9 %collective-permute-start.3 = (f32[384,384]{1,0:T(8,128)S(1)}, f32[384,384]{1,0:T(8,128)S(1)}, u32[]{:S(2)}, u32[]{:S(2)}) collective-permute-start(f32[384,384]{1,0:T(8,128)S(1)} %fusion.40), channel_id=1, source_target_pairs={{0,32},{4,36},{8,40},{12,44},{16,48},{20,52},{24,56},{28,60},{32,6... | collective-permute-start | bytes 1769480 | tf_op jit(solution)/shard_map/ppermute | solution.py:10
  84.8 1.7 convolution_reduce_fusion.16
  88.3 1.8 convolution_reduce_fusion.14
  90.0 1.9 %collective-permute-start.8 = (f32[384]{0:T(512)S(1)}, f32[384]{0:T(512)S(1)}, u32[]{:S(2)}, u32[]{:S(2)}) collective-permute-start(f32[384]{0:T(512)S(1)} %add_select_fusion), channel_id=1, source_target_pairs={{0,4},{4,8},{8,12},{12,16},{16,20},{20,24},{24,28},{28,32},{32,36}... | collective-permute-start | bytes 4616 | tf_op jit(solution)/shard_map/ppermute | solution.py:10
  92.0 6.3 %collective-permute-done.8 = f32[384]{0:T(512)S(1)} collective-permute-done((f32[384]{0:T(512)S(1)}, f32[384]{0:T(512)S(1)}, u32[]{:S(2)}, u32[]{:S(2)}) %collective-permute-start.8) | collective-permute-done | bytes 1568 | tf_op jit(solution)/shard_map/ppermute | solution.py:10
  99.6 2.8 %collective-permute-start.4 = (f32[384,384]{1,0:T(8,128)S(1)}, f32[384,384]{1,0:T(8,128)S(1)}, u32[]{:S(2)}, u32[]{:S(2)}) collective-permute-start(f32[384,384]{1,0:T(8,128)S(1)} %fusion.41), channel_id=1, source_target_pairs={{0,64},{4,68},{8,72},{12,76},{16,80},{20,84},{24,88},{28,92},{32,9... | collective-permute-start | bytes 1769480 | tf_op jit(solution)/shard_map/ppermute | solution.py:10
  103.1 1.9 %collective-permute-start.9 = (f32[384]{0:T(512)S(1)}, f32[384]{0:T(512)S(1)}, u32[]{:S(2)}, u32[]{:S(2)}) collective-permute-start(f32[384]{0:T(512)S(1)} %add.114), channel_id=1, source_target_pairs={{0,8},{4,12},{8,16},{12,20},{16,24},{20,28},{24,32},{28,36},{32,40... | collective-permute-start | bytes 4616 | tf_op jit(solution)/shard_map/ppermute | solution.py:10
  105.0 20.5 %collective-permute-done.9 = f32[384]{0:T(512)S(1)} collective-permute-done((f32[384]{0:T(512)S(1)}, f32[384]{0:T(512)S(1)}, u32[]{:S(2)}, u32[]{:S(2)}) %collective-permute-start.9) | collective-permute-done | bytes 1568 | tf_op jit(solution)/shard_map/ppermute | solution.py:10
  126.2 1.9 %collective-permute-start.10 = (f32[384]{0:T(512)S(1)}, f32[384]{0:T(512)S(1)}, u32[]{:S(2)}, u32[]{:S(2)}) collective-permute-start(f32[384]{0:T(512)S(1)} %add.115), channel_id=1, source_target_pairs={{0,16},{4,20},{8,24},{12,28},{16,32},{20,36},{24,40},{28,44},{32,4... | collective-permute-start | bytes 4616 | tf_op jit(solution)/shard_map/ppermute | solution.py:10
  128.2 7.2 %collective-permute-done.10 = f32[384]{0:T(512)S(1)} collective-permute-done((f32[384]{0:T(512)S(1)}, f32[384]{0:T(512)S(1)}, u32[]{:S(2)}, u32[]{:S(2)}) %collective-permute-start.10) | collective-permute-done | bytes 1568 | tf_op jit(solution)/shard_map/ppermute | solution.py:10
  136.0 1.9 %collective-permute-start.11 = (f32[384]{0:T(512)S(1)}, f32[384]{0:T(512)S(1)}, u32[]{:S(2)}, u32[]{:S(2)}) collective-permute-start(f32[384]{0:T(512)S(1)} %add.116), channel_id=1, source_target_pairs={{0,32},{4,36},{8,40},{12,44},{16,48},{20,52},{24,56},{28,60},{32,6... | collective-permute-start | bytes 4616 | tf_op jit(solution)/shard_map/ppermute | solution.py:10
  137.9 4.8 %collective-permute-done.11 = f32[384]{0:T(512)S(1)} collective-permute-done((f32[384]{0:T(512)S(1)}, f32[384]{0:T(512)S(1)}, u32[]{:S(2)}, u32[]{:S(2)}) %collective-permute-start.11) | collective-permute-done | bytes 1568 | tf_op jit(solution)/shard_map/ppermute | solution.py:10
  143.4 2.6 %collective-permute-start.12 = (f32[384]{0:T(512)S(1)}, f32[384]{0:T(512)S(1)}, u32[]{:S(2)}, u32[]{:S(2)}) collective-permute-start(f32[384]{0:T(512)S(1)} %add.117), channel_id=1, source_target_pairs={{0,64},{4,68},{8,72},{12,76},{16,80},{20,84},{24,88},{28,92},{32,9... | collective-permute-start | bytes 4616 | tf_op jit(solution)/shard_map/ppermute | solution.py:10
  146.0 5.0 %collective-permute-done.12 = f32[384]{0:T(512)S(1)} collective-permute-done((f32[384]{0:T(512)S(1)}, f32[384]{0:T(512)S(1)}, u32[]{:S(2)}, u32[]{:S(2)}) %collective-permute-start.12) | collective-permute-done | bytes 1568 | tf_op jit(solution)/shard_map/ppermute | solution.py:10
  152.9 8.1 %collective-permute-done.13 = f32[384]{0:T(512)S(1)} collective-permute-done((f32[384]{0:T(512)S(1)}, f32[384]{0:T(512)S(1)}, u32[]{:S(2)}, u32[]{:S(2)}) %collective-permute-start.13) | collective-permute-done | bytes 1568 | tf_op jit(solution)/shard_map/ppermute | solution.py:10
  163.0 1.9 %collective-permute-start.14 = (f32[384]{0:T(512)S(1)}, f32[384]{0:T(512)S(1)}, u32[]{:S(2)}, u32[]{:S(2)}) collective-permute-start(f32[384]{0:T(512)S(1)} %add.119), channel_id=1, source_target_pairs={{0,4},{4,8},{8,12},{12,16},{16,20},{20,24},{24,28},{28,32},{32,36}... | collective-permute-start | bytes 4616 | tf_op jit(solution)/shard_map/ppermute | solution.py:10
  164.9 6.3 %collective-permute-done.14 = f32[384]{0:T(512)S(1)} collective-permute-done((f32[384]{0:T(512)S(1)}, f32[384]{0:T(512)S(1)}, u32[]{:S(2)}, u32[]{:S(2)}) %collective-permute-start.14) | collective-permute-done | bytes 1568 | tf_op jit(solution)/shard_map/ppermute | solution.py:10
  (129 shorter events, 33.0 us)
Async XLA Ops:
  0.0 45.9 %copy-start = (f32[8,384,48]{1,2,0:T(8,128)S(1)}, f32[8,384,48]{1,2,0:T(8,128)}, u32[]{:S(2)}) copy-start(f32[8,384,48]{1,2,0:T(8,128)} %param.8) | copy-start | bytes 1769476
  0.0 10.4 %copy-start.1 = (bf16[512,192]{0,1:T(8,128)(2,1)S(1)}, bf16[512,192]{0,1:T(8,128)(2,1)}, u32[]{:S(2)}) copy-start(bf16[512,192]{0,1:T(8,128)(2,1)} %param.10) | copy-start | bytes 589828
  0.0 10.4 %copy-start.3 = (f32[512]{0:T(512)S(1)}, f32[512]{0:T(512)}, u32[]{:S(2)}) copy-start(f32[512]{0:T(512)} %param.11) | copy-start | bytes 6148
  6.6 4.7 %copy-start.4 = (s32[512]{0:T(512)S(1)}, s32[512]{0:T(512)}, u32[]{:S(2)}) copy-start(s32[512]{0:T(512)} %param.12) | copy-start | bytes 6148
  6.6 4.8 %copy-start.5 = (s32[1,64]{1,0:T(1,128)S(1)}, s32[1,64]{1,0:T(1,128)}, u32[]{:S(2)}) copy-start(s32[1,64]{1,0:T(1,128)} %param.13) | copy-start | bytes 772
  9.1 20.6 %copy-start.2 = (f32[384]{0:T(512)S(1)}, f32[384]{0:T(512)}, u32[]{:S(2)}) copy-start(f32[384]{0:T(512)} %param.9) | copy-start | bytes 4612
  13.8 24.6 %all-to-all-start = ((bf16[256,2,196]{2,1,0:T(2,128)(2,1)}), bf16[256,2,196]{2,1,0:T(2,128)(2,1)S(1)}, u32[]{:S(2)}, u32[]{:S(2)}) async-start(bf16[256,2,196]{2,1,0:T(2,128)(2,1)} %reshape.234), calls=%async_computation | async-start | bytes 524288 | tf_op jit(solution)/shard_map/all_to_all | solution.py:55
  27.7 14.9 %collective-permute-start = (f32[384,384]{1,0:T(8,128)S(1)}, f32[384,384]{1,0:T(8,128)S(1)}, u32[]{:S(2)}, u32[]{:S(2)}) collective-permute-start(f32[384,384]{1,0:T(8,128)S(1)} %broadcast_select_fusion), channel_id=1, source_target_pairs={{0,4},{4,8},{8,12},{12,16},{16,20},{20,24},{24,28},{28,32},{32,36}... | collective-permute-start | bytes 1769480 | tf_op jit(solution)/shard_map/ppermute | solution.py:10
  43.8 18.5 %collective-permute-start.1 = (f32[384,384]{1,0:T(8,128)S(1)}, f32[384,384]{1,0:T(8,128)S(1)}, u32[]{:S(2)}, u32[]{:S(2)}) collective-permute-start(f32[384,384]{1,0:T(8,128)S(1)} %fusion.38), channel_id=1, source_target_pairs={{0,8},{4,12},{8,16},{12,20},{16,24},{20,28},{24,32},{28,36},{32,40... | collective-permute-start | bytes 1769480 | tf_op jit(solution)/shard_map/ppermute | solution.py:10
  46.4 5.4 %collective-permute-start.5 = (f32[8,384]{1,0:T(8,128)S(1)}, f32[8,384]{1,0:T(8,128)S(1)}, u32[]{:S(2)}, u32[]{:S(2)}) collective-permute-start(f32[8,384]{1,0:T(8,128)S(1)} %bitcast.141), channel_id=1, source_target_pairs={{0,1},{1,2},{2,3},{3,0},{4,5},{5,6},{6,7},{7,4},{8,9},{9,10},{10,1... | collective-permute-start | bytes 36872 | tf_op jit(solution)/shard_map/ppermute | solution.py:16
  47.7 5.2 %collective-permute-start.6 = (f32[8,384]{1,0:T(8,128)S(1)}, f32[8,384]{1,0:T(8,128)S(1)}, u32[]{:S(2)}, u32[]{:S(2)}) collective-permute-start(f32[8,384]{1,0:T(8,128)S(1)} %bitcast.142), channel_id=1, source_target_pairs={{0,2},{1,3},{2,0},{3,1},{4,6},{5,7},{6,4},{7,5},{8,10},{9,11},{10,... | collective-permute-start | bytes 36872 | tf_op jit(solution)/shard_map/ppermute | solution.py:16
  50.3 3.7 %collective-permute-start.7 = (f32[8,384]{1,0:T(8,128)S(1)}, f32[8,384]{1,0:T(8,128)S(1)}, u32[]{:S(2)}, u32[]{:S(2)}) collective-permute-start(f32[8,384]{1,0:T(8,128)S(1)} %bitcast.143), channel_id=1, source_target_pairs={{0,3},{1,0},{2,1},{3,2},{4,7},{5,4},{6,5},{7,6},{8,11},{9,8},{10,9... | collective-permute-start | bytes 36872 | tf_op jit(solution)/shard_map/ppermute | solution.py:16
  62.3 108.9 %slice-start = ((s8[4718592]{0:T(1024)(128)(4,1)}), s8[4194304]{0:T(1024)(128)(4,1)S(1)}, s32[]{:S(2)}) async-start(s8[4718592]{0:T(1024)(128)(4,1)} %bitcast.133), calls=%async_computation.1 | async-start | bytes 8388608
  63.6 18.0 %collective-permute-start.2 = (f32[384,384]{1,0:T(8,128)S(1)}, f32[384,384]{1,0:T(8,128)S(1)}, u32[]{:S(2)}, u32[]{:S(2)}) collective-permute-start(f32[384,384]{1,0:T(8,128)S(1)} %fusion.39), channel_id=1, source_target_pairs={{0,16},{4,20},{8,24},{12,28},{16,32},{20,36},{24,40},{28,44},{32,4... | collective-permute-start | bytes 1769480 | tf_op jit(solution)/shard_map/ppermute | solution.py:10
  82.8 15.4 %collective-permute-start.3 = (f32[384,384]{1,0:T(8,128)S(1)}, f32[384,384]{1,0:T(8,128)S(1)}, u32[]{:S(2)}, u32[]{:S(2)}) collective-permute-start(f32[384,384]{1,0:T(8,128)S(1)} %fusion.40), channel_id=1, source_target_pairs={{0,32},{4,36},{8,40},{12,44},{16,48},{20,52},{24,56},{28,60},{32,6... | collective-permute-start | bytes 1769480 | tf_op jit(solution)/shard_map/ppermute | solution.py:10
  88.2 83.0 %slice-start.1 = ((s8[4718592]{0:T(1024)(128)(4,1)}), s8[524288]{0:T(1024)(128)(4,1)S(1)}, s32[]{:S(2)}) async-start(s8[4718592]{0:T(1024)(128)(4,1)} %bitcast.133), calls=%async_computation.2 | async-start | bytes 1048576
  90.0 8.2 %collective-permute-start.8 = (f32[384]{0:T(512)S(1)}, f32[384]{0:T(512)S(1)}, u32[]{:S(2)}, u32[]{:S(2)}) collective-permute-start(f32[384]{0:T(512)S(1)} %add_select_fusion), channel_id=1, source_target_pairs={{0,4},{4,8},{8,12},{12,16},{16,20},{20,24},{24,28},{28,32},{32,36}... | collective-permute-start | bytes 4616 | tf_op jit(solution)/shard_map/ppermute | solution.py:10
  99.6 61.5 %collective-permute-start.4 = (f32[384,384]{1,0:T(8,128)S(1)}, f32[384,384]{1,0:T(8,128)S(1)}, u32[]{:S(2)}, u32[]{:S(2)}) collective-permute-start(f32[384,384]{1,0:T(8,128)S(1)} %fusion.41), channel_id=1, source_target_pairs={{0,64},{4,68},{8,72},{12,76},{16,80},{20,84},{24,88},{28,92},{32,9... | collective-permute-start | bytes 1769480 | tf_op jit(solution)/shard_map/ppermute | solution.py:10
  103.1 22.5 %collective-permute-start.9 = (f32[384]{0:T(512)S(1)}, f32[384]{0:T(512)S(1)}, u32[]{:S(2)}, u32[]{:S(2)}) collective-permute-start(f32[384]{0:T(512)S(1)} %add.114), channel_id=1, source_target_pairs={{0,8},{4,12},{8,16},{12,20},{16,24},{20,28},{24,32},{28,36},{32,40... | collective-permute-start | bytes 4616 | tf_op jit(solution)/shard_map/ppermute | solution.py:10
  126.2 9.1 %collective-permute-start.10 = (f32[384]{0:T(512)S(1)}, f32[384]{0:T(512)S(1)}, u32[]{:S(2)}, u32[]{:S(2)}) collective-permute-start(f32[384]{0:T(512)S(1)} %add.115), channel_id=1, source_target_pairs={{0,16},{4,20},{8,24},{12,28},{16,32},{20,36},{24,40},{28,44},{32,4... | collective-permute-start | bytes 4616 | tf_op jit(solution)/shard_map/ppermute | solution.py:10
  136.0 6.7 %collective-permute-start.11 = (f32[384]{0:T(512)S(1)}, f32[384]{0:T(512)S(1)}, u32[]{:S(2)}, u32[]{:S(2)}) collective-permute-start(f32[384]{0:T(512)S(1)} %add.116), channel_id=1, source_target_pairs={{0,32},{4,36},{8,40},{12,44},{16,48},{20,52},{24,56},{28,60},{32,6... | collective-permute-start | bytes 4616 | tf_op jit(solution)/shard_map/ppermute | solution.py:10
  143.4 7.6 %collective-permute-start.12 = (f32[384]{0:T(512)S(1)}, f32[384]{0:T(512)S(1)}, u32[]{:S(2)}, u32[]{:S(2)}) collective-permute-start(f32[384]{0:T(512)S(1)} %add.117), channel_id=1, source_target_pairs={{0,64},{4,68},{8,72},{12,76},{16,80},{20,84},{24,88},{28,92},{32,9... | collective-permute-start | bytes 4616 | tf_op jit(solution)/shard_map/ppermute | solution.py:10
  151.6 9.4 %collective-permute-start.13 = (f32[384]{0:T(512)S(1)}, f32[384]{0:T(512)S(1)}, u32[]{:S(2)}, u32[]{:S(2)}) collective-permute-start(f32[384]{0:T(512)S(1)} %add.118), channel_id=1, source_target_pairs={{0,128},{4,132},{8,136},{12,140},{16,144},{20,148},{24,152},{28,15... | collective-permute-start | bytes 4616 | tf_op jit(solution)/shard_map/ppermute | solution.py:10
  163.0 8.2 %collective-permute-start.14 = (f32[384]{0:T(512)S(1)}, f32[384]{0:T(512)S(1)}, u32[]{:S(2)}, u32[]{:S(2)}) collective-permute-start(f32[384]{0:T(512)S(1)} %add.119), channel_id=1, source_target_pairs={{0,4},{4,8},{8,12},{12,16},{16,20},{20,24},{24,28},{28,32},{32,36}... | collective-permute-start | bytes 4616 | tf_op jit(solution)/shard_map/ppermute | solution.py:10

commit v6 on v4

--- a/solution.py
+++ b/solution.py
@@ -56,22 +56,14 @@
     forcing = summed_over(partial_force, "ingest")
 
     pairs = trans.reshape(steps_here // 2, 2, state_width, state_width)
-    force_pairs = forcing.reshape(steps_here // 2, 2, state_width)
     level_t = jnp.einsum("jba,jcb->jac", pairs[:, 0], pairs[:, 1], precision=exact)
-    level_off = (
-        jnp.einsum("jab,jb->ja", pairs[:, 1], force_pairs[:, 0], precision=exact)
-        + force_pairs[:, 1]
-    )
     while level_t.shape[0] > 1:
         map_pairs = level_t.reshape(-1, 2, state_width, state_width)
-        off_pairs = level_off.reshape(-1, 2, state_width)
-        level_off = (
-            jnp.einsum("ja,jab->jb", off_pairs[:, 0], map_pairs[:, 1], precision=exact)
-            + off_pairs[:, 1]
-        )
         level_t = jnp.einsum("jab,jbc->jac", map_pairs[:, 0], map_pairs[:, 1], precision=exact)
     slab_t = level_t[0]
-    offset = level_off[0]
+    offset = forcing[0]
+    for step in range(1, steps_here):
+        offset = jnp.dot(trans[step], offset, precision=exact) + forcing[step]
 
     tm_index = lax.axis_index("tm")
     is_first = tm_index == 0
@@ -82,11 +74,6 @@
         if distance * 2 >= tm_count:
             got_vec = passed_along(acc_vec, "tm", distance)
             acc_vec = jnp.dot(got_vec, acc_t, precision=exact) + acc_vec
-        elif distance < 4:
-            got_vec = passed_along(acc_vec, "tm", distance)
-            got_t = passed_along(acc_t, "tm", distance)
-            acc_vec = jnp.dot(got_vec, acc_t, precision=exact) + acc_vec
-            acc_t = jnp.dot(got_t, acc_t, precision=exact)
         else:
             carried = jnp.concatenate([acc_t, acc_vec[None]], axis=0)
             got = jnp.dot(passed_along(carried, "tm", distance), acc_t, precision=exact)

time: 205 us -> 189 us (0.922)
  the two profiles are of different devices: /device:TPU:128 before, /device:TPU:24 now
where the time goes in v6:
time: 189 us; the launch traced here: 188 us
  starting transfers between devices  67.7 us (36%)
  waiting for transfers between devices  62.4 us (33%)
  matrix products  48.1 us (25%)
  local copies, waits for them, and re-layouts  6.29 us (3%)
  other arithmetic  2.86 us (2%)
    ppermute x7, waiting for transfers between devices, passed_along(): return lax.ppermute(block, axis, route)  58.4 us
    ppermute x7, starting transfers between devices, passed_along(): return lax.ppermute(block, axis, route)  48.7 us
    all_to_all x1, starting transfers between devices, on_device(): lax.all_to_all(sent, ('tm', 'ingest'), split_axis=0, concat_axis=0, tiled...  14.4 us
    dot_general x8, matrix products, on_device(): state = jnp.dot(trans[step], state, precision=exact) + forcing[step]  13.7 us
    dot_general x7, matrix products, on_device(): offset = jnp.dot(trans[step], offset, precision=exact) + forcing[step]  12 us
    dot_general x1, matrix products, on_device(): jnp.einsum('jba,jcb->jac', pairs[:, 0], pairs[:, 1], precision=exact)  9.65 us
    dot_general x5, matrix products, on_device(): got = jnp.dot(passed_along(carried, 'tm', distance), acc_t, precision=exact)  7.1 us
    ppermute x3, starting transfers between devices, summed_over(): lax.ppermute(block, axis, [(i, (i + shift) % count) for i in range(count)])  4.5 us
  transfers between devices with their start and end apart: 11, of which 9 were waited for; matrix products, arithmetic and copies ran while one was open for 7% of the time, Pallas kernels for 0%

profile of v6, /device:TPU:24, one launch (start us, length us, event | category | flops | bytes accessed | tf_op | source)
XLA Modules:
  0.0 188.1 jit_solution(16566393147143497573)
XLA Ops:
  5.7 14.4 %all-to-all-start = ((bf16[256,2,196]{2,1,0:T(2,128)(2,1)}), bf16[256,2,196]{2,1,0:T(2,128)(2,1)S(1)}, u32[]{:S(2)}, u32[]{:S(2)}) async-start(bf16[256,2,196]{2,1,0:T(2,128)(2,1)} %reshape.224), calls=%async_computation | async-start | bytes 524288 | tf_op jit(solution)/shard_map/all_to_all | solution.py:49
  20.1 9.7 %fusion = f32[4,384,384]{2,1,0:T(8,128)S(1)} fusion(f32[4,2,384,384]{3,2,1,0:T(8,128)} %bitcast.121), kind=kOutput, calls=%fused_computation.2 | convolution fusion | flops 2717908992 | bytes 7077888 | tf_op jit(solution)/shard_map/jba,jcb->jac/dot_general | solution.py:59
  29.8 2.4 %convolution_bitcast_fusion = f32[1,2,384,384]{3,2,1,0:T(8,128)S(1)} fusion(f32[2,2,384,384]{3,2,1,0:T(8,128)S(1)} %bitcast.122), kind=kOutput, calls=%fused_computation.4 | convolution fusion | flops 1358954496 | bytes 3538944 | tf_op jit(solution)/shard_map/jab,jbc->jac/dot_general | solution.py:62
  36.8 2.8 %collective-permute-start.2 = (f32[8,384]{1,0:T(8,128)S(1)}, f32[8,384]{1,0:T(8,128)S(1)}, u32[]{:S(2)}, u32[]{:S(2)}) collective-permute-start(f32[8,384]{1,0:T(8,128)S(1)} %bitcast.127), channel_id=1, source_target_pairs={{0,3},{1,0},{2,1},{3,2},{4,7},{5,4},{6,5},{7,6},{8,11},{9,8},{10,9... | collective-permute-start | bytes 36872 | tf_op jit(solution)/shard_map/ppermute | solution.py:16
  41.3 3.5 %collective-permute-done.1 = f32[8,384]{1,0:T(8,128)S(1)} collective-permute-done((f32[8,384]{1,0:T(8,128)S(1)}, f32[8,384]{1,0:T(8,128)S(1)}, u32[]{:S(2)}, u32[]{:S(2)}) %collective-permute-start.1) | collective-permute-done | bytes 12320 | tf_op jit(solution)/shard_map/ppermute | solution.py:16
  45.9 1.7 convolution_reduce_fusion.15
  47.7 1.7 convolution_reduce_fusion.14
  49.4 1.7 convolution_reduce_fusion.13
  51.2 1.7 convolution_reduce_fusion.12
  52.9 1.7 convolution_reduce_fusion.11
  54.7 1.7 convolution_reduce_fusion.10
  56.4 1.7 convolution_reduce_fusion.9
  58.2 1.9 %collective-permute-start.3 = (f32[385,384]{1,0:T(8,128)S(1)}, f32[385,384]{1,0:T(8,128)S(1)}, u32[]{:S(2)}, u32[]{:S(2)}) collective-permute-start(f32[385,384]{1,0:T(8,128)S(1)} %pad_maximum_fusion), channel_id=1, source_target_pairs={{0,4},{4,8},{8,12},{12,16},{16,20},{20,24},{24,28},{28,32},{32,36}... | collective-permute-start | bytes 1774088 | tf_op jit(solution)/shard_map/ppermute | solution.py:10
  60.1 9.4 %collective-permute-done.3 = f32[385,384]{1,0:T(8,128)S(1)} collective-permute-done((f32[385,384]{1,0:T(8,128)S(1)}, f32[385,384]{1,0:T(8,128)S(1)}, u32[]{:S(2)}, u32[]{:S(2)}) %collective-permute-start.3) | collective-permute-done | bytes 591392 | tf_op jit(solution)/shard_map/ppermute | solution.py:10
  71.1 5.5 %collective-permute-start.4 = (f32[385,384]{1,0:T(8,128)S(1)}, f32[385,384]{1,0:T(8,128)S(1)}, u32[]{:S(2)}, u32[]{:S(2)}) collective-permute-start(f32[385,384]{1,0:T(8,128)S(1)} %pad_maximum_fusion.1), channel_id=1, source_target_pairs={{0,8},{4,12},{8,16},{12,20},{16,24},{20,28},{24,32},{28,36},{32,40... | collective-permute-start | bytes 1774088 | tf_op jit(solution)/shard_map/ppermute | solution.py:10
  76.6 11.0 %collective-permute-done.4 = f32[385,384]{1,0:T(8,128)S(1)} collective-permute-done((f32[385,384]{1,0:T(8,128)S(1)}, f32[385,384]{1,0:T(8,128)S(1)}, u32[]{:S(2)}, u32[]{:S(2)}) %collective-permute-start.4) | collective-permute-done | bytes 591392 | tf_op jit(solution)/shard_map/ppermute | solution.py:10
  89.2 4.4 %collective-permute-start.5 = (f32[385,384]{1,0:T(8,128)S(1)}, f32[385,384]{1,0:T(8,128)S(1)}, u32[]{:S(2)}, u32[]{:S(2)}) collective-permute-start(f32[385,384]{1,0:T(8,128)S(1)} %pad_maximum_fusion.2), channel_id=1, source_target_pairs={{0,16},{4,20},{8,24},{12,28},{16,32},{20,36},{24,40},{28,44},{32,4... | collective-permute-start | bytes 1774088 | tf_op jit(solution)/shard_map/ppermute | solution.py:10
  93.6 12.8 %collective-permute-done.5 = f32[385,384]{1,0:T(8,128)S(1)} collective-permute-done((f32[385,384]{1,0:T(8,128)S(1)}, f32[385,384]{1,0:T(8,128)S(1)}, u32[]{:S(2)}, u32[]{:S(2)}) %collective-permute-start.5) | collective-permute-done | bytes 591392 | tf_op jit(solution)/shard_map/ppermute | solution.py:10
  107.9 3.7 %collective-permute-start.6 = (f32[385,384]{1,0:T(8,128)S(1)}, f32[385,384]{1,0:T(8,128)S(1)}, u32[]{:S(2)}, u32[]{:S(2)}) collective-permute-start(f32[385,384]{1,0:T(8,128)S(1)} %pad_maximum_fusion.3), channel_id=1, source_target_pairs={{0,32},{4,36},{8,40},{12,44},{16,48},{20,52},{24,56},{28,60},{32,6... | collective-permute-start | bytes 1774088 | tf_op jit(solution)/shard_map/ppermute | solution.py:10
  111.6 10.4 %collective-permute-done.6 = f32[385,384]{1,0:T(8,128)S(1)} collective-permute-done((f32[385,384]{1,0:T(8,128)S(1)}, f32[385,384]{1,0:T(8,128)S(1)}, u32[]{:S(2)}, u32[]{:S(2)}) %collective-permute-start.6) | collective-permute-done | bytes 591392 | tf_op jit(solution)/shard_map/ppermute | solution.py:10
  123.6 8.5 %collective-permute-start.7 = (f32[385,384]{1,0:T(8,128)S(1)}, f32[385,384]{1,0:T(8,128)S(1)}, u32[]{:S(2)}, u32[]{:S(2)}) collective-permute-start(f32[385,384]{1,0:T(8,128)S(1)} %pad_maximum_fusion.4), channel_id=1, source_target_pairs={{0,64},{4,68},{8,72},{12,76},{16,80},{20,84},{24,88},{28,92},{32,9... | collective-permute-start | bytes 1774088 | tf_op jit(solution)/shard_map/ppermute | solution.py:10
  132.1 10.8 %collective-permute-done.7 = f32[385,384]{1,0:T(8,128)S(1)} collective-permute-done((f32[385,384]{1,0:T(8,128)S(1)}, f32[385,384]{1,0:T(8,128)S(1)}, u32[]{:S(2)}, u32[]{:S(2)}) %collective-permute-start.7) | collective-permute-done | bytes 591392 | tf_op jit(solution)/shard_map/ppermute | solution.py:10
  144.4 22.5 %collective-permute-start.8 = (f32[384]{0:T(512)S(1)}, f32[384]{0:T(512)S(1)}, u32[]{:S(2)}, u32[]{:S(2)}) collective-permute-start(f32[384]{0:T(512)S(1)} %add.118), channel_id=1, source_target_pairs={{0,128},{4,132},{8,136},{12,140},{16,144},{20,148},{24,152},{28,15... | collective-permute-start | bytes 4616 | tf_op jit(solution)/shard_map/ppermute | solution.py:10
  168.6 2.2 %collective-permute-start.9 = (f32[384]{0:T(512)S(1)}, f32[384]{0:T(512)S(1)}, u32[]{:S(2)}, u32[]{:S(2)}) collective-permute-start(f32[384]{0:T(512)S(1)} %add.119), channel_id=1, source_target_pairs={{0,4},{4,8},{8,12},{12,16},{16,20},{20,24},{24,28},{28,32},{32,36}... | collective-permute-start | bytes 4616 | tf_op jit(solution)/shard_map/ppermute | solution.py:10
  170.8 2.7 %collective-permute-done.9 = f32[384]{0:T(512)S(1)} collective-permute-done((f32[384]{0:T(512)S(1)}, f32[384]{0:T(512)S(1)}, u32[]{:S(2)}, u32[]{:S(2)}) %collective-permute-start.9) | collective-permute-done | bytes 1568 | tf_op jit(solution)/shard_map/ppermute | solution.py:10
  175.3 1.7 convolution_reduce_fusion.6
  177.0 1.7 convolution_reduce_fusion.5
  178.8 1.7 convolution_reduce_fusion.4
  180.5 1.7 convolution_reduce_fusion.3
  182.2 1.7 convolution_reduce_fusion.2
  184.0 1.7 convolution_reduce_fusion.1
  185.7 1.7 convolution_reduce_fusion
  (114 shorter events, 24.8 us)
Async XLA Ops:
  0.0 36.3 %copy-start = (f32[8,384,48]{1,2,0:T(8,128)S(1)}, f32[8,384,48]{1,2,0:T(8,128)}, u32[]{:S(2)}) copy-start(f32[8,384,48]{1,2,0:T(8,128)} %param.8) | copy-start | bytes 1769476
  5.7 28.3 %all-to-all-start = ((bf16[256,2,196]{2,1,0:T(2,128)(2,1)}), bf16[256,2,196]{2,1,0:T(2,128)(2,1)S(1)}, u32[]{:S(2)}, u32[]{:S(2)}) async-start(bf16[256,2,196]{2,1,0:T(2,128)(2,1)} %reshape.224), calls=%async_computation | async-start | bytes 524288 | tf_op jit(solution)/shard_map/all_to_all | solution.py:49
  20.1 12.1 %copy-start.1 = (f32[384]{0:T(512)S(1)}, f32[384]{0:T(512)}, u32[]{:S(2)}) copy-start(f32[384]{0:T(512)} %param.9) | copy-start | bytes 4612
  36.8 4.5 %collective-permute-start.2 = (f32[8,384]{1,0:T(8,128)S(1)}, f32[8,384]{1,0:T(8,128)S(1)}, u32[]{:S(2)}, u32[]{:S(2)}) collective-permute-start(f32[8,384]{1,0:T(8,128)S(1)} %bitcast.127), channel_id=1, source_target_pairs={{0,3},{1,0},{2,1},{3,2},{4,7},{5,4},{6,5},{7,6},{8,11},{9,8},{10,9... | collective-permute-start | bytes 36872 | tf_op jit(solution)/shard_map/ppermute | solution.py:16
  39.6 5.2 %collective-permute-start.1 = (f32[8,384]{1,0:T(8,128)S(1)}, f32[8,384]{1,0:T(8,128)S(1)}, u32[]{:S(2)}, u32[]{:S(2)}) collective-permute-start(f32[8,384]{1,0:T(8,128)S(1)} %bitcast.128), channel_id=1, source_target_pairs={{0,2},{1,3},{2,0},{3,1},{4,6},{5,7},{6,4},{7,5},{8,10},{9,11},{10,... | collective-permute-start | bytes 36872 | tf_op jit(solution)/shard_map/ppermute | solution.py:16
  40.4 4.9 %collective-permute-start = (f32[8,384]{1,0:T(8,128)S(1)}, f32[8,384]{1,0:T(8,128)S(1)}, u32[]{:S(2)}, u32[]{:S(2)}) collective-permute-start(f32[8,384]{1,0:T(8,128)S(1)} %bitcast.129), channel_id=1, source_target_pairs={{0,1},{1,2},{2,3},{3,0},{4,5},{5,6},{6,7},{7,4},{8,9},{9,10},{10,1... | collective-permute-start | bytes 36872 | tf_op jit(solution)/shard_map/ppermute | solution.py:16
  58.2 11.3 %collective-permute-start.3 = (f32[385,384]{1,0:T(8,128)S(1)}, f32[385,384]{1,0:T(8,128)S(1)}, u32[]{:S(2)}, u32[]{:S(2)}) collective-permute-start(f32[385,384]{1,0:T(8,128)S(1)} %pad_maximum_fusion), channel_id=1, source_target_pairs={{0,4},{4,8},{8,12},{12,16},{16,20},{20,24},{24,28},{28,32},{32,36}... | collective-permute-start | bytes 1774088 | tf_op jit(solution)/shard_map/ppermute | solution.py:10
  71.1 16.5 %collective-permute-start.4 = (f32[385,384]{1,0:T(8,128)S(1)}, f32[385,384]{1,0:T(8,128)S(1)}, u32[]{:S(2)}, u32[]{:S(2)}) collective-permute-start(f32[385,384]{1,0:T(8,128)S(1)} %pad_maximum_fusion.1), channel_id=1, source_target_pairs={{0,8},{4,12},{8,16},{12,20},{16,24},{20,28},{24,32},{28,36},{32,40... | collective-permute-start | bytes 1774088 | tf_op jit(solution)/shard_map/ppermute | solution.py:10
  89.2 17.2 %collective-permute-start.5 = (f32[385,384]{1,0:T(8,128)S(1)}, f32[385,384]{1,0:T(8,128)S(1)}, u32[]{:S(2)}, u32[]{:S(2)}) collective-permute-start(f32[385,384]{1,0:T(8,128)S(1)} %pad_maximum_fusion.2), channel_id=1, source_target_pairs={{0,16},{4,20},{8,24},{12,28},{16,32},{20,36},{24,40},{28,44},{32,4... | collective-permute-start | bytes 1774088 | tf_op jit(solution)/shard_map/ppermute | solution.py:10
  107.9 14.1 %collective-permute-start.6 = (f32[385,384]{1,0:T(8,128)S(1)}, f32[385,384]{1,0:T(8,128)S(1)}, u32[]{:S(2)}, u32[]{:S(2)}) collective-permute-start(f32[385,384]{1,0:T(8,128)S(1)} %pad_maximum_fusion.3), channel_id=1, source_target_pairs={{0,32},{4,36},{8,40},{12,44},{16,48},{20,52},{24,56},{28,60},{32,6... | collective-permute-start | bytes 1774088 | tf_op jit(solution)/shard_map/ppermute | solution.py:10
  123.6 19.3 %collective-permute-start.7 = (f32[385,384]{1,0:T(8,128)S(1)}, f32[385,384]{1,0:T(8,128)S(1)}, u32[]{:S(2)}, u32[]{:S(2)}) collective-permute-start(f32[385,384]{1,0:T(8,128)S(1)} %pad_maximum_fusion.4), channel_id=1, source_target_pairs={{0,64},{4,68},{8,72},{12,76},{16,80},{20,84},{24,88},{28,92},{32,9... | collective-permute-start | bytes 1774088 | tf_op jit(solution)/shard_map/ppermute | solution.py:10
  144.4 23.8 %collective-permute-start.8 = (f32[384]{0:T(512)S(1)}, f32[384]{0:T(512)S(1)}, u32[]{:S(2)}, u32[]{:S(2)}) collective-permute-start(f32[384]{0:T(512)S(1)} %add.118), channel_id=1, source_target_pairs={{0,128},{4,132},{8,136},{12,140},{16,144},{20,148},{24,152},{28,15... | collective-permute-start | bytes 4616 | tf_op jit(solution)/shard_map/ppermute | solution.py:10
  168.6 4.9 %collective-permute-start.9 = (f32[384]{0:T(512)S(1)}, f32[384]{0:T(512)S(1)}, u32[]{:S(2)}, u32[]{:S(2)}) collective-permute-start(f32[384]{0:T(512)S(1)} %add.119), channel_id=1, source_target_pairs={{0,4},{4,8},{8,12},{12,16},{16,20},{20,24},{24,28},{28,32},{32,36}... | collective-permute-start | bytes 4616 | tf_op jit(solution)/shard_map/ppermute | solution.py:10

commit v7 on v6

--- a/solution.py
+++ b/solution.py
@@ -1,6 +1,8 @@
 import jax
 import jax.numpy as jnp
 from jax import lax
+from jax.experimental import pallas as pl
+from jax.experimental.pallas import tpu as pltpu
 from jax.sharding import PartitionSpec as P
 
 
@@ -21,6 +23,41 @@
     for source in range(1, count):
         total = total + by_source[source]
     return total
+
+
+def recurrence_kernel(map_ref, force_ref, start_ref, out_ref, state_ref):
+    step = pl.program_id(0)
+
+    @pl.when(step == 0)
+    def _():
+        state_ref[...] = jnp.broadcast_to(start_ref[...], state_ref.shape)
+
+    moved = lax.dot_general(
+        state_ref[...],
+        map_ref[0],
+        (((1,), (1,)), ((), ())),
+        precision=lax.Precision.HIGHEST,
+        preferred_element_type=jnp.float32,
+    )
+    state = moved + force_ref[pl.ds(step, 1), :]
+    state_ref[...] = state
+    out_ref[pl.ds(step, 1), :] = state[0:1, :]
+
+
+def run_recurrence(trans, forcing, start):
+    steps, width = forcing.shape
+    return pl.pallas_call(
+        recurrence_kernel,
+        grid=(steps,),
+        in_specs=[
+            pl.BlockSpec((1, width, width), lambda t: (t, 0, 0)),
+            pl.BlockSpec((steps, width), lambda t: (0, 0)),
+            pl.BlockSpec((1, width), lambda t: (0, 0)),
+        ],
+        out_specs=pl.BlockSpec((steps, width), lambda t: (0, 0)),
+        out_shape=jax.ShapeDtypeStruct((steps, width), jnp.float32),
+        scratch_shapes=[pltpu.VMEM((8, width), jnp.float32)],
+    )(trans, forcing, start.reshape(1, width))
 
 
 def on_device(
@@ -61,9 +98,7 @@
         map_pairs = level_t.reshape(-1, 2, state_width, state_width)
         level_t = jnp.einsum("jab,jbc->jac", map_pairs[:, 0], map_pairs[:, 1], precision=exact)
     slab_t = level_t[0]
-    offset = forcing[0]
-    for step in range(1, steps_here):
-        offset = jnp.dot(trans[step], offset, precision=exact) + forcing[step]
+    offset = run_recurrence(trans, forcing, jnp.zeros((state_width,), jnp.float32))[-1]
 
     tm_index = lax.axis_index("tm")
     is_first = tm_index == 0
@@ -81,11 +116,7 @@
             acc_vec = got[state_width] + acc_vec
         distance *= 2
     state = jnp.where(is_first, prior_mean, passed_along(acc_vec, "tm", 1))
-    means = []
-    for step in range(steps_here):
-        state = jnp.dot(trans[step], state, precision=exact) + forcing[step]
-        means.append(state)
-    return jnp.stack(means)
+    return run_recurrence(trans, forcing, state)
 
 
 def solution(mesh):

time: 189 us -> 180 us (0.952)
  matrix products: 48.1 us -> 22.4 us
  Pallas kernels: 0 us -> 16.3 us
    dot_general x15 -> x0, matrix products: 25.6 us -> none  [the longest x8 13.7 us: on_device(): state = jnp.dot(trans[step], state, precision=exact) + forcing[step]]
    pallas_call x0 -> x2, Pallas kernels: none -> 16.3 us  [run_recurrence(): pl.pallas_call(recurrence_kernel, grid=(steps,), in_specs=[pl.BlockSpec((...]
  transfers between devices with their start and end apart: 11 -> 11, of which waited for: 9 -> 10; matrix products, arithmetic and copies ran while one was open for 7% -> 8% of each run, Pallas kernels for 0% -> 0%
where the time goes in v7:
time: 180 us; the launch traced here: 179 us
  starting transfers between devices  68 us (38%)
  waiting for transfers between devices  62.7 us (35%)
  matrix products  22.4 us (12%)
  Pallas kernels  16.3 us (9%)
  local copies, waits for them, and re-layouts  6.72 us (4%)
  other arithmetic  2.79 us (2%)
    ppermute x7, waiting for transfers between devices, passed_along(): return lax.ppermute(block, axis, route)  58.7 us
    ppermute x7, starting transfers between devices, passed_along(): return lax.ppermute(block, axis, route)  48.4 us
    pallas_call x2, Pallas kernels, run_recurrence(): pl.pallas_call(recurrence_kernel, grid=(steps,), in_specs=[pl.BlockSpec((...  16.3 us
    all_to_all x1, starting transfers between devices, on_device(): lax.all_to_all(sent, ('tm', 'ingest'), split_axis=0, concat_axis=0, tiled...  14.4 us
    dot_general x1, matrix products, on_device(): jnp.einsum('jba,jcb->jac', pairs[:, 0], pairs[:, 1], precision=exact)  9.65 us
    dot_general x5, matrix products, on_device(): got = jnp.dot(passed_along(carried, 'tm', distance), acc_t, precision=exact)  7.1 us
    ppermute x3, starting transfers between devices, summed_over(): lax.ppermute(block, axis, [(i, (i + shift) % count) for i in range(count)])  5.12 us
    ppermute x3, waiting for transfers between devices, summed_over(): lax.ppermute(block, axis, [(i, (i + shift) % count) for i in range(count)])  4.03 us
  transfers between devices with their start and end apart: 11, of which 10 were waited for; matrix products, arithmetic and copies ran while one was open for 8% of the time, Pallas kernels for 0%

profile of v7, /device:TPU:24, one launch (start us, length us, event | category | flops | bytes accessed | tf_op | source)
XLA Modules:
  0.0 179.4 jit_solution(2504708055094289039)
XLA Ops:
  0.0 1.0 multiply_convert_fusion
  3.5 0.9 reshape.163
  4.4 14.4 %all-to-all-start = ((bf16[256,2,196]{2,1,0:T(2,128)(2,1)}), bf16[256,2,196]{2,1,0:T(2,128)(2,1)S(1)}, u32[]{:S(2)}, u32[]{:S(2)}) async-start(bf16[256,2,196]{2,1,0:T(2,128)(2,1)} %reshape.163), calls=%async_computation | async-start | bytes 524288 | tf_op jit(solution)/shard_map/all_to_all | solution.py:86
  18.8 9.7 %fusion = f32[4,384,384]{2,1,0:T(8,128)S(1)} fusion(f32[4,2,384,384]{3,2,1,0:T(8,128)} %bitcast.68), kind=kOutput, calls=%fused_computation.2 | convolution fusion | flops 2717908992 | bytes 7077888 | tf_op jit(solution)/shard_map/jba,jcb->jac/dot_general | solution.py:96
  28.5 2.4 %convolution_bitcast_fusion = f32[1,2,384,384]{3,2,1,0:T(8,128)S(1)} fusion(f32[2,2,384,384]{3,2,1,0:T(8,128)S(1)} %bitcast.69), kind=kOutput, calls=%fused_computation.4 | convolution fusion | flops 1358954496 | bytes 3538944 | tf_op jit(solution)/shard_map/jab,jbc->jac/dot_general | solution.py:99
  30.9 1.3 broadcast_select_fusion
  35.5 3.1 %collective-permute-start.1 = (f32[8,384]{1,0:T(8,128)S(1)}, f32[8,384]{1,0:T(8,128)S(1)}, u32[]{:S(2)}, u32[]{:S(2)}) collective-permute-start(f32[8,384]{1,0:T(8,128)S(1)} %bitcast.74), channel_id=1, source_target_pairs={{0,2},{1,3},{2,0},{3,1},{4,6},{5,7},{6,4},{7,5},{8,10},{9,11},{10,... | collective-permute-start | bytes 36872 | tf_op jit(solution)/shard_map/ppermute | solution.py:18
  38.6 1.2 collective-permute-start.2
  39.7 0.9 collective-permute-start
  40.8 1.5 collective-permute-done.2
  42.3 2.4 %collective-permute-done = f32[8,384]{1,0:T(8,128)S(1)} collective-permute-done((f32[8,384]{1,0:T(8,128)S(1)}, f32[8,384]{1,0:T(8,128)S(1)}, u32[]{:S(2)}, u32[]{:S(2)}) %collective-permute-start) | collective-permute-done | bytes 12320 | tf_op jit(solution)/shard_map/ppermute | solution.py:18
  46.4 8.2 %shard_map.73 = f32[8,384]{1,0:T(8,128)} custom-call(f32[8,384,384]{2,1,0:T(8,128)} %map_ref.3, f32[8,384]{1,0:T(8,128)} %fusion.5.force_ref, f32[1,384]{1,0:T(1,128)} %reshape.138.start_ref), custom_call_target="tpu_custom_call" | custom-call | tf_op jit(solution)/shard_map/pallas_call | solution.py:49
  55.3 1.9 %collective-permute-start.3 = (f32[385,384]{1,0:T(8,128)S(1)}, f32[385,384]{1,0:T(8,128)S(1)}, u32[]{:S(2)}, u32[]{:S(2)}) collective-permute-start(f32[385,384]{1,0:T(8,128)S(1)} %pad_maximum_fusion), channel_id=1, source_target_pairs={{0,4},{4,8},{8,12},{12,16},{16,20},{20,24},{24,28},{28,32},{32,36}... | collective-permute-start | bytes 1774088 | tf_op jit(solution)/shard_map/ppermute | solution.py:12
  57.3 9.4 %collective-permute-done.3 = f32[385,384]{1,0:T(8,128)S(1)} collective-permute-done((f32[385,384]{1,0:T(8,128)S(1)}, f32[385,384]{1,0:T(8,128)S(1)}, u32[]{:S(2)}, u32[]{:S(2)}) %collective-permute-start.3) | collective-permute-done | bytes 591392 | tf_op jit(solution)/shard_map/ppermute | solution.py:12
  66.7 1.4 fusion.17
  68.2 5.5 %collective-permute-start.4 = (f32[385,384]{1,0:T(8,128)S(1)}, f32[385,384]{1,0:T(8,128)S(1)}, u32[]{:S(2)}, u32[]{:S(2)}) collective-permute-start(f32[385,384]{1,0:T(8,128)S(1)} %pad_maximum_fusion.1), channel_id=1, source_target_pairs={{0,8},{4,12},{8,16},{12,20},{16,24},{20,28},{24,32},{28,36},{32,40... | collective-permute-start | bytes 1774088 | tf_op jit(solution)/shard_map/ppermute | solution.py:12
  73.8 11.0 %collective-permute-done.4 = f32[385,384]{1,0:T(8,128)S(1)} collective-permute-done((f32[385,384]{1,0:T(8,128)S(1)}, f32[385,384]{1,0:T(8,128)S(1)}, u32[]{:S(2)}, u32[]{:S(2)}) %collective-permute-start.4) | collective-permute-done | bytes 591392 | tf_op jit(solution)/shard_map/ppermute | solution.py:12
  84.8 1.4 fusion.14
  86.4 4.4 %collective-permute-start.5 = (f32[385,384]{1,0:T(8,128)S(1)}, f32[385,384]{1,0:T(8,128)S(1)}, u32[]{:S(2)}, u32[]{:S(2)}) collective-permute-start(f32[385,384]{1,0:T(8,128)S(1)} %pad_maximum_fusion.2), channel_id=1, source_target_pairs={{0,16},{4,20},{8,24},{12,28},{16,32},{20,36},{24,40},{28,44},{32,4... | collective-permute-start | bytes 1774088 | tf_op jit(solution)/shard_map/ppermute | solution.py:12
  90.8 12.8 %collective-permute-done.5 = f32[385,384]{1,0:T(8,128)S(1)} collective-permute-done((f32[385,384]{1,0:T(8,128)S(1)}, f32[385,384]{1,0:T(8,128)S(1)}, u32[]{:S(2)}, u32[]{:S(2)}) %collective-permute-start.5) | collective-permute-done | bytes 591392 | tf_op jit(solution)/shard_map/ppermute | solution.py:12
  103.6 1.4 fusion.12
  105.1 3.7 %collective-permute-start.6 = (f32[385,384]{1,0:T(8,128)S(1)}, f32[385,384]{1,0:T(8,128)S(1)}, u32[]{:S(2)}, u32[]{:S(2)}) collective-permute-start(f32[385,384]{1,0:T(8,128)S(1)} %pad_maximum_fusion.3), channel_id=1, source_target_pairs={{0,32},{4,36},{8,40},{12,44},{16,48},{20,52},{24,56},{28,60},{32,6... | collective-permute-start | bytes 1774088 | tf_op jit(solution)/shard_map/ppermute | solution.py:12
  108.8 10.4 %collective-permute-done.6 = f32[385,384]{1,0:T(8,128)S(1)} collective-permute-done((f32[385,384]{1,0:T(8,128)S(1)}, f32[385,384]{1,0:T(8,128)S(1)}, u32[]{:S(2)}, u32[]{:S(2)}) %collective-permute-start.6) | collective-permute-done | bytes 591392 | tf_op jit(solution)/shard_map/ppermute | solution.py:12
  119.2 1.4 fusion.10
  120.8 8.5 %collective-permute-start.7 = (f32[385,384]{1,0:T(8,128)S(1)}, f32[385,384]{1,0:T(8,128)S(1)}, u32[]{:S(2)}, u32[]{:S(2)}) collective-permute-start(f32[385,384]{1,0:T(8,128)S(1)} %pad_maximum_fusion.4), channel_id=1, source_target_pairs={{0,64},{4,68},{8,72},{12,76},{16,80},{20,84},{24,88},{28,92},{32,9... | collective-permute-start | bytes 1774088 | tf_op jit(solution)/shard_map/ppermute | solution.py:12
  129.3 10.8 %collective-permute-done.7 = f32[385,384]{1,0:T(8,128)S(1)} collective-permute-done((f32[385,384]{1,0:T(8,128)S(1)}, f32[385,384]{1,0:T(8,128)S(1)}, u32[]{:S(2)}, u32[]{:S(2)}) %collective-permute-start.7) | collective-permute-done | bytes 591392 | tf_op jit(solution)/shard_map/ppermute | solution.py:12
  140.1 1.4 fusion.8
  141.5 22.5 %collective-permute-start.8 = (f32[384]{0:T(512)S(1)}, f32[384]{0:T(512)S(1)}, u32[]{:S(2)}, u32[]{:S(2)}) collective-permute-start(f32[384]{0:T(512)S(1)} %add.68), channel_id=1, source_target_pairs={{0,128},{4,132},{8,136},{12,140},{16,144},{20,148},{24,152},{28,15... | collective-permute-start | bytes 4616 | tf_op jit(solution)/shard_map/ppermute | solution.py:12
  164.0 1.3 collective-permute-done.8
  165.8 1.9 %collective-permute-start.9 = (f32[384]{0:T(512)S(1)}, f32[384]{0:T(512)S(1)}, u32[]{:S(2)}, u32[]{:S(2)}) collective-permute-start(f32[384]{0:T(512)S(1)} %add.69), channel_id=1, source_target_pairs={{0,4},{4,8},{8,12},{12,16},{16,20},{20,24},{24,28},{28,32},{32,36}... | collective-permute-start | bytes 4616 | tf_op jit(solution)/shard_map/ppermute | solution.py:12
  167.7 3.0 %collective-permute-done.9 = f32[384]{0:T(512)S(1)} collective-permute-done((f32[384]{0:T(512)S(1)}, f32[384]{0:T(512)S(1)}, u32[]{:S(2)}, u32[]{:S(2)}) %collective-permute-start.9) | collective-permute-done | bytes 1568 | tf_op jit(solution)/shard_map/ppermute | solution.py:12
  171.3 8.2 %shard_map.74 = f32[8,384]{1,0:T(8,128)} custom-call(f32[8,384,384]{2,1,0:T(8,128)} %map_ref.3, f32[8,384]{1,0:T(8,128)} %fusion.5.force_ref, f32[1,384]{1,0:T(1,128)} %reshape.139.start_ref), custom_call_target="tpu_custom_call" | custom-call | tf_op jit(solution)/shard_map/pallas_call | solution.py:49
  (70 shorter events, 9.8 us)
Async XLA Ops:
  0.0 35.0 %copy-start = (f32[8,384,48]{1,2,0:T(8,128)S(1)}, f32[8,384,48]{1,2,0:T(8,128)}, u32[]{:S(2)}) copy-start(f32[8,384,48]{1,2,0:T(8,128)} %param.8) | copy-start | bytes 1769476
  0.0 1.9 %copy-start.2 = (s32[512]{0:T(512)S(1)}, s32[512]{0:T(512)}, u32[]{:S(2)}) copy-start(s32[512]{0:T(512)} %param.12) | copy-start | bytes 6148
  0.0 2.0 %copy-start.3 = (s32[1,64]{1,0:T(1,128)S(1)}, s32[1,64]{1,0:T(1,128)}, u32[]{:S(2)}) copy-start(s32[1,64]{1,0:T(1,128)} %param.13) | copy-start | bytes 772
  4.4 28.3 %all-to-all-start = ((bf16[256,2,196]{2,1,0:T(2,128)(2,1)}), bf16[256,2,196]{2,1,0:T(2,128)(2,1)S(1)}, u32[]{:S(2)}, u32[]{:S(2)}) async-start(bf16[256,2,196]{2,1,0:T(2,128)(2,1)} %reshape.163), calls=%async_computation | async-start | bytes 524288 | tf_op jit(solution)/shard_map/all_to_all | solution.py:86
  28.5 2.4 %copy-start.1 = (f32[384]{0:T(512)S(1)}, f32[384]{0:T(512)}, u32[]{:S(2)}) copy-start(f32[384]{0:T(512)} %param.9) | copy-start | bytes 4612
  35.5 5.3 %collective-permute-start.1 = (f32[8,384]{1,0:T(8,128)S(1)}, f32[8,384]{1,0:T(8,128)S(1)}, u32[]{:S(2)}, u32[]{:S(2)}) collective-permute-start(f32[8,384]{1,0:T(8,128)S(1)} %bitcast.74), channel_id=1, source_target_pairs={{0,2},{1,3},{2,0},{3,1},{4,6},{5,7},{6,4},{7,5},{8,10},{9,11},{10,... | collective-permute-start | bytes 36872 | tf_op jit(solution)/shard_map/ppermute | solution.py:18
  38.6 3.7 %collective-permute-start.2 = (f32[8,384]{1,0:T(8,128)S(1)}, f32[8,384]{1,0:T(8,128)S(1)}, u32[]{:S(2)}, u32[]{:S(2)}) collective-permute-start(f32[8,384]{1,0:T(8,128)S(1)} %bitcast.75), channel_id=1, source_target_pairs={{0,3},{1,0},{2,1},{3,2},{4,7},{5,4},{6,5},{7,6},{8,11},{9,8},{10,9... | collective-permute-start | bytes 36872 | tf_op jit(solution)/shard_map/ppermute | solution.py:18
  39.7 4.9 %collective-permute-start = (f32[8,384]{1,0:T(8,128)S(1)}, f32[8,384]{1,0:T(8,128)S(1)}, u32[]{:S(2)}, u32[]{:S(2)}) collective-permute-start(f32[8,384]{1,0:T(8,128)S(1)} %bitcast.76), channel_id=1, source_target_pairs={{0,1},{1,2},{2,3},{3,0},{4,5},{5,6},{6,7},{7,4},{8,9},{9,10},{10,1... | collective-permute-start | bytes 36872 | tf_op jit(solution)/shard_map/ppermute | solution.py:18
  55.3 11.3 %collective-permute-start.3 = (f32[385,384]{1,0:T(8,128)S(1)}, f32[385,384]{1,0:T(8,128)S(1)}, u32[]{:S(2)}, u32[]{:S(2)}) collective-permute-start(f32[385,384]{1,0:T(8,128)S(1)} %pad_maximum_fusion), channel_id=1, source_target_pairs={{0,4},{4,8},{8,12},{12,16},{16,20},{20,24},{24,28},{28,32},{32,36}... | collective-permute-start | bytes 1774088 | tf_op jit(solution)/shard_map/ppermute | solution.py:12
  68.2 16.5 %collective-permute-start.4 = (f32[385,384]{1,0:T(8,128)S(1)}, f32[385,384]{1,0:T(8,128)S(1)}, u32[]{:S(2)}, u32[]{:S(2)}) collective-permute-start(f32[385,384]{1,0:T(8,128)S(1)} %pad_maximum_fusion.1), channel_id=1, source_target_pairs={{0,8},{4,12},{8,16},{12,20},{16,24},{20,28},{24,32},{28,36},{32,40... | collective-permute-start | bytes 1774088 | tf_op jit(solution)/shard_map/ppermute | solution.py:12
  86.4 17.2 %collective-permute-start.5 = (f32[385,384]{1,0:T(8,128)S(1)}, f32[385,384]{1,0:T(8,128)S(1)}, u32[]{:S(2)}, u32[]{:S(2)}) collective-permute-start(f32[385,384]{1,0:T(8,128)S(1)} %pad_maximum_fusion.2), channel_id=1, source_target_pairs={{0,16},{4,20},{8,24},{12,28},{16,32},{20,36},{24,40},{28,44},{32,4... | collective-permute-start | bytes 1774088 | tf_op jit(solution)/shard_map/ppermute | solution.py:12
  105.1 14.1 %collective-permute-start.6 = (f32[385,384]{1,0:T(8,128)S(1)}, f32[385,384]{1,0:T(8,128)S(1)}, u32[]{:S(2)}, u32[]{:S(2)}) collective-permute-start(f32[385,384]{1,0:T(8,128)S(1)} %pad_maximum_fusion.3), channel_id=1, source_target_pairs={{0,32},{4,36},{8,40},{12,44},{16,48},{20,52},{24,56},{28,60},{32,6... | collective-permute-start | bytes 1774088 | tf_op jit(solution)/shard_map/ppermute | solution.py:12
  120.8 19.3 %collective-permute-start.7 = (f32[385,384]{1,0:T(8,128)S(1)}, f32[385,384]{1,0:T(8,128)S(1)}, u32[]{:S(2)}, u32[]{:S(2)}) collective-permute-start(f32[385,384]{1,0:T(8,128)S(1)} %pad_maximum_fusion.4), channel_id=1, source_target_pairs={{0,64},{4,68},{8,72},{12,76},{16,80},{20,84},{24,88},{28,92},{32,9... | collective-permute-start | bytes 1774088 | tf_op jit(solution)/shard_map/ppermute | solution.py:12
  141.5 23.8 %collective-permute-start.8 = (f32[384]{0:T(512)S(1)}, f32[384]{0:T(512)S(1)}, u32[]{:S(2)}, u32[]{:S(2)}) collective-permute-start(f32[384]{0:T(512)S(1)} %add.68), channel_id=1, source_target_pairs={{0,128},{4,132},{8,136},{12,140},{16,144},{20,148},{24,152},{28,15... | collective-permute-start | bytes 4616 | tf_op jit(solution)/shard_map/ppermute | solution.py:12
  165.8 4.9 %collective-permute-start.9 = (f32[384]{0:T(512)S(1)}, f32[384]{0:T(512)S(1)}, u32[]{:S(2)}, u32[]{:S(2)}) collective-permute-start(f32[384]{0:T(512)S(1)} %add.69), channel_id=1, source_target_pairs={{0,4},{4,8},{8,12},{12,16},{16,20},{20,24},{24,28},{28,32},{32,36}... | collective-permute-start | bytes 4616 | tf_op jit(solution)/shard_map/ppermute | solution.py:12

commit v8 on v7

--- a/solution.py
+++ b/solution.py
@@ -105,17 +105,16 @@
     acc_vec = jnp.where(is_first, jnp.dot(prior_mean, slab_t, precision=exact) + offset, offset)
     acc_t = jnp.where(is_first, jnp.zeros_like(slab_t), slab_t)
     distance = 1
-    while distance < tm_count:
-        if distance * 2 >= tm_count:
-            got_vec = passed_along(acc_vec, "tm", distance)
-            acc_vec = jnp.dot(got_vec, acc_t, precision=exact) + acc_vec
-        else:
-            carried = jnp.concatenate([acc_t, acc_vec[None]], axis=0)
-            got = jnp.dot(passed_along(carried, "tm", distance), acc_t, precision=exact)
-            acc_t = got[:state_width]
-            acc_vec = got[state_width] + acc_vec
+    while distance * 2 < tm_count:
+        carried = jnp.concatenate([acc_t, acc_vec[None]], axis=0)
+        got = jnp.dot(passed_along(carried, "tm", distance), acc_t, precision=exact)
+        acc_t = got[:state_width]
+        acc_vec = got[state_width] + acc_vec
         distance *= 2
-    state = jnp.where(is_first, prior_mean, passed_along(acc_vec, "tm", 1))
+    previous = passed_along(jnp.concatenate([acc_t, acc_vec[None]], axis=0), "tm", 1)
+    before_span = passed_along(acc_vec, "tm", distance + 1)
+    entering = jnp.dot(before_span, previous[:state_width], precision=exact) + previous[state_width]
+    state = jnp.where(is_first, prior_mean, entering)
     return run_recurrence(trans, forcing, state)
 
 

time: 180 us -> 178 us (0.989)
  the two profiles are of different devices: /device:TPU:24 before, /device:TPU:128 now
where the time goes in v8:
time: 178 us; the launch traced here: 175 us
  waiting for transfers between devices  95.2 us (53%)
  starting transfers between devices  31.1 us (17%)
  matrix products  22.4 us (13%)
  Pallas kernels  16.3 us (9%)
  local copies, waits for them, and re-layouts  6.78 us (4%)
  other arithmetic  2.83 us (2%)
    ppermute x7, waiting for transfers between devices, passed_along(): return lax.ppermute(block, axis, route)  91.2 us
    pallas_call x2, Pallas kernels, run_recurrence(): pl.pallas_call(recurrence_kernel, grid=(steps,), in_specs=[pl.BlockSpec((...  16.3 us
    all_to_all x1, starting transfers between devices, on_device(): lax.all_to_all(sent, ('tm', 'ingest'), split_axis=0, concat_axis=0, tiled...  13.8 us
    ppermute x7, starting transfers between devices, passed_along(): return lax.ppermute(block, axis, route)  12.2 us
    dot_general x1, matrix products, on_device(): jnp.einsum('jba,jcb->jac', pairs[:, 0], pairs[:, 1], precision=exact)  9.66 us
    dot_general x5, matrix products, on_device(): got = jnp.dot(passed_along(carried, 'tm', distance), acc_t, precision=exact)  7.1 us
    ppermute x3, starting transfers between devices, summed_over(): lax.ppermute(block, axis, [(i, (i + shift) % count) for i in range(count)])  5.11 us
    ppermute x3, waiting for transfers between devices, summed_over(): lax.ppermute(block, axis, [(i, (i + shift) % count) for i in range(count)])  4.02 us
  transfers between devices with their start and end apart: 11, of which 9 were waited for; matrix products, arithmetic and copies ran while one was open for 8% of the time, Pallas kernels for 0%

profile of v8, /device:TPU:128, one launch (start us, length us, event | category | flops | bytes accessed | tf_op | source)
XLA Modules:
  0.0 175.2 jit_solution(7286091092535251739)
XLA Ops:
  0.0 1.0 multiply_convert_fusion
  2.7 0.8 reduce.18
  3.5 0.9 reshape.164
  4.4 13.8 %all-to-all-start = ((bf16[256,2,196]{2,1,0:T(2,128)(2,1)}), bf16[256,2,196]{2,1,0:T(2,128)(2,1)S(1)}, u32[]{:S(2)}, u32[]{:S(2)}) async-start(bf16[256,2,196]{2,1,0:T(2,128)(2,1)} %reshape.164), calls=%async_computation | async-start | bytes 524288 | tf_op jit(solution)/shard_map/all_to_all | solution.py:86
  18.2 9.7 %fusion = f32[4,384,384]{2,1,0:T(8,128)S(1)} fusion(f32[4,2,384,384]{3,2,1,0:T(8,128)} %bitcast.68), kind=kOutput, calls=%fused_computation.2 | convolution fusion | flops 2717908992 | bytes 7077888 | tf_op jit(solution)/shard_map/jba,jcb->jac/dot_general | solution.py:96
  27.9 2.4 %convolution_bitcast_fusion = f32[1,2,384,384]{3,2,1,0:T(8,128)S(1)} fusion(f32[2,2,384,384]{3,2,1,0:T(8,128)S(1)} %bitcast.69), kind=kOutput, calls=%fused_computation.4 | convolution fusion | flops 1358954496 | bytes 3538944 | tf_op jit(solution)/shard_map/jab,jbc->jac/dot_general | solution.py:99
  30.3 1.3 broadcast_select_fusion
  34.9 3.1 %collective-permute-start.1 = (f32[8,384]{1,0:T(8,128)S(1)}, f32[8,384]{1,0:T(8,128)S(1)}, u32[]{:S(2)}, u32[]{:S(2)}) collective-permute-start(f32[8,384]{1,0:T(8,128)S(1)} %bitcast.74), channel_id=1, source_target_pairs={{0,2},{1,3},{2,0},{3,1},{4,6},{5,7},{6,4},{7,5},{8,10},{9,11},{10,... | collective-permute-start | bytes 36872 | tf_op jit(solution)/shard_map/ppermute | solution.py:18
  38.0 1.1 collective-permute-start.2
  39.1 0.9 collective-permute-start
  40.2 1.5 collective-permute-done.2
  41.7 2.4 %collective-permute-done = f32[8,384]{1,0:T(8,128)S(1)} collective-permute-done((f32[8,384]{1,0:T(8,128)S(1)}, f32[8,384]{1,0:T(8,128)S(1)}, u32[]{:S(2)}, u32[]{:S(2)}) %collective-permute-start) | collective-permute-done | bytes 12320 | tf_op jit(solution)/shard_map/ppermute | solution.py:18
  45.8 8.2 %shard_map.73 = f32[8,384]{1,0:T(8,128)} custom-call(f32[8,384,384]{2,1,0:T(8,128)} %map_ref.3, f32[8,384]{1,0:T(8,128)} %fusion.5.force_ref, f32[1,384]{1,0:T(1,128)} %reshape.138.start_ref), custom_call_target="tpu_custom_call" | custom-call | tf_op jit(solution)/shard_map/pallas_call | solution.py:49
  53.9 0.7 slice_reduce_fusion.6
  54.7 1.9 %collective-permute-start.3 = (f32[385,384]{1,0:T(8,128)S(1)}, f32[385,384]{1,0:T(8,128)S(1)}, u32[]{:S(2)}, u32[]{:S(2)}) collective-permute-start(f32[385,384]{1,0:T(8,128)S(1)} %pad_maximum_fusion), channel_id=1, source_target_pairs={{0,4},{4,8},{8,12},{12,16},{16,20},{20,24},{24,28},{28,32},{32,36}... | collective-permute-start | bytes 1774088 | tf_op jit(solution)/shard_map/ppermute | solution.py:12
  56.7 12.7 %collective-permute-done.3 = f32[385,384]{1,0:T(8,128)S(1)} collective-permute-done((f32[385,384]{1,0:T(8,128)S(1)}, f32[385,384]{1,0:T(8,128)S(1)}, u32[]{:S(2)}, u32[]{:S(2)}) %collective-permute-start.3) | collective-permute-done | bytes 591392 | tf_op jit(solution)/shard_map/ppermute | solution.py:12
  69.4 1.4 fusion.17
  71.0 1.9 %collective-permute-start.4 = (f32[385,384]{1,0:T(8,128)S(1)}, f32[385,384]{1,0:T(8,128)S(1)}, u32[]{:S(2)}, u32[]{:S(2)}) collective-permute-start(f32[385,384]{1,0:T(8,128)S(1)} %pad_maximum_fusion.1), channel_id=1, source_target_pairs={{0,8},{4,12},{8,16},{12,20},{16,24},{20,28},{24,32},{28,36},{32,40... | collective-permute-start | bytes 1774088 | tf_op jit(solution)/shard_map/ppermute | solution.py:12
  72.9 14.6 %collective-permute-done.4 = f32[385,384]{1,0:T(8,128)S(1)} collective-permute-done((f32[385,384]{1,0:T(8,128)S(1)}, f32[385,384]{1,0:T(8,128)S(1)}, u32[]{:S(2)}, u32[]{:S(2)}) %collective-permute-start.4) | collective-permute-done | bytes 591392 | tf_op jit(solution)/shard_map/ppermute | solution.py:12
  87.5 1.4 fusion.14
  89.1 1.9 %collective-permute-start.5 = (f32[385,384]{1,0:T(8,128)S(1)}, f32[385,384]{1,0:T(8,128)S(1)}, u32[]{:S(2)}, u32[]{:S(2)}) collective-permute-start(f32[385,384]{1,0:T(8,128)S(1)} %pad_maximum_fusion.2), channel_id=1, source_target_pairs={{0,16},{4,20},{8,24},{12,28},{16,32},{20,36},{24,40},{28,44},{32,4... | collective-permute-start | bytes 1774088 | tf_op jit(solution)/shard_map/ppermute | solution.py:12
  91.0 14.1 %collective-permute-done.5 = f32[385,384]{1,0:T(8,128)S(1)} collective-permute-done((f32[385,384]{1,0:T(8,128)S(1)}, f32[385,384]{1,0:T(8,128)S(1)}, u32[]{:S(2)}, u32[]{:S(2)}) %collective-permute-start.5) | collective-permute-done | bytes 591392 | tf_op jit(solution)/shard_map/ppermute | solution.py:12
  105.1 1.4 fusion.12
  106.7 1.9 %collective-permute-start.6 = (f32[385,384]{1,0:T(8,128)S(1)}, f32[385,384]{1,0:T(8,128)S(1)}, u32[]{:S(2)}, u32[]{:S(2)}) collective-permute-start(f32[385,384]{1,0:T(8,128)S(1)} %pad_maximum_fusion.3), channel_id=1, source_target_pairs={{0,32},{4,36},{8,40},{12,44},{16,48},{20,52},{24,56},{28,60},{32,6... | collective-permute-start | bytes 1774088 | tf_op jit(solution)/shard_map/ppermute | solution.py:12
  108.6 11.2 %collective-permute-done.6 = f32[385,384]{1,0:T(8,128)S(1)} collective-permute-done((f32[385,384]{1,0:T(8,128)S(1)}, f32[385,384]{1,0:T(8,128)S(1)}, u32[]{:S(2)}, u32[]{:S(2)}) %collective-permute-start.6) | collective-permute-done | bytes 591392 | tf_op jit(solution)/shard_map/ppermute | solution.py:12
  119.8 1.4 fusion.10
  121.3 1.9 %collective-permute-start.7 = (f32[385,384]{1,0:T(8,128)S(1)}, f32[385,384]{1,0:T(8,128)S(1)}, u32[]{:S(2)}, u32[]{:S(2)}) collective-permute-start(f32[385,384]{1,0:T(8,128)S(1)} %pad_maximum_fusion.4), channel_id=1, source_target_pairs={{0,64},{4,68},{8,72},{12,76},{16,80},{20,84},{24,88},{28,92},{32,9... | collective-permute-start | bytes 1774088 | tf_op jit(solution)/shard_map/ppermute | solution.py:12
  123.3 12.1 %collective-permute-done.7 = f32[385,384]{1,0:T(8,128)S(1)} collective-permute-done((f32[385,384]{1,0:T(8,128)S(1)}, f32[385,384]{1,0:T(8,128)S(1)}, u32[]{:S(2)}, u32[]{:S(2)}) %collective-permute-start.7) | collective-permute-done | bytes 591392 | tf_op jit(solution)/shard_map/ppermute | solution.py:12
  135.4 1.4 fusion.8
  136.9 1.9 %collective-permute-start.9 = (f32[385,384]{1,0:T(8,128)S(1)}, f32[385,384]{1,0:T(8,128)S(1)}, u32[]{:S(2)}, u32[]{:S(2)}) collective-permute-start(f32[385,384]{1,0:T(8,128)S(1)} %pad_maximum_fusion.5), channel_id=1, source_target_pairs={{0,4},{4,8},{8,12},{12,16},{16,20},{20,24},{24,28},{28,32},{32,36}... | collective-permute-start | bytes 1774088 | tf_op jit(solution)/shard_map/ppermute | solution.py:12
  139.5 26.5 %collective-permute-done.9 = f32[385,384]{1,0:T(8,128)S(1)} collective-permute-done((f32[385,384]{1,0:T(8,128)S(1)}, f32[385,384]{1,0:T(8,128)S(1)}, u32[]{:S(2)}, u32[]{:S(2)}) %collective-permute-start.9) | collective-permute-done | bytes 591392 | tf_op jit(solution)/shard_map/ppermute | solution.py:12
  167.1 8.2 %shard_map.74 = f32[8,384]{1,0:T(8,128)} custom-call(f32[8,384,384]{2,1,0:T(8,128)} %map_ref.3, f32[8,384]{1,0:T(8,128)} %fusion.5.force_ref, f32[1,384]{1,0:T(1,128)} %reshape.139.start_ref), custom_call_target="tpu_custom_call" | custom-call | tf_op jit(solution)/shard_map/pallas_call | solution.py:49
  (73 shorter events, 9.1 us)
Async XLA Ops:
  0.0 34.4 %copy-start = (f32[8,384,48]{1,2,0:T(8,128)S(1)}, f32[8,384,48]{1,2,0:T(8,128)}, u32[]{:S(2)}) copy-start(f32[8,384,48]{1,2,0:T(8,128)} %param.8) | copy-start | bytes 1769476
  0.0 1.9 %copy-start.2 = (s32[512]{0:T(512)S(1)}, s32[512]{0:T(512)}, u32[]{:S(2)}) copy-start(s32[512]{0:T(512)} %param.12) | copy-start | bytes 6148
  0.0 2.0 %copy-start.3 = (s32[1,64]{1,0:T(1,128)S(1)}, s32[1,64]{1,0:T(1,128)}, u32[]{:S(2)}) copy-start(s32[1,64]{1,0:T(1,128)} %param.13) | copy-start | bytes 772
  4.4 27.7 %all-to-all-start = ((bf16[256,2,196]{2,1,0:T(2,128)(2,1)}), bf16[256,2,196]{2,1,0:T(2,128)(2,1)S(1)}, u32[]{:S(2)}, u32[]{:S(2)}) async-start(bf16[256,2,196]{2,1,0:T(2,128)(2,1)} %reshape.164), calls=%async_computation | async-start | bytes 524288 | tf_op jit(solution)/shard_map/all_to_all | solution.py:86
  27.9 2.4 %copy-start.1 = (f32[384]{0:T(512)S(1)}, f32[384]{0:T(512)}, u32[]{:S(2)}) copy-start(f32[384]{0:T(512)} %param.9) | copy-start | bytes 4612
  34.9 5.3 %collective-permute-start.1 = (f32[8,384]{1,0:T(8,128)S(1)}, f32[8,384]{1,0:T(8,128)S(1)}, u32[]{:S(2)}, u32[]{:S(2)}) collective-permute-start(f32[8,384]{1,0:T(8,128)S(1)} %bitcast.74), channel_id=1, source_target_pairs={{0,2},{1,3},{2,0},{3,1},{4,6},{5,7},{6,4},{7,5},{8,10},{9,11},{10,... | collective-permute-start | bytes 36872 | tf_op jit(solution)/shard_map/ppermute | solution.py:18
  38.0 3.7 %collective-permute-start.2 = (f32[8,384]{1,0:T(8,128)S(1)}, f32[8,384]{1,0:T(8,128)S(1)}, u32[]{:S(2)}, u32[]{:S(2)}) collective-permute-start(f32[8,384]{1,0:T(8,128)S(1)} %bitcast.75), channel_id=1, source_target_pairs={{0,3},{1,0},{2,1},{3,2},{4,7},{5,4},{6,5},{7,6},{8,11},{9,8},{10,9... | collective-permute-start | bytes 36872 | tf_op jit(solution)/shard_map/ppermute | solution.py:18
  39.1 4.9 %collective-permute-start = (f32[8,384]{1,0:T(8,128)S(1)}, f32[8,384]{1,0:T(8,128)S(1)}, u32[]{:S(2)}, u32[]{:S(2)}) collective-permute-start(f32[8,384]{1,0:T(8,128)S(1)} %bitcast.76), channel_id=1, source_target_pairs={{0,1},{1,2},{2,3},{3,0},{4,5},{5,6},{6,7},{7,4},{8,9},{9,10},{10,1... | collective-permute-start | bytes 36872 | tf_op jit(solution)/shard_map/ppermute | solution.py:18
  54.7 14.7 %collective-permute-start.3 = (f32[385,384]{1,0:T(8,128)S(1)}, f32[385,384]{1,0:T(8,128)S(1)}, u32[]{:S(2)}, u32[]{:S(2)}) collective-permute-start(f32[385,384]{1,0:T(8,128)S(1)} %pad_maximum_fusion), channel_id=1, source_target_pairs={{0,4},{4,8},{8,12},{12,16},{16,20},{20,24},{24,28},{28,32},{32,36}... | collective-permute-start | bytes 1774088 | tf_op jit(solution)/shard_map/ppermute | solution.py:12
  71.0 16.6 %collective-permute-start.4 = (f32[385,384]{1,0:T(8,128)S(1)}, f32[385,384]{1,0:T(8,128)S(1)}, u32[]{:S(2)}, u32[]{:S(2)}) collective-permute-start(f32[385,384]{1,0:T(8,128)S(1)} %pad_maximum_fusion.1), channel_id=1, source_target_pairs={{0,8},{4,12},{8,16},{12,20},{16,24},{20,28},{24,32},{28,36},{32,40... | collective-permute-start | bytes 1774088 | tf_op jit(solution)/shard_map/ppermute | solution.py:12
  89.1 16.0 %collective-permute-start.5 = (f32[385,384]{1,0:T(8,128)S(1)}, f32[385,384]{1,0:T(8,128)S(1)}, u32[]{:S(2)}, u32[]{:S(2)}) collective-permute-start(f32[385,384]{1,0:T(8,128)S(1)} %pad_maximum_fusion.2), channel_id=1, source_target_pairs={{0,16},{4,20},{8,24},{12,28},{16,32},{20,36},{24,40},{28,44},{32,4... | collective-permute-start | bytes 1774088 | tf_op jit(solution)/shard_map/ppermute | solution.py:12
  106.7 13.1 %collective-permute-start.6 = (f32[385,384]{1,0:T(8,128)S(1)}, f32[385,384]{1,0:T(8,128)S(1)}, u32[]{:S(2)}, u32[]{:S(2)}) collective-permute-start(f32[385,384]{1,0:T(8,128)S(1)} %pad_maximum_fusion.3), channel_id=1, source_target_pairs={{0,32},{4,36},{8,40},{12,44},{16,48},{20,52},{24,56},{28,60},{32,6... | collective-permute-start | bytes 1774088 | tf_op jit(solution)/shard_map/ppermute | solution.py:12
  121.3 14.0 %collective-permute-start.7 = (f32[385,384]{1,0:T(8,128)S(1)}, f32[385,384]{1,0:T(8,128)S(1)}, u32[]{:S(2)}, u32[]{:S(2)}) collective-permute-start(f32[385,384]{1,0:T(8,128)S(1)} %pad_maximum_fusion.4), channel_id=1, source_target_pairs={{0,64},{4,68},{8,72},{12,76},{16,80},{20,84},{24,88},{28,92},{32,9... | collective-permute-start | bytes 1774088 | tf_op jit(solution)/shard_map/ppermute | solution.py:12
  136.9 29.1 %collective-permute-start.9 = (f32[385,384]{1,0:T(8,128)S(1)}, f32[385,384]{1,0:T(8,128)S(1)}, u32[]{:S(2)}, u32[]{:S(2)}) collective-permute-start(f32[385,384]{1,0:T(8,128)S(1)} %pad_maximum_fusion.5), channel_id=1, source_target_pairs={{0,4},{4,8},{8,12},{12,16},{16,20},{20,24},{24,28},{28,32},{32,36}... | collective-permute-start | bytes 1774088 | tf_op jit(solution)/shard_map/ppermute | solution.py:12
  138.9 0.7 collective-permute-start.8

commit v9 on v8

--- a/solution.py
+++ b/solution.py
@@ -104,7 +104,10 @@
     is_first = tm_index == 0
     acc_vec = jnp.where(is_first, jnp.dot(prior_mean, slab_t, precision=exact) + offset, offset)
     acc_t = jnp.where(is_first, jnp.zeros_like(slab_t), slab_t)
-    distance = 1
+    got_t = passed_along(acc_t, "tm", 1)
+    acc_vec = jnp.dot(passed_along(acc_vec, "tm", 1), acc_t, precision=exact) + acc_vec
+    acc_t = jnp.dot(got_t, acc_t, precision=exact)
+    distance = 2
     while distance * 2 < tm_count:
         carried = jnp.concatenate([acc_t, acc_vec[None]], axis=0)
         got = jnp.dot(passed_along(carried, "tm", distance), acc_t, precision=exact)

time: 178 us -> 177 us (level)
  waiting for transfers between devices: 95.2 us -> 90 us
  starting transfers between devices: 31.1 us -> 33.4 us
    ppermute x7 -> x8, waiting for transfers between devices: 91.2 us -> 85.9 us  [passed_along(): return lax.ppermute(block, axis, route)]
    dot_general x0 -> x2, matrix products: none -> 2.74 us  [the longest x1 2.33 us: on_device(): acc_t = jnp.dot(got_t, acc_t, precision=exact)]
    ppermute x7 -> x8, starting transfers between devices: 12.2 us -> 14.5 us  [passed_along(): return lax.ppermute(block, axis, route)]
    dot_general x5 -> x4, matrix products: 7.1 us -> 5.68 us  [on_device(): got = jnp.dot(passed_along(carried, 'tm', distance), acc_t, precision=exact)]
  transfers between devices with their start and end apart: 11 -> 12, of which waited for: 9 -> 9; matrix products, arithmetic and copies ran while one was open for 8% -> 11% of each run, Pallas kernels for 0% -> 5%
where the time goes in v9:
time: 177 us; the launch traced here: 174 us
  waiting for transfers between devices  90 us (51%)
  starting transfers between devices  33.4 us (19%)
  matrix products  23.7 us (13%)
  Pallas kernels  16.3 us (9%)
  local copies, waits for them, and re-layouts  6.71 us (4%)
  other arithmetic  2.79 us (2%)
    ppermute x8, waiting for transfers between devices, passed_along(): return lax.ppermute(block, axis, route)  85.9 us
    pallas_call x2, Pallas kernels, run_recurrence(): pl.pallas_call(recurrence_kernel, grid=(steps,), in_specs=[pl.BlockSpec((...  16.3 us
    ppermute x8, starting transfers between devices, passed_along(): return lax.ppermute(block, axis, route)  14.5 us
    all_to_all x1, starting transfers between devices, on_device(): lax.all_to_all(sent, ('tm', 'ingest'), split_axis=0, concat_axis=0, tiled...  13.8 us
    dot_general x1, matrix products, on_device(): jnp.einsum('jba,jcb->jac', pairs[:, 0], pairs[:, 1], precision=exact)  9.66 us
    dot_general x4, matrix products, on_device(): got = jnp.dot(passed_along(carried, 'tm', distance), acc_t, precision=exact)  5.68 us
    ppermute x3, starting transfers between devices, summed_over(): lax.ppermute(block, axis, [(i, (i + shift) % count) for i in range(count)])  5.11 us
    ppermute x3, waiting for transfers between devices, summed_over(): lax.ppermute(block, axis, [(i, (i + shift) % count) for i in range(count)])  4.15 us
  transfers between devices with their start and end apart: 12, of which 9 were waited for; matrix products, arithmetic and copies ran while one was open for 11% of the time, Pallas kernels for 5%

profile of v9, /device:TPU:128, one launch (start us, length us, event | category | flops | bytes accessed | tf_op | source)
XLA Modules:
  0.0 173.5 jit_solution(17888248817108455091)
XLA Ops:
  0.0 1.0 multiply_convert_fusion
  2.7 0.8 reduce.18
  3.5 0.9 reshape.166
  4.4 13.8 %all-to-all-start = ((bf16[256,2,196]{2,1,0:T(2,128)(2,1)}), bf16[256,2,196]{2,1,0:T(2,128)(2,1)S(1)}, u32[]{:S(2)}, u32[]{:S(2)}) async-start(bf16[256,2,196]{2,1,0:T(2,128)(2,1)} %reshape.166), calls=%async_computation | async-start | bytes 524288 | tf_op jit(solution)/shard_map/all_to_all | solution.py:86
  18.2 9.7 %fusion = f32[4,384,384]{2,1,0:T(8,128)S(1)} fusion(f32[4,2,384,384]{3,2,1,0:T(8,128)} %bitcast.71), kind=kOutput, calls=%fused_computation.2 | convolution fusion | flops 2717908992 | bytes 7077888 | tf_op jit(solution)/shard_map/jba,jcb->jac/dot_general | solution.py:96
  27.9 2.4 %convolution_bitcast_fusion = f32[1,2,384,384]{3,2,1,0:T(8,128)S(1)} fusion(f32[2,2,384,384]{3,2,1,0:T(8,128)S(1)} %bitcast.72), kind=kOutput, calls=%fused_computation.4 | convolution fusion | flops 1358954496 | bytes 3538944 | tf_op jit(solution)/shard_map/jab,jbc->jac/dot_general | solution.py:99
  30.3 1.3 broadcast_select_fusion
  31.5 2.2 %collective-permute-start.3 = (f32[384,384]{1,0:T(8,128)S(1)}, f32[384,384]{1,0:T(8,128)}, u32[]{:S(2)}, u32[]{:S(2)}) collective-permute-start(f32[384,384]{1,0:T(8,128)S(1)} %get-tuple-element.7), channel_id=1, source_target_pairs={{0,4},{4,8},{8,12},{12,16},{16,20},{20,24},{24,28},{28,32},{32,36}... | collective-permute-start | bytes 1769480 | tf_op jit(solution)/shard_map/ppermute | solution.py:12
  37.1 3.1 %collective-permute-start.1 = (f32[8,384]{1,0:T(8,128)S(1)}, f32[8,384]{1,0:T(8,128)S(1)}, u32[]{:S(2)}, u32[]{:S(2)}) collective-permute-start(f32[8,384]{1,0:T(8,128)S(1)} %bitcast.77), channel_id=1, source_target_pairs={{0,2},{1,3},{2,0},{3,1},{4,6},{5,7},{6,4},{7,5},{8,10},{9,11},{10,... | collective-permute-start | bytes 36872 | tf_op jit(solution)/shard_map/ppermute | solution.py:18
  40.2 1.2 collective-permute-start.2
  41.3 0.9 collective-permute-start
  42.4 1.5 collective-permute-done.2
  43.9 2.5 %collective-permute-done = f32[8,384]{1,0:T(8,128)S(1)} collective-permute-done((f32[8,384]{1,0:T(8,128)S(1)}, f32[8,384]{1,0:T(8,128)S(1)}, u32[]{:S(2)}, u32[]{:S(2)}) %collective-permute-start) | collective-permute-done | bytes 12320 | tf_op jit(solution)/shard_map/ppermute | solution.py:18
  48.1 8.2 %shard_map.73 = f32[8,384]{1,0:T(8,128)} custom-call(f32[8,384,384]{2,1,0:T(8,128)} %map_ref.3, f32[8,384]{1,0:T(8,128)} %fusion.5.force_ref, f32[1,384]{1,0:T(1,128)} %reshape.138.start_ref), custom_call_target="tpu_custom_call" | custom-call | tf_op jit(solution)/shard_map/pallas_call | solution.py:49
  57.0 2.0 %collective-permute-start.4 = (f32[384]{0:T(512)S(1)}, f32[384]{0:T(512)S(1)}, u32[]{:S(2)}, u32[]{:S(2)}) collective-permute-start(f32[384]{0:T(512)S(1)} %add_select_fusion), channel_id=1, source_target_pairs={{0,4},{4,8},{8,12},{12,16},{16,20},{20,24},{24,28},{28,32},{32,36}... | collective-permute-start | bytes 4616 | tf_op jit(solution)/shard_map/ppermute | solution.py:12
  59.0 6.2 %collective-permute-done.4 = f32[384]{0:T(512)S(1)} collective-permute-done((f32[384]{0:T(512)S(1)}, f32[384]{0:T(512)S(1)}, u32[]{:S(2)}, u32[]{:S(2)}) %collective-permute-start.4) | collective-permute-done | bytes 1568 | tf_op jit(solution)/shard_map/ppermute | solution.py:12
  65.7 2.3 %fusion.15 = f32[384,384]{1,0:T(8,128)S(1)} fusion(f32[384,384]{1,0:T(8,128)} %collective-permute-done.3, f32[384,384]{1,0:T(8,128)S(1)} %get-tuple-element.7), kind=kOutput, calls=%fused_computation.57 | convolution fusion | flops 679477248 | bytes 1769472 | tf_op jit(solution)/shard_map/dot_general | solution.py:109
  68.1 1.9 %collective-permute-start.5 = (f32[385,384]{1,0:T(8,128)S(1)}, f32[385,384]{1,0:T(8,128)S(1)}, u32[]{:S(2)}, u32[]{:S(2)}) collective-permute-start(f32[385,384]{1,0:T(8,128)S(1)} %pad_maximum_fusion), channel_id=1, source_target_pairs={{0,8},{4,12},{8,16},{12,20},{16,24},{20,28},{24,32},{28,36},{32,40... | collective-permute-start | bytes 1774088 | tf_op jit(solution)/shard_map/ppermute | solution.py:12
  70.0 14.8 %collective-permute-done.5 = f32[385,384]{1,0:T(8,128)S(1)} collective-permute-done((f32[385,384]{1,0:T(8,128)S(1)}, f32[385,384]{1,0:T(8,128)S(1)}, u32[]{:S(2)}, u32[]{:S(2)}) %collective-permute-start.5) | collective-permute-done | bytes 591392 | tf_op jit(solution)/shard_map/ppermute | solution.py:12
  84.8 1.4 fusion.16
  86.4 1.9 %collective-permute-start.6 = (f32[385,384]{1,0:T(8,128)S(1)}, f32[385,384]{1,0:T(8,128)S(1)}, u32[]{:S(2)}, u32[]{:S(2)}) collective-permute-start(f32[385,384]{1,0:T(8,128)S(1)} %pad_maximum_fusion.1), channel_id=1, source_target_pairs={{0,16},{4,20},{8,24},{12,28},{16,32},{20,36},{24,40},{28,44},{32,4... | collective-permute-start | bytes 1774088 | tf_op jit(solution)/shard_map/ppermute | solution.py:12
  88.3 14.3 %collective-permute-done.6 = f32[385,384]{1,0:T(8,128)S(1)} collective-permute-done((f32[385,384]{1,0:T(8,128)S(1)}, f32[385,384]{1,0:T(8,128)S(1)}, u32[]{:S(2)}, u32[]{:S(2)}) %collective-permute-start.6) | collective-permute-done | bytes 591392 | tf_op jit(solution)/shard_map/ppermute | solution.py:12
  102.6 1.4 fusion.12
  104.2 1.9 %collective-permute-start.7 = (f32[385,384]{1,0:T(8,128)S(1)}, f32[385,384]{1,0:T(8,128)S(1)}, u32[]{:S(2)}, u32[]{:S(2)}) collective-permute-start(f32[385,384]{1,0:T(8,128)S(1)} %pad_maximum_fusion.2), channel_id=1, source_target_pairs={{0,32},{4,36},{8,40},{12,44},{16,48},{20,52},{24,56},{28,60},{32,6... | collective-permute-start | bytes 1774088 | tf_op jit(solution)/shard_map/ppermute | solution.py:12
  106.1 11.3 %collective-permute-done.7 = f32[385,384]{1,0:T(8,128)S(1)} collective-permute-done((f32[385,384]{1,0:T(8,128)S(1)}, f32[385,384]{1,0:T(8,128)S(1)}, u32[]{:S(2)}, u32[]{:S(2)}) %collective-permute-start.7) | collective-permute-done | bytes 591392 | tf_op jit(solution)/shard_map/ppermute | solution.py:12
  117.4 1.4 fusion.10
  119.0 1.9 %collective-permute-start.8 = (f32[385,384]{1,0:T(8,128)S(1)}, f32[385,384]{1,0:T(8,128)S(1)}, u32[]{:S(2)}, u32[]{:S(2)}) collective-permute-start(f32[385,384]{1,0:T(8,128)S(1)} %pad_maximum_fusion.3), channel_id=1, source_target_pairs={{0,64},{4,68},{8,72},{12,76},{16,80},{20,84},{24,88},{28,92},{32,9... | collective-permute-start | bytes 1774088 | tf_op jit(solution)/shard_map/ppermute | solution.py:12
  120.9 12.2 %collective-permute-done.8 = f32[385,384]{1,0:T(8,128)S(1)} collective-permute-done((f32[385,384]{1,0:T(8,128)S(1)}, f32[385,384]{1,0:T(8,128)S(1)}, u32[]{:S(2)}, u32[]{:S(2)}) %collective-permute-start.8) | collective-permute-done | bytes 591392 | tf_op jit(solution)/shard_map/ppermute | solution.py:12
  133.1 1.4 fusion.8
  134.7 1.9 %collective-permute-start.10 = (f32[385,384]{1,0:T(8,128)S(1)}, f32[385,384]{1,0:T(8,128)S(1)}, u32[]{:S(2)}, u32[]{:S(2)}) collective-permute-start(f32[385,384]{1,0:T(8,128)S(1)} %pad_maximum_fusion.4), channel_id=1, source_target_pairs={{0,4},{4,8},{8,12},{12,16},{16,20},{20,24},{24,28},{28,32},{32,36}... | collective-permute-start | bytes 1774088 | tf_op jit(solution)/shard_map/ppermute | solution.py:12
  137.3 27.0 %collective-permute-done.10 = f32[385,384]{1,0:T(8,128)S(1)} collective-permute-done((f32[385,384]{1,0:T(8,128)S(1)}, f32[385,384]{1,0:T(8,128)S(1)}, u32[]{:S(2)}, u32[]{:S(2)}) %collective-permute-start.10) | collective-permute-done | bytes 591392 | tf_op jit(solution)/shard_map/ppermute | solution.py:12
  165.4 8.2 %shard_map.74 = f32[8,384]{1,0:T(8,128)} custom-call(f32[8,384,384]{2,1,0:T(8,128)} %map_ref.3, f32[8,384]{1,0:T(8,128)} %fusion.5.force_ref, f32[1,384]{1,0:T(1,128)} %reshape.139.start_ref), custom_call_target="tpu_custom_call" | custom-call | tf_op jit(solution)/shard_map/pallas_call | solution.py:49
  (73 shorter events, 10.1 us)
Async XLA Ops:
  0.0 36.6 %copy-start = (f32[8,384,48]{1,2,0:T(8,128)S(1)}, f32[8,384,48]{1,2,0:T(8,128)}, u32[]{:S(2)}) copy-start(f32[8,384,48]{1,2,0:T(8,128)} %param.8) | copy-start | bytes 1769476
  0.0 1.9 %copy-start.2 = (s32[512]{0:T(512)S(1)}, s32[512]{0:T(512)}, u32[]{:S(2)}) copy-start(s32[512]{0:T(512)} %param.12) | copy-start | bytes 6148
  0.0 2.0 %copy-start.3 = (s32[1,64]{1,0:T(1,128)S(1)}, s32[1,64]{1,0:T(1,128)}, u32[]{:S(2)}) copy-start(s32[1,64]{1,0:T(1,128)} %param.13) | copy-start | bytes 772
  4.4 29.9 %all-to-all-start = ((bf16[256,2,196]{2,1,0:T(2,128)(2,1)}), bf16[256,2,196]{2,1,0:T(2,128)(2,1)S(1)}, u32[]{:S(2)}, u32[]{:S(2)}) async-start(bf16[256,2,196]{2,1,0:T(2,128)(2,1)} %reshape.166), calls=%async_computation | async-start | bytes 524288 | tf_op jit(solution)/shard_map/all_to_all | solution.py:86
  27.9 5.9 %copy-start.1 = (f32[384]{0:T(512)S(1)}, f32[384]{0:T(512)}, u32[]{:S(2)}) copy-start(f32[384]{0:T(512)} %param.9) | copy-start | bytes 4612
  31.5 34.1 %collective-permute-start.3 = (f32[384,384]{1,0:T(8,128)S(1)}, f32[384,384]{1,0:T(8,128)}, u32[]{:S(2)}, u32[]{:S(2)}) collective-permute-start(f32[384,384]{1,0:T(8,128)S(1)} %get-tuple-element.7), channel_id=1, source_target_pairs={{0,4},{4,8},{8,12},{12,16},{16,20},{20,24},{24,28},{28,32},{32,36}... | collective-permute-start | bytes 1769480 | tf_op jit(solution)/shard_map/ppermute | solution.py:12
  37.1 5.3 %collective-permute-start.1 = (f32[8,384]{1,0:T(8,128)S(1)}, f32[8,384]{1,0:T(8,128)S(1)}, u32[]{:S(2)}, u32[]{:S(2)}) collective-permute-start(f32[8,384]{1,0:T(8,128)S(1)} %bitcast.77), channel_id=1, source_target_pairs={{0,2},{1,3},{2,0},{3,1},{4,6},{5,7},{6,4},{7,5},{8,10},{9,11},{10,... | collective-permute-start | bytes 36872 | tf_op jit(solution)/shard_map/ppermute | solution.py:18
  40.2 3.7 %collective-permute-start.2 = (f32[8,384]{1,0:T(8,128)S(1)}, f32[8,384]{1,0:T(8,128)S(1)}, u32[]{:S(2)}, u32[]{:S(2)}) collective-permute-start(f32[8,384]{1,0:T(8,128)S(1)} %bitcast.78), channel_id=1, source_target_pairs={{0,3},{1,0},{2,1},{3,2},{4,7},{5,4},{6,5},{7,6},{8,11},{9,8},{10,9... | collective-permute-start | bytes 36872 | tf_op jit(solution)/shard_map/ppermute | solution.py:18
  41.3 5.0 %collective-permute-start = (f32[8,384]{1,0:T(8,128)S(1)}, f32[8,384]{1,0:T(8,128)S(1)}, u32[]{:S(2)}, u32[]{:S(2)}) collective-permute-start(f32[8,384]{1,0:T(8,128)S(1)} %bitcast.79), channel_id=1, source_target_pairs={{0,1},{1,2},{2,3},{3,0},{4,5},{5,6},{6,7},{7,4},{8,9},{9,10},{10,1... | collective-permute-start | bytes 36872 | tf_op jit(solution)/shard_map/ppermute | solution.py:18
  57.0 8.2 %collective-permute-start.4 = (f32[384]{0:T(512)S(1)}, f32[384]{0:T(512)S(1)}, u32[]{:S(2)}, u32[]{:S(2)}) collective-permute-start(f32[384]{0:T(512)S(1)} %add_select_fusion), channel_id=1, source_target_pairs={{0,4},{4,8},{8,12},{12,16},{16,20},{20,24},{24,28},{28,32},{32,36}... | collective-permute-start | bytes 4616 | tf_op jit(solution)/shard_map/ppermute | solution.py:12
  68.1 16.8 %collective-permute-start.5 = (f32[385,384]{1,0:T(8,128)S(1)}, f32[385,384]{1,0:T(8,128)S(1)}, u32[]{:S(2)}, u32[]{:S(2)}) collective-permute-start(f32[385,384]{1,0:T(8,128)S(1)} %pad_maximum_fusion), channel_id=1, source_target_pairs={{0,8},{4,12},{8,16},{12,20},{16,24},{20,28},{24,32},{28,36},{32,40... | collective-permute-start | bytes 1774088 | tf_op jit(solution)/shard_map/ppermute | solution.py:12
  86.4 16.2 %collective-permute-start.6 = (f32[385,384]{1,0:T(8,128)S(1)}, f32[385,384]{1,0:T(8,128)S(1)}, u32[]{:S(2)}, u32[]{:S(2)}) collective-permute-start(f32[385,384]{1,0:T(8,128)S(1)} %pad_maximum_fusion.1), channel_id=1, source_target_pairs={{0,16},{4,20},{8,24},{12,28},{16,32},{20,36},{24,40},{28,44},{32,4... | collective-permute-start | bytes 1774088 | tf_op jit(solution)/shard_map/ppermute | solution.py:12
  104.2 13.2 %collective-permute-start.7 = (f32[385,384]{1,0:T(8,128)S(1)}, f32[385,384]{1,0:T(8,128)S(1)}, u32[]{:S(2)}, u32[]{:S(2)}) collective-permute-start(f32[385,384]{1,0:T(8,128)S(1)} %pad_maximum_fusion.2), channel_id=1, source_target_pairs={{0,32},{4,36},{8,40},{12,44},{16,48},{20,52},{24,56},{28,60},{32,6... | collective-permute-start | bytes 1774088 | tf_op jit(solution)/shard_map/ppermute | solution.py:12
  119.0 14.2 %collective-permute-start.8 = (f32[385,384]{1,0:T(8,128)S(1)}, f32[385,384]{1,0:T(8,128)S(1)}, u32[]{:S(2)}, u32[]{:S(2)}) collective-permute-start(f32[385,384]{1,0:T(8,128)S(1)} %pad_maximum_fusion.3), channel_id=1, source_target_pairs={{0,64},{4,68},{8,72},{12,76},{16,80},{20,84},{24,88},{28,92},{32,9... | collective-permute-start | bytes 1774088 | tf_op jit(solution)/shard_map/ppermute | solution.py:12
  134.7 29.6 %collective-permute-start.10 = (f32[385,384]{1,0:T(8,128)S(1)}, f32[385,384]{1,0:T(8,128)S(1)}, u32[]{:S(2)}, u32[]{:S(2)}) collective-permute-start(f32[385,384]{1,0:T(8,128)S(1)} %pad_maximum_fusion.4), channel_id=1, source_target_pairs={{0,4},{4,8},{8,12},{12,16},{16,20},{20,24},{24,28},{28,32},{32,36}... | collective-permute-start | bytes 1774088 | tf_op jit(solution)/shard_map/ppermute | solution.py:12
  136.6 0.7 collective-permute-start.9

commit v10 on v9

--- a/solution.py
+++ b/solution.py
@@ -36,7 +36,7 @@
         state_ref[...],
         map_ref[0],
         (((1,), (1,)), ((), ())),
-        precision=lax.Precision.HIGHEST,
+        precision=lax.Precision.HIGH,
         preferred_element_type=jnp.float32,
     )
     state = moved + force_ref[pl.ds(step, 1), :]
@@ -63,7 +63,7 @@
 def on_device(
     trans, gain, prior_mean, obs_basis, obs_value, measurement_within_tile, observed_row_count
 ):
-    exact = lax.Precision.HIGHEST
+    precise = lax.Precision.HIGH
     tm_count = lax.axis_size("tm")
     in_count = lax.axis_size("ingest")
     steps_here = trans.shape[0]
@@ -89,34 +89,34 @@
     step_ids = lax.broadcasted_iota(jnp.int32, (1, steps_here), 1)
     onehot = (got_marks[:, None] == step_ids).astype(jnp.bfloat16)
     drive_piece = jnp.einsum("rl,rq->lq", onehot, got_rows, preferred_element_type=jnp.float32)
-    partial_force = jnp.einsum("lsq,lq->ls", gain, drive_piece, precision=exact)
+    partial_force = jnp.einsum("lsq,lq->ls", gain, drive_piece, precision=precise)
     forcing = summed_over(partial_force, "ingest")
 
     pairs = trans.reshape(steps_here // 2, 2, state_width, state_width)
-    level_t = jnp.einsum("jba,jcb->jac", pairs[:, 0], pairs[:, 1], precision=exact)
+    level_t = jnp.einsum("jba,jcb->jac", pairs[:, 0], pairs[:, 1], precision=precise)
     while level_t.shape[0] > 1:
         map_pairs = level_t.reshape(-1, 2, state_width, state_width)
-        level_t = jnp.einsum("jab,jbc->jac", map_pairs[:, 0], map_pairs[:, 1], precision=exact)
+        level_t = jnp.einsum("jab,jbc->jac", map_pairs[:, 0], map_pairs[:, 1], precision=precise)
     slab_t = level_t[0]
     offset = run_recurrence(trans, forcing, jnp.zeros((state_width,), jnp.float32))[-1]
 
     tm_index = lax.axis_index("tm")
     is_first = tm_index == 0
-    acc_vec = jnp.where(is_first, jnp.dot(prior_mean, slab_t, precision=exact) + offset, offset)
+    acc_vec = jnp.where(is_first, jnp.dot(prior_mean, slab_t, precision=precise) + offset, offset)
     acc_t = jnp.where(is_first, jnp.zeros_like(slab_t), slab_t)
     got_t = passed_along(acc_t, "tm", 1)
-    acc_vec = jnp.dot(passed_along(acc_vec, "tm", 1), acc_t, precision=exact) + acc_vec
-    acc_t = jnp.dot(got_t, acc_t, precision=exact)
+    acc_vec = jnp.dot(passed_along(acc_vec, "tm", 1), acc_t, precision=precise) + acc_vec
+    acc_t = jnp.dot(got_t, acc_t, precision=precise)
     distance = 2
     while distance * 2 < tm_count:
         carried = jnp.concatenate([acc_t, acc_vec[None]], axis=0)
-        got = jnp.dot(passed_along(carried, "tm", distance), acc_t, precision=exact)
+        got = jnp.dot(passed_along(carried, "tm", distance), acc_t, precision=precise)
         acc_t = got[:state_width]
         acc_vec = got[state_width] + acc_vec
         distance *= 2
     previous = passed_along(jnp.concatenate([acc_t, acc_vec[None]], axis=0), "tm", 1)
     before_span = passed_along(acc_vec, "tm", distance + 1)
-    entering = jnp.dot(before_span, previous[:state_width], precision=exact) + previous[state_width]
+    entering = jnp.dot(before_span, previous[:state_width], precision=precise) + previous[state_width]
     state = jnp.where(is_first, prior_mean, entering)
     return run_recurrence(trans, forcing, state)
 

time: 177 us -> 165 us (0.932)
  matrix products: 23.7 us -> 15.3 us
  Pallas kernels: 16.3 us -> 13.9 us
    dot_general x12, matrix products: 23 us -> 14.6 us  [the longest x1 6.36 us: on_device(): jnp.einsum('jba,jcb->jac', pairs[:, 0], pairs[:, 1], precision=precise)]
    pallas_call x2, Pallas kernels: 16.3 us -> 13.9 us  [run_recurrence(): pl.pallas_call(recurrence_kernel, grid=(steps,), in_specs=[pl.BlockSpec((...]
  transfers between devices with their start and end apart: 12 -> 12, of which waited for: 9 -> 9; matrix products, arithmetic and copies ran while one was open for 11% -> 9% of each run, Pallas kernels for 5% -> 4%
where the time goes in v10:
time: 165 us; the launch traced here: 162 us
  waiting for transfers between devices  89.9 us (54%)
  starting transfers between devices  33.4 us (20%)
  matrix products  15.3 us (9%)
  Pallas kernels  13.9 us (8%)
  local copies, waits for them, and re-layouts  6.72 us (4%)
  other arithmetic  2.79 us (2%)
    ppermute x8, waiting for transfers between devices, passed_along(): return lax.ppermute(block, axis, route)  85.8 us
    ppermute x8, starting transfers between devices, passed_along(): return lax.ppermute(block, axis, route)  14.4 us
    pallas_call x2, Pallas kernels, run_recurrence(): pl.pallas_call(recurrence_kernel, grid=(steps,), in_specs=[pl.BlockSpec((...  13.9 us
    all_to_all x1, starting transfers between devices, on_device(): lax.all_to_all(sent, ('tm', 'ingest'), split_axis=0, concat_axis=0, tiled...  13.8 us
    dot_general x1, matrix products, on_device(): jnp.einsum('jba,jcb->jac', pairs[:, 0], pairs[:, 1], precision=precise)  6.36 us
    ppermute x3, starting transfers between devices, summed_over(): lax.ppermute(block, axis, [(i, (i + shift) % count) for i in range(count)])  5.11 us
    ppermute x3, waiting for transfers between devices, summed_over(): lax.ppermute(block, axis, [(i, (i + shift) % count) for i in range(count)])  4.15 us
  transfers between devices with their start and end apart: 12, of which 9 were waited for; matrix products, arithmetic and copies ran while one was open for 9% of the time, Pallas kernels for 4%

profile of v10, /device:TPU:128, one launch (start us, length us, event | category | flops | bytes accessed | tf_op | source)
XLA Modules:
  0.0 162.4 jit_solution(842326556063341853)
XLA Ops:
  0.0 1.0 multiply_convert_fusion
  2.7 0.8 reduce.18
  3.5 0.9 reshape.166
  4.4 13.8 %all-to-all-start = ((bf16[256,2,196]{2,1,0:T(2,128)(2,1)}), bf16[256,2,196]{2,1,0:T(2,128)(2,1)S(1)}, u32[]{:S(2)}, u32[]{:S(2)}) async-start(bf16[256,2,196]{2,1,0:T(2,128)(2,1)} %reshape.166), calls=%async_computation | async-start | bytes 524288 | tf_op jit(solution)/shard_map/all_to_all | solution.py:86
  18.2 6.4 %fusion = f32[4,384,384]{2,1,0:T(8,128)S(1)} fusion(f32[4,2,384,384]{3,2,1,0:T(8,128)} %bitcast.71), kind=kOutput, calls=%fused_computation.2 | convolution fusion | flops 1358954496 | bytes 7077888 | tf_op jit(solution)/shard_map/jba,jcb->jac/dot_general | solution.py:96
  24.6 1.3 convolution_bitcast_fusion
  26.6 2.0 %collective-permute-start.3 = (f32[384,384]{1,0:T(8,128)S(1)}, f32[384,384]{1,0:T(8,128)}, u32[]{:S(2)}, u32[]{:S(2)}) collective-permute-start(f32[384,384]{1,0:T(8,128)S(1)} %get-tuple-element.7), channel_id=1, source_target_pairs={{0,4},{4,8},{8,12},{12,16},{16,20},{20,24},{24,28},{28,32},{32,36}... | collective-permute-start | bytes 1769480 | tf_op jit(solution)/shard_map/ppermute | solution.py:12
  31.7 3.1 %collective-permute-start.1 = (f32[8,384]{1,0:T(8,128)S(1)}, f32[8,384]{1,0:T(8,128)S(1)}, u32[]{:S(2)}, u32[]{:S(2)}) collective-permute-start(f32[8,384]{1,0:T(8,128)S(1)} %bitcast.77), channel_id=1, source_target_pairs={{0,2},{1,3},{2,0},{3,1},{4,6},{5,7},{6,4},{7,5},{8,10},{9,11},{10,... | collective-permute-start | bytes 36872 | tf_op jit(solution)/shard_map/ppermute | solution.py:18
  34.8 1.2 collective-permute-start.2
  35.9 0.9 collective-permute-start
  37.0 1.5 collective-permute-done.2
  38.5 2.5 %collective-permute-done = f32[8,384]{1,0:T(8,128)S(1)} collective-permute-done((f32[8,384]{1,0:T(8,128)S(1)}, f32[8,384]{1,0:T(8,128)S(1)}, u32[]{:S(2)}, u32[]{:S(2)}) %collective-permute-start) | collective-permute-done | bytes 12320 | tf_op jit(solution)/shard_map/ppermute | solution.py:18
  42.7 6.9 %shard_map.73 = f32[8,384]{1,0:T(8,128)} custom-call(f32[8,384,384]{2,1,0:T(8,128)} %map_ref.3, f32[8,384]{1,0:T(8,128)} %fusion.5.force_ref, f32[1,384]{1,0:T(1,128)} %reshape.138.start_ref), custom_call_target="tpu_custom_call" | custom-call | tf_op jit(solution)/shard_map/pallas_call | solution.py:49
  49.6 0.7 slice_reduce_fusion.5
  50.4 2.1 %collective-permute-start.4 = (f32[384]{0:T(512)S(1)}, f32[384]{0:T(512)S(1)}, u32[]{:S(2)}, u32[]{:S(2)}) collective-permute-start(f32[384]{0:T(512)S(1)} %add_select_fusion), channel_id=1, source_target_pairs={{0,4},{4,8},{8,12},{12,16},{16,20},{20,24},{24,28},{28,32},{32,36}... | collective-permute-start | bytes 4616 | tf_op jit(solution)/shard_map/ppermute | solution.py:12
  52.5 6.1 %collective-permute-done.4 = f32[384]{0:T(512)S(1)} collective-permute-done((f32[384]{0:T(512)S(1)}, f32[384]{0:T(512)S(1)}, u32[]{:S(2)}, u32[]{:S(2)}) %collective-permute-start.4) | collective-permute-done | bytes 1568 | tf_op jit(solution)/shard_map/ppermute | solution.py:12
  58.9 1.8 %fusion.15 = f32[384,384]{1,0:T(8,128)S(1)} fusion(f32[384,384]{1,0:T(8,128)} %collective-permute-done.3, f32[384,384]{1,0:T(8,128)S(1)} %get-tuple-element.7), kind=kOutput, calls=%fused_computation.57 | convolution fusion | flops 339738624 | bytes 1769472 | tf_op jit(solution)/shard_map/dot_general | solution.py:109
  60.7 1.9 %collective-permute-start.5 = (f32[385,384]{1,0:T(8,128)S(1)}, f32[385,384]{1,0:T(8,128)S(1)}, u32[]{:S(2)}, u32[]{:S(2)}) collective-permute-start(f32[385,384]{1,0:T(8,128)S(1)} %pad_maximum_fusion), channel_id=1, source_target_pairs={{0,8},{4,12},{8,16},{12,20},{16,24},{20,28},{24,32},{28,36},{32,40... | collective-permute-start | bytes 1774088 | tf_op jit(solution)/shard_map/ppermute | solution.py:12
  62.7 14.8 %collective-permute-done.5 = f32[385,384]{1,0:T(8,128)S(1)} collective-permute-done((f32[385,384]{1,0:T(8,128)S(1)}, f32[385,384]{1,0:T(8,128)S(1)}, u32[]{:S(2)}, u32[]{:S(2)}) %collective-permute-start.5) | collective-permute-done | bytes 591392 | tf_op jit(solution)/shard_map/ppermute | solution.py:12
  77.5 0.8 fusion.16
  78.5 1.9 %collective-permute-start.6 = (f32[385,384]{1,0:T(8,128)S(1)}, f32[385,384]{1,0:T(8,128)S(1)}, u32[]{:S(2)}, u32[]{:S(2)}) collective-permute-start(f32[385,384]{1,0:T(8,128)S(1)} %pad_maximum_fusion.1), channel_id=1, source_target_pairs={{0,16},{4,20},{8,24},{12,28},{16,32},{20,36},{24,40},{28,44},{32,4... | collective-permute-start | bytes 1774088 | tf_op jit(solution)/shard_map/ppermute | solution.py:12
  80.4 14.3 %collective-permute-done.6 = f32[385,384]{1,0:T(8,128)S(1)} collective-permute-done((f32[385,384]{1,0:T(8,128)S(1)}, f32[385,384]{1,0:T(8,128)S(1)}, u32[]{:S(2)}, u32[]{:S(2)}) %collective-permute-start.6) | collective-permute-done | bytes 591392 | tf_op jit(solution)/shard_map/ppermute | solution.py:12
  94.7 0.8 fusion.12
  95.6 1.9 %collective-permute-start.7 = (f32[385,384]{1,0:T(8,128)S(1)}, f32[385,384]{1,0:T(8,128)S(1)}, u32[]{:S(2)}, u32[]{:S(2)}) collective-permute-start(f32[385,384]{1,0:T(8,128)S(1)} %pad_maximum_fusion.2), channel_id=1, source_target_pairs={{0,32},{4,36},{8,40},{12,44},{16,48},{20,52},{24,56},{28,60},{32,6... | collective-permute-start | bytes 1774088 | tf_op jit(solution)/shard_map/ppermute | solution.py:12
  97.5 11.3 %collective-permute-done.7 = f32[385,384]{1,0:T(8,128)S(1)} collective-permute-done((f32[385,384]{1,0:T(8,128)S(1)}, f32[385,384]{1,0:T(8,128)S(1)}, u32[]{:S(2)}, u32[]{:S(2)}) %collective-permute-start.7) | collective-permute-done | bytes 591392 | tf_op jit(solution)/shard_map/ppermute | solution.py:12
  108.9 0.8 fusion.10
  109.8 1.9 %collective-permute-start.8 = (f32[385,384]{1,0:T(8,128)S(1)}, f32[385,384]{1,0:T(8,128)S(1)}, u32[]{:S(2)}, u32[]{:S(2)}) collective-permute-start(f32[385,384]{1,0:T(8,128)S(1)} %pad_maximum_fusion.3), channel_id=1, source_target_pairs={{0,64},{4,68},{8,72},{12,76},{16,80},{20,84},{24,88},{28,92},{32,9... | collective-permute-start | bytes 1774088 | tf_op jit(solution)/shard_map/ppermute | solution.py:12
  111.7 12.7 %collective-permute-done.8 = f32[385,384]{1,0:T(8,128)S(1)} collective-permute-done((f32[385,384]{1,0:T(8,128)S(1)}, f32[385,384]{1,0:T(8,128)S(1)}, u32[]{:S(2)}, u32[]{:S(2)}) %collective-permute-start.8) | collective-permute-done | bytes 591392 | tf_op jit(solution)/shard_map/ppermute | solution.py:12
  124.5 0.8 fusion.8
  125.4 1.9 %collective-permute-start.10 = (f32[385,384]{1,0:T(8,128)S(1)}, f32[385,384]{1,0:T(8,128)S(1)}, u32[]{:S(2)}, u32[]{:S(2)}) collective-permute-start(f32[385,384]{1,0:T(8,128)S(1)} %pad_maximum_fusion.4), channel_id=1, source_target_pairs={{0,4},{4,8},{8,12},{12,16},{16,20},{20,24},{24,28},{28,32},{32,36}... | collective-permute-start | bytes 1774088 | tf_op jit(solution)/shard_map/ppermute | solution.py:12
  128.0 26.5 %collective-permute-done.10 = f32[385,384]{1,0:T(8,128)S(1)} collective-permute-done((f32[385,384]{1,0:T(8,128)S(1)}, f32[385,384]{1,0:T(8,128)S(1)}, u32[]{:S(2)}, u32[]{:S(2)}) %collective-permute-start.10) | collective-permute-done | bytes 591392 | tf_op jit(solution)/shard_map/ppermute | solution.py:12
  155.5 6.9 %shard_map.74 = f32[8,384]{1,0:T(8,128)} custom-call(f32[8,384,384]{2,1,0:T(8,128)} %map_ref.3, f32[8,384]{1,0:T(8,128)} %fusion.5.force_ref, f32[1,384]{1,0:T(1,128)} %reshape.139.start_ref), custom_call_target="tpu_custom_call" | custom-call | tf_op jit(solution)/shard_map/pallas_call | solution.py:49
  (73 shorter events, 9.5 us)
Async XLA Ops:
  0.0 31.4 %copy-start = (f32[8,384,48]{1,2,0:T(8,128)S(1)}, f32[8,384,48]{1,2,0:T(8,128)}, u32[]{:S(2)}) copy-start(f32[8,384,48]{1,2,0:T(8,128)} %param.8) | copy-start | bytes 1769476
  0.0 1.9 %copy-start.2 = (s32[512]{0:T(512)S(1)}, s32[512]{0:T(512)}, u32[]{:S(2)}) copy-start(s32[512]{0:T(512)} %param.12) | copy-start | bytes 6148
  0.0 2.0 %copy-start.3 = (s32[1,64]{1,0:T(1,128)S(1)}, s32[1,64]{1,0:T(1,128)}, u32[]{:S(2)}) copy-start(s32[1,64]{1,0:T(1,128)} %param.13) | copy-start | bytes 772
  4.4 24.6 %all-to-all-start = ((bf16[256,2,196]{2,1,0:T(2,128)(2,1)}), bf16[256,2,196]{2,1,0:T(2,128)(2,1)S(1)}, u32[]{:S(2)}, u32[]{:S(2)}) async-start(bf16[256,2,196]{2,1,0:T(2,128)(2,1)} %reshape.166), calls=%async_computation | async-start | bytes 524288 | tf_op jit(solution)/shard_map/all_to_all | solution.py:86
  24.6 4.1 %copy-start.1 = (f32[384]{0:T(512)S(1)}, f32[384]{0:T(512)}, u32[]{:S(2)}) copy-start(f32[384]{0:T(512)} %param.9) | copy-start | bytes 4612
  26.6 32.3 %collective-permute-start.3 = (f32[384,384]{1,0:T(8,128)S(1)}, f32[384,384]{1,0:T(8,128)}, u32[]{:S(2)}, u32[]{:S(2)}) collective-permute-start(f32[384,384]{1,0:T(8,128)S(1)} %get-tuple-element.7), channel_id=1, source_target_pairs={{0,4},{4,8},{8,12},{12,16},{16,20},{20,24},{24,28},{28,32},{32,36}... | collective-permute-start | bytes 1769480 | tf_op jit(solution)/shard_map/ppermute | solution.py:12
  31.7 5.3 %collective-permute-start.1 = (f32[8,384]{1,0:T(8,128)S(1)}, f32[8,384]{1,0:T(8,128)S(1)}, u32[]{:S(2)}, u32[]{:S(2)}) collective-permute-start(f32[8,384]{1,0:T(8,128)S(1)} %bitcast.77), channel_id=1, source_target_pairs={{0,2},{1,3},{2,0},{3,1},{4,6},{5,7},{6,4},{7,5},{8,10},{9,11},{10,... | collective-permute-start | bytes 36872 | tf_op jit(solution)/shard_map/ppermute | solution.py:18
  34.8 3.7 %collective-permute-start.2 = (f32[8,384]{1,0:T(8,128)S(1)}, f32[8,384]{1,0:T(8,128)S(1)}, u32[]{:S(2)}, u32[]{:S(2)}) collective-permute-start(f32[8,384]{1,0:T(8,128)S(1)} %bitcast.78), channel_id=1, source_target_pairs={{0,3},{1,0},{2,1},{3,2},{4,7},{5,4},{6,5},{7,6},{8,11},{9,8},{10,9... | collective-permute-start | bytes 36872 | tf_op jit(solution)/shard_map/ppermute | solution.py:18
  35.9 5.0 %collective-permute-start = (f32[8,384]{1,0:T(8,128)S(1)}, f32[8,384]{1,0:T(8,128)S(1)}, u32[]{:S(2)}, u32[]{:S(2)}) collective-permute-start(f32[8,384]{1,0:T(8,128)S(1)} %bitcast.79), channel_id=1, source_target_pairs={{0,1},{1,2},{2,3},{3,0},{4,5},{5,6},{6,7},{7,4},{8,9},{9,10},{10,1... | collective-permute-start | bytes 36872 | tf_op jit(solution)/shard_map/ppermute | solution.py:18
  50.4 8.2 %collective-permute-start.4 = (f32[384]{0:T(512)S(1)}, f32[384]{0:T(512)S(1)}, u32[]{:S(2)}, u32[]{:S(2)}) collective-permute-start(f32[384]{0:T(512)S(1)} %add_select_fusion), channel_id=1, source_target_pairs={{0,4},{4,8},{8,12},{12,16},{16,20},{20,24},{24,28},{28,32},{32,36}... | collective-permute-start | bytes 4616 | tf_op jit(solution)/shard_map/ppermute | solution.py:12
  60.7 16.8 %collective-permute-start.5 = (f32[385,384]{1,0:T(8,128)S(1)}, f32[385,384]{1,0:T(8,128)S(1)}, u32[]{:S(2)}, u32[]{:S(2)}) collective-permute-start(f32[385,384]{1,0:T(8,128)S(1)} %pad_maximum_fusion), channel_id=1, source_target_pairs={{0,8},{4,12},{8,16},{12,20},{16,24},{20,28},{24,32},{28,36},{32,40... | collective-permute-start | bytes 1774088 | tf_op jit(solution)/shard_map/ppermute | solution.py:12
  78.5 16.2 %collective-permute-start.6 = (f32[385,384]{1,0:T(8,128)S(1)}, f32[385,384]{1,0:T(8,128)S(1)}, u32[]{:S(2)}, u32[]{:S(2)}) collective-permute-start(f32[385,384]{1,0:T(8,128)S(1)} %pad_maximum_fusion.1), channel_id=1, source_target_pairs={{0,16},{4,20},{8,24},{12,28},{16,32},{20,36},{24,40},{28,44},{32,4... | collective-permute-start | bytes 1774088 | tf_op jit(solution)/shard_map/ppermute | solution.py:12
  95.6 13.3 %collective-permute-start.7 = (f32[385,384]{1,0:T(8,128)S(1)}, f32[385,384]{1,0:T(8,128)S(1)}, u32[]{:S(2)}, u32[]{:S(2)}) collective-permute-start(f32[385,384]{1,0:T(8,128)S(1)} %pad_maximum_fusion.2), channel_id=1, source_target_pairs={{0,32},{4,36},{8,40},{12,44},{16,48},{20,52},{24,56},{28,60},{32,6... | collective-permute-start | bytes 1774088 | tf_op jit(solution)/shard_map/ppermute | solution.py:12
  109.8 14.7 %collective-permute-start.8 = (f32[385,384]{1,0:T(8,128)S(1)}, f32[385,384]{1,0:T(8,128)S(1)}, u32[]{:S(2)}, u32[]{:S(2)}) collective-permute-start(f32[385,384]{1,0:T(8,128)S(1)} %pad_maximum_fusion.3), channel_id=1, source_target_pairs={{0,64},{4,68},{8,72},{12,76},{16,80},{20,84},{24,88},{28,92},{32,9... | collective-permute-start | bytes 1774088 | tf_op jit(solution)/shard_map/ppermute | solution.py:12
  125.4 29.2 %collective-permute-start.10 = (f32[385,384]{1,0:T(8,128)S(1)}, f32[385,384]{1,0:T(8,128)S(1)}, u32[]{:S(2)}, u32[]{:S(2)}) collective-permute-start(f32[385,384]{1,0:T(8,128)S(1)} %pad_maximum_fusion.4), channel_id=1, source_target_pairs={{0,4},{4,8},{8,12},{12,16},{16,20},{20,24},{24,28},{28,32},{32,36}... | collective-permute-start | bytes 1774088 | tf_op jit(solution)/shard_map/ppermute | solution.py:12
  127.3 0.7 collective-permute-start.9

commit v11 on v10

--- a/solution.py
+++ b/solution.py
@@ -9,6 +9,12 @@
 def passed_along(block, axis, distance):
     devices = range(lax.axis_size(axis))
     route = [(i - distance, i) for i in devices if i - distance in devices]
+    return lax.ppermute(block, axis, route)
+
+
+def sent_to_odd(block, axis, distance):
+    devices = range(lax.axis_size(axis))
+    route = [(i - distance, i) for i in devices if i % 2 == 1 and i - distance in devices]
     return lax.ppermute(block, axis, route)
 
 
@@ -102,21 +108,28 @@
 
     tm_index = lax.axis_index("tm")
     is_first = tm_index == 0
+    is_odd = tm_index % 2 == 1
     acc_vec = jnp.where(is_first, jnp.dot(prior_mean, slab_t, precision=precise) + offset, offset)
     acc_t = jnp.where(is_first, jnp.zeros_like(slab_t), slab_t)
-    got_t = passed_along(acc_t, "tm", 1)
-    acc_vec = jnp.dot(passed_along(acc_vec, "tm", 1), acc_t, precision=precise) + acc_vec
-    acc_t = jnp.dot(got_t, acc_t, precision=precise)
+    pair_t = sent_to_odd(acc_t, "tm", 1)
+    pair_vec = sent_to_odd(acc_vec, "tm", 1)
+    acc_vec = jnp.dot(pair_vec, acc_t, precision=precise) + acc_vec
+    acc_t = jnp.dot(pair_t, acc_t, precision=precise)
     distance = 2
     while distance * 2 < tm_count:
         carried = jnp.concatenate([acc_t, acc_vec[None]], axis=0)
-        got = jnp.dot(passed_along(carried, "tm", distance), acc_t, precision=precise)
+        got = jnp.dot(sent_to_odd(carried, "tm", distance), acc_t, precision=precise)
         acc_t = got[:state_width]
         acc_vec = got[state_width] + acc_vec
         distance *= 2
-    previous = passed_along(jnp.concatenate([acc_t, acc_vec[None]], axis=0), "tm", 1)
-    before_span = passed_along(acc_vec, "tm", distance + 1)
-    entering = jnp.dot(before_span, previous[:state_width], precision=precise) + previous[state_width]
+    acc_vec = jnp.dot(sent_to_odd(acc_vec, "tm", distance), acc_t, precision=precise) + acc_vec
+    to_even = lax.ppermute(
+        acc_vec, "tm", [(i - 1, i) for i in range(tm_count) if i % 2 == 0 and i >= 1]
+    )
+    to_odd = sent_to_odd(acc_vec, "tm", 2)
+    entering = jnp.where(
+        is_odd, jnp.dot(to_odd, pair_t, precision=precise) + pair_vec, to_even
+    )
     state = jnp.where(is_first, prior_mean, entering)
     return run_recurrence(trans, forcing, state)
 

time: 165 us -> 143 us (0.87); the launches traced: 162 us -> 142 us
  waiting for transfers between devices: 89.9 us -> 76.4 us
  starting transfers between devices: 33.4 us -> 27.7 us
    ppermute x8 -> x9, waiting for transfers between devices: 85.8 us -> 72.4 us  [the longest x1 71.6 us: on_device(): lax.ppermute(acc_vec, 'tm', [(i - 1, i) for i in range(tm_count) if i % 2...]
    ppermute x8 -> x9, starting transfers between devices: 14.4 us -> 8.77 us  [the longest x8 7.47 us: sent_to_odd(): return lax.ppermute(block, axis, route)]
    dot_general x7 -> x8, matrix products: 5.59 us -> 4.83 us  [the longest x4 3.26 us: on_device(): jnp.dot(sent_to_odd(carried, 'tm', distance), acc_t, precision=precise)]
  transfers between devices with their start and end apart: 12 -> 13, of which waited for: 9 -> 5; matrix products, arithmetic and copies ran while one was open for 9% -> 10% of each run, Pallas kernels for 4% -> 5%
where the time goes in v11:
time: 143 us; the launch traced here: 142 us
  waiting for transfers between devices  76.4 us (53%)
  starting transfers between devices  27.7 us (19%)
  matrix products  14.5 us (10%)
  Pallas kernels  13.9 us (10%)
  local copies, waits for them, and re-layouts  6.66 us (5%)
  other arithmetic  2.76 us (2%)
    ppermute x1, waiting for transfers between devices, on_device(): lax.ppermute(acc_vec, 'tm', [(i - 1, i) for i in range(tm_count) if i % 2...  71.6 us
    pallas_call x2, Pallas kernels, run_recurrence(): pl.pallas_call(recurrence_kernel, grid=(steps,), in_specs=[pl.BlockSpec((...  13.9 us
    all_to_all x1, starting transfers between devices, on_device(): lax.all_to_all(sent, ('tm', 'ingest'), split_axis=0, concat_axis=0, tiled...  13.8 us
    ppermute x8, starting transfers between devices, sent_to_odd(): return lax.ppermute(block, axis, route)  7.47 us
    dot_general x1, matrix products, on_device(): jnp.einsum('jba,jcb->jac', pairs[:, 0], pairs[:, 1], precision=precise)  6.36 us
    ppermute x3, starting transfers between devices, summed_over(): lax.ppermute(block, axis, [(i, (i + shift) % count) for i in range(count)])  5.11 us
    ppermute x3, waiting for transfers between devices, summed_over(): lax.ppermute(block, axis, [(i, (i + shift) % count) for i in range(count)])  4.03 us
    dot_general x4, matrix products, on_device(): jnp.dot(sent_to_odd(carried, 'tm', distance), acc_t, precision=precise)  3.26 us
  transfers between devices with their start and end apart: 13, of which 5 were waited for; matrix products, arithmetic and copies ran while one was open for 10% of the time, Pallas kernels for 5%

profile of v11, /device:TPU:128, one launch (start us, length us, event | category | flops | bytes accessed | tf_op | source)
XLA Modules:
  0.0 142.5 jit_solution(1522553659882435673)
XLA Ops:
  0.0 1.0 multiply_convert_fusion
  2.7 0.8 reduce.18
  3.5 0.9 reshape.168
  4.4 13.8 %all-to-all-start = ((bf16[256,2,196]{2,1,0:T(2,128)(2,1)}), bf16[256,2,196]{2,1,0:T(2,128)(2,1)S(1)}, u32[]{:S(2)}, u32[]{:S(2)}) async-start(bf16[256,2,196]{2,1,0:T(2,128)(2,1)} %reshape.168), calls=%async_computation | async-start | bytes 524288 | tf_op jit(solution)/shard_map/all_to_all | solution.py:92
  18.2 6.4 %fusion = f32[4,384,384]{2,1,0:T(8,128)S(1)} fusion(f32[4,2,384,384]{3,2,1,0:T(8,128)} %bitcast.73), kind=kOutput, calls=%fused_computation.2 | convolution fusion | flops 1358954496 | bytes 7077888 | tf_op jit(solution)/shard_map/jba,jcb->jac/dot_general | solution.py:102
  24.6 1.3 convolution_bitcast_fusion
  25.9 0.7 broadcast_select_fusion
  26.6 2.1 %collective-permute-start.3 = (f32[384,384]{1,0:T(8,128)S(1)}, f32[384,384]{1,0:T(8,128)S(1)}, u32[]{:S(2)}, u32[]{:S(2)}) collective-permute-start(f32[384,384]{1,0:T(8,128)S(1)} %get-tuple-element.7), channel_id=1, source_target_pairs={{0,4},{8,12},{16,20},{24,28},{32,36},{40,44},{48,52},{56,60},{64,6... | collective-permute-start | bytes 1769480 | tf_op jit(solution)/shard_map/ppermute | solution.py:18
  30.7 0.7 fusion.1
  31.7 3.1 %collective-permute-start.1 = (f32[8,384]{1,0:T(8,128)S(1)}, f32[8,384]{1,0:T(8,128)S(1)}, u32[]{:S(2)}, u32[]{:S(2)}) collective-permute-start(f32[8,384]{1,0:T(8,128)S(1)} %bitcast.79), channel_id=1, source_target_pairs={{0,2},{1,3},{2,0},{3,1},{4,6},{5,7},{6,4},{7,5},{8,10},{9,11},{10,... | collective-permute-start | bytes 36872 | tf_op jit(solution)/shard_map/ppermute | solution.py:24
  34.8 1.2 collective-permute-start.2
  36.0 0.9 collective-permute-start
  37.0 1.5 %collective-permute-done.2 = f32[8,384]{1,0:T(8,128)S(1)} collective-permute-done((f32[8,384]{1,0:T(8,128)S(1)}, f32[8,384]{1,0:T(8,128)S(1)}, u32[]{:S(2)}, u32[]{:S(2)}) %collective-permute-start.2) | collective-permute-done | bytes 12320 | tf_op jit(solution)/shard_map/ppermute | solution.py:24
  38.5 2.4 %collective-permute-done = f32[8,384]{1,0:T(8,128)S(1)} collective-permute-done((f32[8,384]{1,0:T(8,128)S(1)}, f32[8,384]{1,0:T(8,128)S(1)}, u32[]{:S(2)}, u32[]{:S(2)}) %collective-permute-start) | collective-permute-done | bytes 12320 | tf_op jit(solution)/shard_map/ppermute | solution.py:24
  42.6 6.9 %shard_map.73 = f32[8,384]{1,0:T(8,128)} custom-call(f32[8,384,384]{2,1,0:T(8,128)} %map_ref.3, f32[8,384]{1,0:T(8,128)} %fusion.5.force_ref, f32[1,384]{1,0:T(1,128)} %reshape.138.start_ref), custom_call_target="tpu_custom_call" | custom-call | tf_op jit(solution)/shard_map/pallas_call | solution.py:55
  49.6 0.7 slice_reduce_fusion.4
  50.3 1.3 collective-permute-start.4
  51.6 0.8 collective-permute-done.4
  52.7 0.7 fusion.15
  53.5 0.7 collective-permute-start.5
  54.2 0.8 fusion.16
  55.1 0.7 collective-permute-start.6
  55.9 0.8 fusion.12
  56.8 0.7 collective-permute-start.7
  57.5 0.8 fusion.10
  58.5 0.7 collective-permute-start.8
  59.2 0.8 fusion.8
  60.1 0.7 collective-permute-start.9
  61.1 0.7 collective-permute-start.10
  61.7 1.3 collective-permute-start.11
  63.4 71.6 %collective-permute-done.11 = f32[384]{0:T(512)S(1)} collective-permute-done((f32[384]{0:T(512)S(1)}, f32[384]{0:T(512)S(1)}, u32[]{:S(2)}, u32[]{:S(2)}) %collective-permute-start.11) | collective-permute-done | bytes 1568 | tf_op jit(solution)/shard_map/ppermute | solution.py:126
  135.5 6.9 %shard_map.74 = f32[8,384]{1,0:T(8,128)} custom-call(f32[8,384,384]{2,1,0:T(8,128)} %map_ref.3, f32[8,384]{1,0:T(8,128)} %fusion.5.force_ref, f32[1,384]{1,0:T(1,128)} %reshape.139.start_ref), custom_call_target="tpu_custom_call" | custom-call | tf_op jit(solution)/shard_map/pallas_call | solution.py:55
  (74 shorter events, 7.7 us)
Async XLA Ops:
  0.0 31.4 %copy-start = (f32[8,384,48]{1,2,0:T(8,128)S(1)}, f32[8,384,48]{1,2,0:T(8,128)}, u32[]{:S(2)}) copy-start(f32[8,384,48]{1,2,0:T(8,128)} %param.8) | copy-start | bytes 1769476
  0.0 1.9 %copy-start.2 = (s32[512]{0:T(512)S(1)}, s32[512]{0:T(512)}, u32[]{:S(2)}) copy-start(s32[512]{0:T(512)} %param.12) | copy-start | bytes 6148
  0.0 2.0 %copy-start.3 = (s32[1,64]{1,0:T(1,128)S(1)}, s32[1,64]{1,0:T(1,128)}, u32[]{:S(2)}) copy-start(s32[1,64]{1,0:T(1,128)} %param.13) | copy-start | bytes 772
  4.4 24.7 %all-to-all-start = ((bf16[256,2,196]{2,1,0:T(2,128)(2,1)}), bf16[256,2,196]{2,1,0:T(2,128)(2,1)S(1)}, u32[]{:S(2)}, u32[]{:S(2)}) async-start(bf16[256,2,196]{2,1,0:T(2,128)(2,1)} %reshape.168), calls=%async_computation | async-start | bytes 524288 | tf_op jit(solution)/shard_map/all_to_all | solution.py:92
  24.6 4.1 %copy-start.1 = (f32[384]{0:T(512)S(1)}, f32[384]{0:T(512)}, u32[]{:S(2)}) copy-start(f32[384]{0:T(512)} %param.9) | copy-start | bytes 4612
  26.6 26.1 %collective-permute-start.3 = (f32[384,384]{1,0:T(8,128)S(1)}, f32[384,384]{1,0:T(8,128)S(1)}, u32[]{:S(2)}, u32[]{:S(2)}) collective-permute-start(f32[384,384]{1,0:T(8,128)S(1)} %get-tuple-element.7), channel_id=1, source_target_pairs={{0,4},{8,12},{16,20},{24,28},{32,36},{40,44},{48,52},{56,60},{64,6... | collective-permute-start | bytes 1769480 | tf_op jit(solution)/shard_map/ppermute | solution.py:18
  31.7 5.3 %collective-permute-start.1 = (f32[8,384]{1,0:T(8,128)S(1)}, f32[8,384]{1,0:T(8,128)S(1)}, u32[]{:S(2)}, u32[]{:S(2)}) collective-permute-start(f32[8,384]{1,0:T(8,128)S(1)} %bitcast.79), channel_id=1, source_target_pairs={{0,2},{1,3},{2,0},{3,1},{4,6},{5,7},{6,4},{7,5},{8,10},{9,11},{10,... | collective-permute-start | bytes 36872 | tf_op jit(solution)/shard_map/ppermute | solution.py:24
  34.8 3.7 %collective-permute-start.2 = (f32[8,384]{1,0:T(8,128)S(1)}, f32[8,384]{1,0:T(8,128)S(1)}, u32[]{:S(2)}, u32[]{:S(2)}) collective-permute-start(f32[8,384]{1,0:T(8,128)S(1)} %bitcast.80), channel_id=1, source_target_pairs={{0,3},{1,0},{2,1},{3,2},{4,7},{5,4},{6,5},{7,6},{8,11},{9,8},{10,9... | collective-permute-start | bytes 36872 | tf_op jit(solution)/shard_map/ppermute | solution.py:24
  36.0 4.9 %collective-permute-start = (f32[8,384]{1,0:T(8,128)S(1)}, f32[8,384]{1,0:T(8,128)S(1)}, u32[]{:S(2)}, u32[]{:S(2)}) collective-permute-start(f32[8,384]{1,0:T(8,128)S(1)} %bitcast.81), channel_id=1, source_target_pairs={{0,1},{1,2},{2,3},{3,0},{4,5},{5,6},{6,7},{7,4},{8,9},{9,10},{10,1... | collective-permute-start | bytes 36872 | tf_op jit(solution)/shard_map/ppermute | solution.py:24
  50.3 2.1 %collective-permute-start.4 = (f32[384]{0:T(512)S(1)}, f32[384]{0:T(512)S(1)}, u32[]{:S(2)}, u32[]{:S(2)}) collective-permute-start(f32[384]{0:T(512)S(1)} %add_select_fusion), channel_id=1, source_target_pairs={{0,4},{8,12},{16,20},{24,28},{32,36},{40,44},{48,52},{56,60},{64,6... | collective-permute-start | bytes 4616 | tf_op jit(solution)/shard_map/ppermute | solution.py:18
  53.5 0.7 collective-permute-start.5
  55.1 0.7 collective-permute-start.6
  56.8 0.7 collective-permute-start.7
  58.5 0.7 collective-permute-start.8
  60.1 0.7 collective-permute-start.9
  61.1 2.0 %collective-permute-start.10 = (f32[384]{0:T(512)S(1)}, f32[384]{0:T(512)S(1)}, u32[]{:S(2)}, u32[]{:S(2)}) collective-permute-start(f32[384]{0:T(512)S(1)} %add.77), channel_id=1, source_target_pairs={{4,12},{12,20},{20,28},{28,36},{36,44},{44,52},{52,60},{60,68},{68... | collective-permute-start | bytes 4616 | tf_op jit(solution)/shard_map/ppermute | solution.py:18
  61.7 73.2 %collective-permute-start.11 = (f32[384]{0:T(512)S(1)}, f32[384]{0:T(512)S(1)}, u32[]{:S(2)}, u32[]{:S(2)}) collective-permute-start(f32[384]{0:T(512)S(1)} %add.77), channel_id=1, source_target_pairs={{4,8},{12,16},{20,24},{28,32},{36,40},{44,48},{52,56},{60,64},{68,... | collective-permute-start | bytes 4616 | tf_op jit(solution)/shard_map/ppermute | solution.py:126

commit v12 on v11

--- a/solution.py
+++ b/solution.py
@@ -90,6 +90,21 @@
     ).reshape(tm_count * in_count, group_rows)
     sent = jnp.concatenate([pieces, marks], axis=1)
     got = lax.all_to_all(sent, ("tm", "ingest"), split_axis=0, concat_axis=0, tiled=True)
+    pairs = trans.reshape(steps_here // 2, 2, state_width, state_width)
+    level_t = jnp.einsum("jba,jcb->jac", pairs[:, 0], pairs[:, 1], precision=precise)
+    while level_t.shape[0] > 1:
+        map_pairs = level_t.reshape(-1, 2, state_width, state_width)
+        level_t = jnp.einsum("jab,jbc->jac", map_pairs[:, 0], map_pairs[:, 1], precision=precise)
+    slab_t = level_t[0]
+    tm_index = lax.axis_index("tm")
+    is_first = tm_index == 0
+    is_odd = tm_index % 2 == 1
+    slab_first = jnp.where(is_first, jnp.zeros_like(slab_t), slab_t)
+    pair_t = sent_to_odd(slab_first, "tm", 1)
+    joined_t = jnp.dot(pair_t, slab_first, precision=precise)
+    got_t = sent_to_odd(joined_t, "tm", 2)
+    got, joined_t = lax.optimization_barrier((got, joined_t))
+    acc_t = jnp.dot(got_t, joined_t, precision=precise)
     got_rows = got[:, : group_rows * piece_width].reshape(-1, piece_width)
     got_marks = got[:, group_rows * piece_width :].reshape(-1).astype(jnp.int32)
     step_ids = lax.broadcasted_iota(jnp.int32, (1, steps_here), 1)
@@ -98,24 +113,13 @@
     partial_force = jnp.einsum("lsq,lq->ls", gain, drive_piece, precision=precise)
     forcing = summed_over(partial_force, "ingest")
 
-    pairs = trans.reshape(steps_here // 2, 2, state_width, state_width)
-    level_t = jnp.einsum("jba,jcb->jac", pairs[:, 0], pairs[:, 1], precision=precise)
-    while level_t.shape[0] > 1:
-        map_pairs = level_t.reshape(-1, 2, state_width, state_width)
-        level_t = jnp.einsum("jab,jbc->jac", map_pairs[:, 0], map_pairs[:, 1], precision=precise)
-    slab_t = level_t[0]
     offset = run_recurrence(trans, forcing, jnp.zeros((state_width,), jnp.float32))[-1]
 
-    tm_index = lax.axis_index("tm")
-    is_first = tm_index == 0
-    is_odd = tm_index % 2 == 1
     acc_vec = jnp.where(is_first, jnp.dot(prior_mean, slab_t, precision=precise) + offset, offset)
-    acc_t = jnp.where(is_first, jnp.zeros_like(slab_t), slab_t)
-    pair_t = sent_to_odd(acc_t, "tm", 1)
     pair_vec = sent_to_odd(acc_vec, "tm", 1)
-    acc_vec = jnp.dot(pair_vec, acc_t, precision=precise) + acc_vec
-    acc_t = jnp.dot(pair_t, acc_t, precision=precise)
-    distance = 2
+    acc_vec = jnp.dot(pair_vec, slab_first, precision=precise) + acc_vec
+    acc_vec = jnp.dot(sent_to_odd(acc_vec, "tm", 2), joined_t, precision=precise) + acc_vec
+    distance = 4
     while distance * 2 < tm_count:
         carried = jnp.concatenate([acc_t, acc_vec[None]], axis=0)
         got = jnp.dot(sent_to_odd(carried, "tm", distance), acc_t, precision=precise)

time: 143 us -> 143 us (level)
  waiting for transfers between devices: 76.4 us -> 78.2 us
    all_to_all x1, waiting for transfers between devices: 0.01 us -> 10.1 us  [on_device(): lax.all_to_all(sent, ('tm', 'ingest'), split_axis=0, concat_axis=0, tiled...]
    ppermute x1, waiting for transfers between devices: 71.6 us -> 65.1 us  [on_device(): lax.ppermute(acc_vec, 'tm', [(i - 1, i) for i in range(tm_count) if i % 2...]
    ppermute x3, waiting for transfers between devices: 4.03 us -> 2.13 us  [summed_over(): lax.ppermute(block, axis, [(i, (i + shift) % count) for i in range(count)])]
    ppermute x3, starting transfers between devices: 5.11 us -> 3.62 us  [summed_over(): lax.ppermute(block, axis, [(i, (i + shift) % count) for i in range(count)])]
    dot_general x4 -> x3, matrix products: 3.26 us -> 2.43 us  [on_device(): jnp.dot(sent_to_odd(carried, 'tm', distance), acc_t, precision=precise)]
    ppermute x8 -> x9, starting transfers between devices: 7.47 us -> 7.83 us  [sent_to_odd(): return lax.ppermute(block, axis, route)]
  transfers between devices with their start and end apart: 13 -> 14, of which waited for: 5 -> 6; matrix products, arithmetic and copies ran while one was open for 10% -> 5% of each run, Pallas kernels for 5% -> 5%
where the time goes in v12:
time: 143 us; the launch traced here: 142 us
  waiting for transfers between devices  78.2 us (55%)
  starting transfers between devices  26.6 us (19%)
  matrix products  14.7 us (10%)
  Pallas kernels  13.9 us (10%)
  local copies, waits for them, and re-layouts  6.61 us (5%)
  other arithmetic  1.73 us (1%)
    ppermute x1, waiting for transfers between devices, on_device(): lax.ppermute(acc_vec, 'tm', [(i - 1, i) for i in range(tm_count) if i % 2...  65.1 us
    pallas_call x2, Pallas kernels, run_recurrence(): pl.pallas_call(recurrence_kernel, grid=(steps,), in_specs=[pl.BlockSpec((...  13.9 us
    all_to_all x1, starting transfers between devices, on_device(): lax.all_to_all(sent, ('tm', 'ingest'), split_axis=0, concat_axis=0, tiled...  13.8 us
    all_to_all x1, waiting for transfers between devices, on_device(): lax.all_to_all(sent, ('tm', 'ingest'), split_axis=0, concat_axis=0, tiled...  10.1 us
    ppermute x9, starting transfers between devices, sent_to_odd(): return lax.ppermute(block, axis, route)  7.83 us
    dot_general x1, matrix products, on_device(): jnp.einsum('jba,jcb->jac', pairs[:, 0], pairs[:, 1], precision=precise)  6.42 us
    ppermute x3, starting transfers between devices, summed_over(): lax.ppermute(block, axis, [(i, (i + shift) % count) for i in range(count)])  3.62 us
  transfers between devices with their start and end apart: 14, of which 6 were waited for; matrix products, arithmetic and copies ran while one was open for 5% of the time, Pallas kernels for 5%

profile of v12, /device:TPU:128, one launch (start us, length us, event | category | flops | bytes accessed | tf_op | source)
XLA Modules:
  0.0 142.3 jit_solution(16006640151991844134)
XLA Ops:
  0.0 6.4 %fusion = f32[4,384,384]{2,1,0:T(8,128)S(1)} fusion(f32[4,2,384,384]{3,2,1,0:T(8,128)} %bitcast.76), kind=kOutput, calls=%fused_computation.2 | convolution fusion | flops 1358954496 | bytes 7077888 | tf_op jit(solution)/shard_map/jba,jcb->jac/dot_general | solution.py:94
  6.5 1.3 convolution_bitcast_fusion
  7.8 0.7 broadcast_select_fusion
  8.5 1.8 %collective-permute-start = (f32[384,384]{1,0:T(8,128)S(1)}, f32[384,384]{1,0:T(8,128)S(1)}, u32[]{:S(2)}, u32[]{:S(2)}) collective-permute-start(f32[384,384]{1,0:T(8,128)S(1)} %get-tuple-element.11), channel_id=1, source_target_pairs={{0,4},{8,12},{16,20},{24,28},{32,36},{40,44},{48,52},{56,60},{64,6... | collective-permute-start | bytes 1769480 | tf_op jit(solution)/shard_map/ppermute | solution.py:18
  12.0 0.8 reduce.18
  12.8 0.9 reshape.170
  13.7 13.8 %all-to-all-start = ((bf16[256,2,196]{2,1,0:T(2,128)(2,1)}), bf16[256,2,196]{2,1,0:T(2,128)(2,1)S(1)}, u32[]{:S(2)}, u32[]{:S(2)}) async-start(bf16[256,2,196]{2,1,0:T(2,128)(2,1)} %reshape.170), calls=%async_computation | async-start | bytes 524288 | tf_op jit(solution)/shard_map/all_to_all | solution.py:92
  27.9 10.1 %all-to-all-done = bf16[256,2,196]{2,1,0:T(2,128)(2,1)S(1)} async-done(((bf16[256,2,196]{2,1,0:T(2,128)(2,1)}), bf16[256,2,196]{2,1,0:T(2,128)(2,1)S(1)}, u32[]{:S(2)}, u32[]{:S(2)}) %all-to-all-start) | async-done | bytes 200736 | tf_op jit(solution)/shard_map/all_to_all | solution.py:92
  38.7 0.7 fusion.12
  40.3 0.7 fusion.1
  41.3 0.7 collective-permute-start.1
  42.0 2.1 %collective-permute-start.2 = (f32[8,384]{1,0:T(8,128)S(1)}, f32[8,384]{1,0:T(8,128)S(1)}, u32[]{:S(2)}, u32[]{:S(2)}) collective-permute-start(f32[8,384]{1,0:T(8,128)S(1)} %bitcast.83), channel_id=1, source_target_pairs={{0,2},{1,3},{2,0},{3,1},{4,6},{5,7},{6,4},{7,5},{8,10},{9,11},{10,... | collective-permute-start | bytes 36872 | tf_op jit(solution)/shard_map/ppermute | solution.py:24
  44.1 0.9 collective-permute-start.3
  45.0 0.7 collective-permute-start.4
  46.3 0.9 collective-permute-done.2
  49.6 6.9 %shard_map.73 = f32[8,384]{1,0:T(8,128)} custom-call(f32[8,384,384]{2,1,0:T(8,128)} %map_ref.3, f32[8,384]{1,0:T(8,128)} %fusion.5.force_ref, f32[1,384]{1,0:T(1,128)} %reshape.138.start_ref), custom_call_target="tpu_custom_call" | custom-call | tf_op jit(solution)/shard_map/pallas_call | solution.py:55
  56.5 0.7 slice_reduce_fusion.3
  57.2 1.3 collective-permute-start.5
  58.5 0.8 collective-permute-done.5
  59.6 0.7 collective-permute-start.6
  60.6 0.7 fusion.14
  61.4 0.7 collective-permute-start.7
  62.1 0.8 fusion.15
  63.1 0.7 collective-permute-start.8
  63.8 0.8 fusion.10
  64.7 0.7 collective-permute-start.9
  65.5 0.8 fusion.8
  66.3 0.7 collective-permute-start.10
  67.3 0.7 collective-permute-start.11
  68.0 1.3 collective-permute-start.12
  69.6 65.1 %collective-permute-done.12 = f32[384]{0:T(512)S(1)} collective-permute-done((f32[384]{0:T(512)S(1)}, f32[384]{0:T(512)S(1)}, u32[]{:S(2)}, u32[]{:S(2)}) %collective-permute-start.12) | collective-permute-done | bytes 1568 | tf_op jit(solution)/shard_map/ppermute | solution.py:130
  135.3 6.9 %shard_map.74 = f32[8,384]{1,0:T(8,128)} custom-call(f32[8,384,384]{2,1,0:T(8,128)} %map_ref.3, f32[8,384]{1,0:T(8,128)} %fusion.5.force_ref, f32[1,384]{1,0:T(1,128)} %reshape.139.start_ref), custom_call_target="tpu_custom_call" | custom-call | tf_op jit(solution)/shard_map/pallas_call | solution.py:55
  (78 shorter events, 9.0 us)
Async XLA Ops:
  0.0 41.0 %copy-start = (f32[8,384,48]{1,2,0:T(8,128)S(1)}, f32[8,384,48]{1,2,0:T(8,128)}, u32[]{:S(2)}) copy-start(f32[8,384,48]{1,2,0:T(8,128)} %param.8) | copy-start | bytes 1769476
  6.4 3.9 %copy-start.4 = (s32[512]{0:T(512)S(1)}, s32[512]{0:T(512)}, u32[]{:S(2)}) copy-start(s32[512]{0:T(512)} %param.12) | copy-start | bytes 6148
  6.4 4.0 %copy-start.1 = (bf16[512,192]{0,1:T(8,128)(2,1)S(1)}, bf16[512,192]{0,1:T(8,128)(2,1)}, u32[]{:S(2)}) copy-start(bf16[512,192]{0,1:T(8,128)(2,1)} %param.10) | copy-start | bytes 589828
  6.5 4.0 %copy-start.3 = (f32[512]{0:T(512)S(1)}, f32[512]{0:T(512)}, u32[]{:S(2)}) copy-start(f32[512]{0:T(512)} %param.11) | copy-start | bytes 6148
  6.5 4.0 %copy-start.5 = (s32[1,64]{1,0:T(1,128)S(1)}, s32[1,64]{1,0:T(1,128)}, u32[]{:S(2)}) copy-start(s32[1,64]{1,0:T(1,128)} %param.13) | copy-start | bytes 772
  8.5 30.2 %collective-permute-start = (f32[384,384]{1,0:T(8,128)S(1)}, f32[384,384]{1,0:T(8,128)S(1)}, u32[]{:S(2)}, u32[]{:S(2)}) collective-permute-start(f32[384,384]{1,0:T(8,128)S(1)} %get-tuple-element.11), channel_id=1, source_target_pairs={{0,4},{8,12},{16,20},{24,28},{32,36},{40,44},{48,52},{56,60},{64,6... | collective-permute-start | bytes 1769480 | tf_op jit(solution)/shard_map/ppermute | solution.py:18
  10.7 16.9 %copy-start.2 = (f32[384]{0:T(512)S(1)}, f32[384]{0:T(512)}, u32[]{:S(2)}) copy-start(f32[384]{0:T(512)} %param.9) | copy-start | bytes 4612
  13.7 24.3 %all-to-all-start = ((bf16[256,2,196]{2,1,0:T(2,128)(2,1)}), bf16[256,2,196]{2,1,0:T(2,128)(2,1)S(1)}, u32[]{:S(2)}, u32[]{:S(2)}) async-start(bf16[256,2,196]{2,1,0:T(2,128)(2,1)} %reshape.170), calls=%async_computation | async-start | bytes 524288 | tf_op jit(solution)/shard_map/all_to_all | solution.py:92
  41.3 5.0 %collective-permute-start.1 = (f32[8,384]{1,0:T(8,128)S(1)}, f32[8,384]{1,0:T(8,128)S(1)}, u32[]{:S(2)}, u32[]{:S(2)}) collective-permute-start(f32[8,384]{1,0:T(8,128)S(1)} %bitcast.82), channel_id=1, source_target_pairs={{0,1},{1,2},{2,3},{3,0},{4,5},{5,6},{6,7},{7,4},{8,9},{9,10},{10,1... | collective-permute-start | bytes 36872 | tf_op jit(solution)/shard_map/ppermute | solution.py:24
  42.0 5.2 %collective-permute-start.2 = (f32[8,384]{1,0:T(8,128)S(1)}, f32[8,384]{1,0:T(8,128)S(1)}, u32[]{:S(2)}, u32[]{:S(2)}) collective-permute-start(f32[8,384]{1,0:T(8,128)S(1)} %bitcast.83), channel_id=1, source_target_pairs={{0,2},{1,3},{2,0},{3,1},{4,6},{5,7},{6,4},{7,5},{8,10},{9,11},{10,... | collective-permute-start | bytes 36872 | tf_op jit(solution)/shard_map/ppermute | solution.py:24
  44.1 3.7 %collective-permute-start.3 = (f32[8,384]{1,0:T(8,128)S(1)}, f32[8,384]{1,0:T(8,128)S(1)}, u32[]{:S(2)}, u32[]{:S(2)}) collective-permute-start(f32[8,384]{1,0:T(8,128)S(1)} %bitcast.84), channel_id=1, source_target_pairs={{0,3},{1,0},{2,1},{3,2},{4,7},{5,4},{6,5},{7,6},{8,11},{9,8},{10,9... | collective-permute-start | bytes 36872 | tf_op jit(solution)/shard_map/ppermute | solution.py:24
  45.0 15.7 %collective-permute-start.4 = (f32[384,384]{1,0:T(8,128)S(1)}, f32[384,384]{1,0:T(8,128)S(1)}, u32[]{:S(2)}, u32[]{:S(2)}) collective-permute-start(f32[384,384]{1,0:T(8,128)S(1)} %fusion.12), channel_id=1, source_target_pairs={{4,12},{12,20},{20,28},{28,36},{36,44},{44,52},{52,60},{60,68},{68... | collective-permute-start | bytes 1769480 | tf_op jit(solution)/shard_map/ppermute | solution.py:18
  57.2 2.1 %collective-permute-start.5 = (f32[384]{0:T(512)S(1)}, f32[384]{0:T(512)S(1)}, u32[]{:S(2)}, u32[]{:S(2)}) collective-permute-start(f32[384]{0:T(512)S(1)} %add_select_fusion), channel_id=1, source_target_pairs={{0,4},{8,12},{16,20},{24,28},{32,36},{40,44},{48,52},{56,60},{64,6... | collective-permute-start | bytes 4616 | tf_op jit(solution)/shard_map/ppermute | solution.py:18
  59.6 0.7 collective-permute-start.6
  61.4 0.7 collective-permute-start.7
  63.1 0.7 collective-permute-start.8
  64.7 0.7 collective-permute-start.9
  66.3 0.7 collective-permute-start.10
  67.3 2.0 %collective-permute-start.11 = (f32[384]{0:T(512)S(1)}, f32[384]{0:T(512)S(1)}, u32[]{:S(2)}, u32[]{:S(2)}) collective-permute-start(f32[384]{0:T(512)S(1)} %add.77), channel_id=1, source_target_pairs={{4,12},{12,20},{20,28},{28,36},{36,44},{44,52},{52,60},{60,68},{68... | collective-permute-start | bytes 4616 | tf_op jit(solution)/shard_map/ppermute | solution.py:18
  68.0 66.8 %collective-permute-start.12 = (f32[384]{0:T(512)S(1)}, f32[384]{0:T(512)S(1)}, u32[]{:S(2)}, u32[]{:S(2)}) collective-permute-start(f32[384]{0:T(512)S(1)} %add.77), channel_id=1, source_target_pairs={{4,8},{12,16},{20,24},{28,32},{36,40},{44,48},{52,56},{60,64},{68,... | collective-permute-start | bytes 4616 | tf_op jit(solution)/shard_map/ppermute | solution.py:130

commit v13 on v12

--- a/solution.py
+++ b/solution.py
@@ -103,7 +103,6 @@
     pair_t = sent_to_odd(slab_first, "tm", 1)
     joined_t = jnp.dot(pair_t, slab_first, precision=precise)
     got_t = sent_to_odd(joined_t, "tm", 2)
-    got, joined_t = lax.optimization_barrier((got, joined_t))
     acc_t = jnp.dot(got_t, joined_t, precision=precise)
     got_rows = got[:, : group_rows * piece_width].reshape(-1, piece_width)
     got_marks = got[:, group_rows * piece_width :].reshape(-1).astype(jnp.int32)
@@ -111,6 +110,7 @@
     onehot = (got_marks[:, None] == step_ids).astype(jnp.bfloat16)
     drive_piece = jnp.einsum("rl,rq->lq", onehot, got_rows, preferred_element_type=jnp.float32)
     partial_force = jnp.einsum("lsq,lq->ls", gain, drive_piece, precision=precise)
+    partial_force, joined_t = lax.optimization_barrier((partial_force, joined_t))
     forcing = summed_over(partial_force, "ingest")
 
     offset = run_recurrence(trans, forcing, jnp.zeros((state_width,), jnp.float32))[-1]

time: 143 us -> 136 us (0.951)
  waiting for transfers between devices: 78.2 us -> 67.5 us
  starting transfers between devices: 26.6 us -> 29 us
    all_to_all x1, waiting for transfers between devices: 10.1 us -> 0.01 us  [on_device(): lax.all_to_all(sent, ('tm', 'ingest'), split_axis=0, concat_axis=0, tiled...]
    ppermute x3, starting transfers between devices: 3.62 us -> 5.71 us  [summed_over(): lax.ppermute(block, axis, [(i, (i + shift) % count) for i in range(count)])]
  transfers between devices with their start and end apart: 14 -> 14, of which waited for: 6 -> 4; matrix products, arithmetic and copies ran while one was open for 5% -> 11% of each run, Pallas kernels for 5% -> 5%
where the time goes in v13:
time: 136 us; the launch traced here: 135 us
  waiting for transfers between devices  67.5 us (50%)
  starting transfers between devices  29 us (21%)
  matrix products  14.7 us (11%)
  Pallas kernels  13.9 us (10%)
  local copies, waits for them, and re-layouts  6.6 us (5%)
  other arithmetic  2.72 us (2%)
    ppermute x1, waiting for transfers between devices, on_device(): lax.ppermute(acc_vec, 'tm', [(i - 1, i) for i in range(tm_count) if i % 2...  65.2 us
    pallas_call x2, Pallas kernels, run_recurrence(): pl.pallas_call(recurrence_kernel, grid=(steps,), in_specs=[pl.BlockSpec((...  13.9 us
    all_to_all x1, starting transfers between devices, on_device(): lax.all_to_all(sent, ('tm', 'ingest'), split_axis=0, concat_axis=0, tiled...  13.8 us
    ppermute x9, starting transfers between devices, sent_to_odd(): return lax.ppermute(block, axis, route)  8.2 us
    dot_general x1, matrix products, on_device(): jnp.einsum('jba,jcb->jac', pairs[:, 0], pairs[:, 1], precision=precise)  6.36 us
    ppermute x3, starting transfers between devices, summed_over(): lax.ppermute(block, axis, [(i, (i + shift) % count) for i in range(count)])  5.71 us
  transfers between devices with their start and end apart: 14, of which 4 were waited for; matrix products, arithmetic and copies ran while one was open for 11% of the time, Pallas kernels for 5%

profile of v13, /device:TPU:128, one launch (start us, length us, event | category | flops | bytes accessed | tf_op | source)
XLA Modules:
  0.0 135.0 jit_solution(2284659316328088850)
XLA Ops:
  0.0 1.0 multiply_convert_fusion
  2.7 0.8 reduce.18
  3.5 0.9 reshape.170
  4.4 13.8 %all-to-all-start = ((bf16[256,2,196]{2,1,0:T(2,128)(2,1)}), bf16[256,2,196]{2,1,0:T(2,128)(2,1)S(1)}, u32[]{:S(2)}, u32[]{:S(2)}) async-start(bf16[256,2,196]{2,1,0:T(2,128)(2,1)} %reshape.170), calls=%async_computation | async-start | bytes 524288 | tf_op jit(solution)/shard_map/all_to_all | solution.py:92
  18.2 6.4 %fusion = f32[4,384,384]{2,1,0:T(8,128)S(1)} fusion(f32[4,2,384,384]{3,2,1,0:T(8,128)} %bitcast.75), kind=kOutput, calls=%fused_computation.2 | convolution fusion | flops 1358954496 | bytes 7077888 | tf_op jit(solution)/shard_map/jba,jcb->jac/dot_general | solution.py:94
  24.6 1.3 convolution_bitcast_fusion
  25.9 0.7 broadcast_select_fusion
  26.6 2.1 %collective-permute-start = (f32[384,384]{1,0:T(8,128)S(1)}, f32[384,384]{1,0:T(8,128)S(1)}, u32[]{:S(2)}, u32[]{:S(2)}) collective-permute-start(f32[384,384]{1,0:T(8,128)S(1)} %get-tuple-element.9), channel_id=1, source_target_pairs={{0,4},{8,12},{16,20},{24,28},{32,36},{40,44},{48,52},{56,60},{64,6... | collective-permute-start | bytes 1769480 | tf_op jit(solution)/shard_map/ppermute | solution.py:18
  30.7 0.7 fusion.1
  31.7 0.7 fusion.13
  32.4 1.6 %collective-permute-start.1 = (f32[8,384]{1,0:T(8,128)S(1)}, f32[8,384]{1,0:T(8,128)S(1)}, u32[]{:S(2)}, u32[]{:S(2)}) collective-permute-start(f32[8,384]{1,0:T(8,128)S(1)} %bitcast.81), channel_id=1, source_target_pairs={{0,1},{1,2},{2,3},{3,0},{4,5},{5,6},{6,7},{7,4},{8,9},{9,10},{10,1... | collective-permute-start | bytes 36872 | tf_op jit(solution)/shard_map/ppermute | solution.py:24
  34.0 2.7 %collective-permute-start.2 = (f32[8,384]{1,0:T(8,128)S(1)}, f32[8,384]{1,0:T(8,128)S(1)}, u32[]{:S(2)}, u32[]{:S(2)}) collective-permute-start(f32[8,384]{1,0:T(8,128)S(1)} %bitcast.82), channel_id=1, source_target_pairs={{0,2},{1,3},{2,0},{3,1},{4,6},{5,7},{6,4},{7,5},{8,10},{9,11},{10,... | collective-permute-start | bytes 36872 | tf_op jit(solution)/shard_map/ppermute | solution.py:24
  36.7 1.4 %collective-permute-start.3 = (f32[8,384]{1,0:T(8,128)S(1)}, f32[8,384]{1,0:T(8,128)S(1)}, u32[]{:S(2)}, u32[]{:S(2)}) collective-permute-start(f32[8,384]{1,0:T(8,128)S(1)} %bitcast.83), channel_id=1, source_target_pairs={{0,3},{1,0},{2,1},{3,2},{4,7},{5,4},{6,5},{7,6},{8,11},{9,8},{10,9... | collective-permute-start | bytes 36872 | tf_op jit(solution)/shard_map/ppermute | solution.py:24
  38.2 0.7 collective-permute-start.4
  39.2 1.2 collective-permute-done.3
  42.2 6.9 %shard_map.73 = f32[8,384]{1,0:T(8,128)} custom-call(f32[8,384,384]{2,1,0:T(8,128)} %map_ref.3, f32[8,384]{1,0:T(8,128)} %fusion.5.force_ref, f32[1,384]{1,0:T(1,128)} %reshape.138.start_ref), custom_call_target="tpu_custom_call" | custom-call | tf_op jit(solution)/shard_map/pallas_call | solution.py:55
  49.1 0.7 slice_reduce_fusion.3
  49.8 1.4 %collective-permute-start.5 = (f32[384]{0:T(512)S(1)}, f32[384]{0:T(512)S(1)}, u32[]{:S(2)}, u32[]{:S(2)}) collective-permute-start(f32[384]{0:T(512)S(1)} %add_select_fusion), channel_id=1, source_target_pairs={{0,4},{8,12},{16,20},{24,28},{32,36},{40,44},{48,52},{56,60},{64,6... | collective-permute-start | bytes 4616 | tf_op jit(solution)/shard_map/ppermute | solution.py:18
  51.2 0.8 collective-permute-done.5
  52.3 0.7 collective-permute-start.6
  53.3 0.7 fusion.14
  54.1 0.7 collective-permute-start.7
  54.8 0.8 fusion.15
  55.7 0.7 collective-permute-start.8
  56.5 0.8 fusion.10
  57.4 0.7 collective-permute-start.9
  58.1 0.8 fusion.8
  59.0 0.7 collective-permute-start.10
  60.0 0.7 collective-permute-start.11
  60.7 1.3 collective-permute-start.12
  62.3 65.2 %collective-permute-done.12 = f32[384]{0:T(512)S(1)} collective-permute-done((f32[384]{0:T(512)S(1)}, f32[384]{0:T(512)S(1)}, u32[]{:S(2)}, u32[]{:S(2)}) %collective-permute-start.12) | collective-permute-done | bytes 1568 | tf_op jit(solution)/shard_map/ppermute | solution.py:130
  128.0 6.9 %shard_map.74 = f32[8,384]{1,0:T(8,128)} custom-call(f32[8,384,384]{2,1,0:T(8,128)} %map_ref.3, f32[8,384]{1,0:T(8,128)} %fusion.5.force_ref, f32[1,384]{1,0:T(1,128)} %reshape.139.start_ref), custom_call_target="tpu_custom_call" | custom-call | tf_op jit(solution)/shard_map/pallas_call | solution.py:55
  (74 shorter events, 8.1 us)
Async XLA Ops:
  0.0 31.4 %copy-start = (f32[8,384,48]{1,2,0:T(8,128)S(1)}, f32[8,384,48]{1,2,0:T(8,128)}, u32[]{:S(2)}) copy-start(f32[8,384,48]{1,2,0:T(8,128)} %param.8) | copy-start | bytes 1769476
  0.0 1.9 %copy-start.2 = (s32[512]{0:T(512)S(1)}, s32[512]{0:T(512)}, u32[]{:S(2)}) copy-start(s32[512]{0:T(512)} %param.12) | copy-start | bytes 6148
  0.0 2.0 %copy-start.3 = (s32[1,64]{1,0:T(1,128)S(1)}, s32[1,64]{1,0:T(1,128)}, u32[]{:S(2)}) copy-start(s32[1,64]{1,0:T(1,128)} %param.13) | copy-start | bytes 772
  4.4 24.7 %all-to-all-start = ((bf16[256,2,196]{2,1,0:T(2,128)(2,1)}), bf16[256,2,196]{2,1,0:T(2,128)(2,1)S(1)}, u32[]{:S(2)}, u32[]{:S(2)}) async-start(bf16[256,2,196]{2,1,0:T(2,128)(2,1)} %reshape.170), calls=%async_computation | async-start | bytes 524288 | tf_op jit(solution)/shard_map/all_to_all | solution.py:92
  24.6 4.1 %copy-start.1 = (f32[384]{0:T(512)S(1)}, f32[384]{0:T(512)}, u32[]{:S(2)}) copy-start(f32[384]{0:T(512)} %param.9) | copy-start | bytes 4612
  26.6 5.1 %collective-permute-start = (f32[384,384]{1,0:T(8,128)S(1)}, f32[384,384]{1,0:T(8,128)S(1)}, u32[]{:S(2)}, u32[]{:S(2)}) collective-permute-start(f32[384,384]{1,0:T(8,128)S(1)} %get-tuple-element.9), channel_id=1, source_target_pairs={{0,4},{8,12},{16,20},{24,28},{32,36},{40,44},{48,52},{56,60},{64,6... | collective-permute-start | bytes 1769480 | tf_op jit(solution)/shard_map/ppermute | solution.py:18
  32.4 6.4 %collective-permute-start.1 = (f32[8,384]{1,0:T(8,128)S(1)}, f32[8,384]{1,0:T(8,128)S(1)}, u32[]{:S(2)}, u32[]{:S(2)}) collective-permute-start(f32[8,384]{1,0:T(8,128)S(1)} %bitcast.81), channel_id=1, source_target_pairs={{0,1},{1,2},{2,3},{3,0},{4,5},{5,6},{6,7},{7,4},{8,9},{9,10},{10,1... | collective-permute-start | bytes 36872 | tf_op jit(solution)/shard_map/ppermute | solution.py:24
  34.0 5.2 %collective-permute-start.2 = (f32[8,384]{1,0:T(8,128)S(1)}, f32[8,384]{1,0:T(8,128)S(1)}, u32[]{:S(2)}, u32[]{:S(2)}) collective-permute-start(f32[8,384]{1,0:T(8,128)S(1)} %bitcast.82), channel_id=1, source_target_pairs={{0,2},{1,3},{2,0},{3,1},{4,6},{5,7},{6,4},{7,5},{8,10},{9,11},{10,... | collective-permute-start | bytes 36872 | tf_op jit(solution)/shard_map/ppermute | solution.py:24
  36.7 3.7 %collective-permute-start.3 = (f32[8,384]{1,0:T(8,128)S(1)}, f32[8,384]{1,0:T(8,128)S(1)}, u32[]{:S(2)}, u32[]{:S(2)}) collective-permute-start(f32[8,384]{1,0:T(8,128)S(1)} %bitcast.83), channel_id=1, source_target_pairs={{0,3},{1,0},{2,1},{3,2},{4,7},{5,4},{6,5},{7,6},{8,11},{9,8},{10,9... | collective-permute-start | bytes 36872 | tf_op jit(solution)/shard_map/ppermute | solution.py:24
  38.2 15.2 %collective-permute-start.4 = (f32[384,384]{1,0:T(8,128)S(1)}, f32[384,384]{1,0:T(8,128)S(1)}, u32[]{:S(2)}, u32[]{:S(2)}) collective-permute-start(f32[384,384]{1,0:T(8,128)S(1)} %fusion.13), channel_id=1, source_target_pairs={{4,12},{12,20},{20,28},{28,36},{36,44},{44,52},{52,60},{60,68},{68... | collective-permute-start | bytes 1769480 | tf_op jit(solution)/shard_map/ppermute | solution.py:18
  49.8 2.2 %collective-permute-start.5 = (f32[384]{0:T(512)S(1)}, f32[384]{0:T(512)S(1)}, u32[]{:S(2)}, u32[]{:S(2)}) collective-permute-start(f32[384]{0:T(512)S(1)} %add_select_fusion), channel_id=1, source_target_pairs={{0,4},{8,12},{16,20},{24,28},{32,36},{40,44},{48,52},{56,60},{64,6... | collective-permute-start | bytes 4616 | tf_op jit(solution)/shard_map/ppermute | solution.py:18
  52.3 0.7 collective-permute-start.6
  54.1 0.7 collective-permute-start.7
  55.7 0.7 collective-permute-start.8
  57.4 0.7 collective-permute-start.9
  59.0 0.7 collective-permute-start.10
  60.0 2.0 %collective-permute-start.11 = (f32[384]{0:T(512)S(1)}, f32[384]{0:T(512)S(1)}, u32[]{:S(2)}, u32[]{:S(2)}) collective-permute-start(f32[384]{0:T(512)S(1)} %add.77), channel_id=1, source_target_pairs={{4,12},{12,20},{20,28},{28,36},{36,44},{44,52},{52,60},{60,68},{68... | collective-permute-start | bytes 4616 | tf_op jit(solution)/shard_map/ppermute | solution.py:18
  60.7 66.8 %collective-permute-start.12 = (f32[384]{0:T(512)S(1)}, f32[384]{0:T(512)S(1)}, u32[]{:S(2)}, u32[]{:S(2)}) collective-permute-start(f32[384]{0:T(512)S(1)} %add.77), channel_id=1, source_target_pairs={{4,8},{12,16},{20,24},{28,32},{36,40},{44,48},{52,56},{60,64},{68,... | collective-permute-start | bytes 4616 | tf_op jit(solution)/shard_map/ppermute | solution.py:130

commit v14 on v13

--- a/solution.py
+++ b/solution.py
@@ -10,6 +10,47 @@
     devices = range(lax.axis_size(axis))
     route = [(i - distance, i) for i in devices if i - distance in devices]
     return lax.ppermute(block, axis, route)
+
+
+def sent_to_odd(block, axis, distance):
+    devices = range(lax.axis_size(axis))
+    route = [(i - distance, i) for i in devices if i % 2 == 1 and i - distance in devices]
+    return lax.ppermute(block, axis, route)
+
+
+def summed_over(block, axis):
+    count = lax.axis_size(axis)
+    shares = [block] + [
+        lax.ppermute(block, axis, [(i, (i + shift) % count) for i in range(count)])
+        for shift in range(1, count)
+    ]
+    by_source = jnp.stack(shares)[(lax.axis_index(axis) - jnp.arange(count)) % count]
+    total = by_source[0]
+    for source in range(1, count):
+        total = total + by_source[source]
+    return total
+
+
+def recurrence_kernel(map_ref, force_ref, start_ref, out_ref):
+    state = jnp.broadcast_to(start_ref[...], (8, start_ref.shape[1]))
+    for step in range(map_ref.shape[0]):
+        moved = lax.dot_general(
+            state,
+            map_ref[step],
+            (((1,), (1,)), ((), ())),
+            precision=lax.Precision.HIGH,
+            preferred_element_type=jnp.float32,
+        )
+        state = moved + force_ref[step : step + 1, :]
+        out_ref[step : step + 1, :] = state[0:1, :]
+
+
+def run_recurrence(trans, forcing, start):
+    steps, width = forcing.shape
+    return pl.pallas_call(
+        recurrence_kernel,
+        out_shape=jax.ShapeDtypeStruct((steps, width), jnp.float32),
+    )(trans, forcing, start.reshape(1, width))
 
 
 def sent_to_odd(block, axis, distance):

time: 136 us -> 136 us (level)
  no operation moved by 1% of the time
where the time goes in v14:
time: 136 us; the launch traced here: 135 us
  waiting for transfers between devices  67.5 us (50%)
  starting transfers between devices  29 us (21%)
  matrix products  14.7 us (11%)
  Pallas kernels  13.9 us (10%)
  local copies, waits for them, and re-layouts  6.6 us (5%)
  other arithmetic  2.72 us (2%)
    ppermute x1, waiting for transfers between devices, on_device(): lax.ppermute(acc_vec, 'tm', [(i - 1, i) for i in range(tm_count) if i % 2...  65.2 us
    pallas_call x2, Pallas kernels, run_recurrence(): pl.pallas_call(recurrence_kernel, grid=(steps,), in_specs=[pl.BlockSpec((...  13.9 us
    all_to_all x1, starting transfers between devices, on_device(): lax.all_to_all(sent, ('tm', 'ingest'), split_axis=0, concat_axis=0, tiled...  13.8 us
    ppermute x9, starting transfers between devices, sent_to_odd(): return lax.ppermute(block, axis, route)  8.2 us
    dot_general x1, matrix products, on_device(): jnp.einsum('jba,jcb->jac', pairs[:, 0], pairs[:, 1], precision=precise)  6.36 us
    ppermute x3, starting transfers between devices, summed_over(): lax.ppermute(block, axis, [(i, (i + shift) % count) for i in range(count)])  5.71 us
  transfers between devices with their start and end apart: 14, of which 4 were waited for; matrix products, arithmetic and copies ran while one was open for 11% of the time, Pallas kernels for 5%

profile of v14, /device:TPU:128, one launch (start us, length us, event | category | flops | bytes accessed | tf_op | source)
XLA Modules:
  0.0 135.0 jit_solution(2284659316328088850)
XLA Ops:
  0.0 1.0 multiply_convert_fusion
  2.7 0.8 reduce.18
  3.5 0.9 reshape.170
  4.4 13.8 %all-to-all-start = ((bf16[256,2,196]{2,1,0:T(2,128)(2,1)}), bf16[256,2,196]{2,1,0:T(2,128)(2,1)S(1)}, u32[]{:S(2)}, u32[]{:S(2)}) async-start(bf16[256,2,196]{2,1,0:T(2,128)(2,1)} %reshape.170), calls=%async_computation | async-start | bytes 524288 | tf_op jit(solution)/shard_map/all_to_all | solution.py:133
  18.2 6.4 %fusion = f32[4,384,384]{2,1,0:T(8,128)S(1)} fusion(f32[4,2,384,384]{3,2,1,0:T(8,128)} %bitcast.75), kind=kOutput, calls=%fused_computation.2 | convolution fusion | flops 1358954496 | bytes 7077888 | tf_op jit(solution)/shard_map/jba,jcb->jac/dot_general | solution.py:135
  24.6 1.3 convolution_bitcast_fusion
  25.9 0.7 broadcast_select_fusion
  26.6 2.1 %collective-permute-start = (f32[384,384]{1,0:T(8,128)S(1)}, f32[384,384]{1,0:T(8,128)S(1)}, u32[]{:S(2)}, u32[]{:S(2)}) collective-permute-start(f32[384,384]{1,0:T(8,128)S(1)} %get-tuple-element.9), channel_id=1, source_target_pairs={{0,4},{8,12},{16,20},{24,28},{32,36},{40,44},{48,52},{56,60},{64,6... | collective-permute-start | bytes 1769480 | tf_op jit(solution)/shard_map/ppermute | solution.py:59
  30.7 0.7 fusion.1
  31.7 0.7 fusion.13
  32.4 1.6 %collective-permute-start.1 = (f32[8,384]{1,0:T(8,128)S(1)}, f32[8,384]{1,0:T(8,128)S(1)}, u32[]{:S(2)}, u32[]{:S(2)}) collective-permute-start(f32[8,384]{1,0:T(8,128)S(1)} %bitcast.81), channel_id=1, source_target_pairs={{0,1},{1,2},{2,3},{3,0},{4,5},{5,6},{6,7},{7,4},{8,9},{9,10},{10,1... | collective-permute-start | bytes 36872 | tf_op jit(solution)/shard_map/ppermute | solution.py:65
  34.0 2.7 %collective-permute-start.2 = (f32[8,384]{1,0:T(8,128)S(1)}, f32[8,384]{1,0:T(8,128)S(1)}, u32[]{:S(2)}, u32[]{:S(2)}) collective-permute-start(f32[8,384]{1,0:T(8,128)S(1)} %bitcast.82), channel_id=1, source_target_pairs={{0,2},{1,3},{2,0},{3,1},{4,6},{5,7},{6,4},{7,5},{8,10},{9,11},{10,... | collective-permute-start | bytes 36872 | tf_op jit(solution)/shard_map/ppermute | solution.py:65
  36.7 1.4 %collective-permute-start.3 = (f32[8,384]{1,0:T(8,128)S(1)}, f32[8,384]{1,0:T(8,128)S(1)}, u32[]{:S(2)}, u32[]{:S(2)}) collective-permute-start(f32[8,384]{1,0:T(8,128)S(1)} %bitcast.83), channel_id=1, source_target_pairs={{0,3},{1,0},{2,1},{3,2},{4,7},{5,4},{6,5},{7,6},{8,11},{9,8},{10,9... | collective-permute-start | bytes 36872 | tf_op jit(solution)/shard_map/ppermute | solution.py:65
  38.2 0.7 collective-permute-start.4
  39.2 1.2 collective-permute-done.3
  42.2 6.9 %shard_map.73 = f32[8,384]{1,0:T(8,128)} custom-call(f32[8,384,384]{2,1,0:T(8,128)} %map_ref.3, f32[8,384]{1,0:T(8,128)} %fusion.5.force_ref, f32[1,384]{1,0:T(1,128)} %reshape.138.start_ref), custom_call_target="tpu_custom_call" | custom-call | tf_op jit(solution)/shard_map/pallas_call | solution.py:96
  49.1 0.7 slice_reduce_fusion.3
  49.8 1.4 %collective-permute-start.5 = (f32[384]{0:T(512)S(1)}, f32[384]{0:T(512)S(1)}, u32[]{:S(2)}, u32[]{:S(2)}) collective-permute-start(f32[384]{0:T(512)S(1)} %add_select_fusion), channel_id=1, source_target_pairs={{0,4},{8,12},{16,20},{24,28},{32,36},{40,44},{48,52},{56,60},{64,6... | collective-permute-start | bytes 4616 | tf_op jit(solution)/shard_map/ppermute | solution.py:59
  51.2 0.8 collective-permute-done.5
  52.3 0.7 collective-permute-start.6
  53.3 0.7 fusion.14
  54.1 0.7 collective-permute-start.7
  54.8 0.8 fusion.15
  55.7 0.7 collective-permute-start.8
  56.5 0.8 fusion.10
  57.4 0.7 collective-permute-start.9
  58.1 0.8 fusion.8
  59.0 0.7 collective-permute-start.10
  60.0 0.7 collective-permute-start.11
  60.7 1.3 collective-permute-start.12
  62.3 65.2 %collective-permute-done.12 = f32[384]{0:T(512)S(1)} collective-permute-done((f32[384]{0:T(512)S(1)}, f32[384]{0:T(512)S(1)}, u32[]{:S(2)}, u32[]{:S(2)}) %collective-permute-start.12) | collective-permute-done | bytes 1568 | tf_op jit(solution)/shard_map/ppermute | solution.py:171
  128.0 6.9 %shard_map.74 = f32[8,384]{1,0:T(8,128)} custom-call(f32[8,384,384]{2,1,0:T(8,128)} %map_ref.3, f32[8,384]{1,0:T(8,128)} %fusion.5.force_ref, f32[1,384]{1,0:T(1,128)} %reshape.139.start_ref), custom_call_target="tpu_custom_call" | custom-call | tf_op jit(solution)/shard_map/pallas_call | solution.py:96
  (74 shorter events, 8.1 us)
Async XLA Ops:
  0.0 31.4 %copy-start = (f32[8,384,48]{1,2,0:T(8,128)S(1)}, f32[8,384,48]{1,2,0:T(8,128)}, u32[]{:S(2)}) copy-start(f32[8,384,48]{1,2,0:T(8,128)} %param.8) | copy-start | bytes 1769476
  0.0 1.9 %copy-start.2 = (s32[512]{0:T(512)S(1)}, s32[512]{0:T(512)}, u32[]{:S(2)}) copy-start(s32[512]{0:T(512)} %param.12) | copy-start | bytes 6148
  0.0 2.0 %copy-start.3 = (s32[1,64]{1,0:T(1,128)S(1)}, s32[1,64]{1,0:T(1,128)}, u32[]{:S(2)}) copy-start(s32[1,64]{1,0:T(1,128)} %param.13) | copy-start | bytes 772
  4.4 24.7 %all-to-all-start = ((bf16[256,2,196]{2,1,0:T(2,128)(2,1)}), bf16[256,2,196]{2,1,0:T(2,128)(2,1)S(1)}, u32[]{:S(2)}, u32[]{:S(2)}) async-start(bf16[256,2,196]{2,1,0:T(2,128)(2,1)} %reshape.170), calls=%async_computation | async-start | bytes 524288 | tf_op jit(solution)/shard_map/all_to_all | solution.py:133
  24.6 4.1 %copy-start.1 = (f32[384]{0:T(512)S(1)}, f32[384]{0:T(512)}, u32[]{:S(2)}) copy-start(f32[384]{0:T(512)} %param.9) | copy-start | bytes 4612
  26.6 5.1 %collective-permute-start = (f32[384,384]{1,0:T(8,128)S(1)}, f32[384,384]{1,0:T(8,128)S(1)}, u32[]{:S(2)}, u32[]{:S(2)}) collective-permute-start(f32[384,384]{1,0:T(8,128)S(1)} %get-tuple-element.9), channel_id=1, source_target_pairs={{0,4},{8,12},{16,20},{24,28},{32,36},{40,44},{48,52},{56,60},{64,6... | collective-permute-start | bytes 1769480 | tf_op jit(solution)/shard_map/ppermute | solution.py:59
  32.4 6.4 %collective-permute-start.1 = (f32[8,384]{1,0:T(8,128)S(1)}, f32[8,384]{1,0:T(8,128)S(1)}, u32[]{:S(2)}, u32[]{:S(2)}) collective-permute-start(f32[8,384]{1,0:T(8,128)S(1)} %bitcast.81), channel_id=1, source_target_pairs={{0,1},{1,2},{2,3},{3,0},{4,5},{5,6},{6,7},{7,4},{8,9},{9,10},{10,1... | collective-permute-start | bytes 36872 | tf_op jit(solution)/shard_map/ppermute | solution.py:65
  34.0 5.2 %collective-permute-start.2 = (f32[8,384]{1,0:T(8,128)S(1)}, f32[8,384]{1,0:T(8,128)S(1)}, u32[]{:S(2)}, u32[]{:S(2)}) collective-permute-start(f32[8,384]{1,0:T(8,128)S(1)} %bitcast.82), channel_id=1, source_target_pairs={{0,2},{1,3},{2,0},{3,1},{4,6},{5,7},{6,4},{7,5},{8,10},{9,11},{10,... | collective-permute-start | bytes 36872 | tf_op jit(solution)/shard_map/ppermute | solution.py:65
  36.7 3.7 %collective-permute-start.3 = (f32[8,384]{1,0:T(8,128)S(1)}, f32[8,384]{1,0:T(8,128)S(1)}, u32[]{:S(2)}, u32[]{:S(2)}) collective-permute-start(f32[8,384]{1,0:T(8,128)S(1)} %bitcast.83), channel_id=1, source_target_pairs={{0,3},{1,0},{2,1},{3,2},{4,7},{5,4},{6,5},{7,6},{8,11},{9,8},{10,9... | collective-permute-start | bytes 36872 | tf_op jit(solution)/shard_map/ppermute | solution.py:65
  38.2 15.2 %collective-permute-start.4 = (f32[384,384]{1,0:T(8,128)S(1)}, f32[384,384]{1,0:T(8,128)S(1)}, u32[]{:S(2)}, u32[]{:S(2)}) collective-permute-start(f32[384,384]{1,0:T(8,128)S(1)} %fusion.13), channel_id=1, source_target_pairs={{4,12},{12,20},{20,28},{28,36},{36,44},{44,52},{52,60},{60,68},{68... | collective-permute-start | bytes 1769480 | tf_op jit(solution)/shard_map/ppermute | solution.py:59
  49.8 2.2 %collective-permute-start.5 = (f32[384]{0:T(512)S(1)}, f32[384]{0:T(512)S(1)}, u32[]{:S(2)}, u32[]{:S(2)}) collective-permute-start(f32[384]{0:T(512)S(1)} %add_select_fusion), channel_id=1, source_target_pairs={{0,4},{8,12},{16,20},{24,28},{32,36},{40,44},{48,52},{56,60},{64,6... | collective-permute-start | bytes 4616 | tf_op jit(solution)/shard_map/ppermute | solution.py:59
  52.3 0.7 collective-permute-start.6
  54.1 0.7 collective-permute-start.7
  55.7 0.7 collective-permute-start.8
  57.4 0.7 collective-permute-start.9
  59.0 0.7 collective-permute-start.10
  60.0 2.0 %collective-permute-start.11 = (f32[384]{0:T(512)S(1)}, f32[384]{0:T(512)S(1)}, u32[]{:S(2)}, u32[]{:S(2)}) collective-permute-start(f32[384]{0:T(512)S(1)} %add.77), channel_id=1, source_target_pairs={{4,12},{12,20},{20,28},{28,36},{36,44},{44,52},{52,60},{60,68},{68... | collective-permute-start | bytes 4616 | tf_op jit(solution)/shard_map/ppermute | solution.py:59
  60.7 66.8 %collective-permute-start.12 = (f32[384]{0:T(512)S(1)}, f32[384]{0:T(512)S(1)}, u32[]{:S(2)}, u32[]{:S(2)}) collective-permute-start(f32[384]{0:T(512)S(1)} %add.77), channel_id=1, source_target_pairs={{4,8},{12,16},{20,24},{28,32},{36,40},{44,48},{52,56},{60,64},{68,... | collective-permute-start | bytes 4616 | tf_op jit(solution)/shard_map/ppermute | solution.py:171
